TPU v7x, 256 devices: a whole 4x4x8 slice. The times are simulated.
256 devices in a mesh: owner: 8 (over z_hi, x), ctx: 32 (over y, z_lo, core).
Axes of the slice: x: 4, y: 4, z: 8 (z_hi: 2, z_lo: 4; z = z_hi * 4 + z_lo), core: 2. Of those that a mesh axis runs over, the one named last changes fastest.
Arguments:
- span_cache: bfloat16 [2048, 128, 1024], P(('owner', 'ctx')), may hold values from -8 to 8
- retrieval: int32 [8, 256], P(None, 'ctx'), may hold values from 0 to 2047, as said below
- counts: int32 [8], replicated, may hold values from 64 to 256, as said below
- recompute_pos: int32 [8, 256], P('owner'), may hold values from 0 to 1023, as said below
- hidden: bfloat16 [8, 256, 8192], P('owner', None, 'ctx'), may hold values from -6 to 6
- kv_weight: bfloat16 [8192, 1024], P('ctx'), may hold values from -0.0625 to 0.0625
- queries: bfloat16 [8, 256, 4096], P('owner', 'ctx'), may hold values from -8 to 8
- block_mask: int32 [8, 256, 256], P('owner', None, 'ctx'), may hold values from 0 to 1, as said below
Outputs:
- context_kv: bfloat16 [8, 32768, 1024], P('owner', 'ctx')
- attended: bfloat16 [8, 256, 4096], P('owner', 'ctx')
Inputs may be any that keep to these rules, and one draw needn't show every extreme that they name: `retrieval`: the span for block b of a request is stored on index b // 8 of ctx of some owner group o: its number is (o * 32 + b // 8) * 8 + s. Among the 8 blocks of one request on one index of ctx at most 4 name spans of one owner group, and in every draw some reach 4. `counts`: some request uses all 256 blocks in every draw. `recompute_pos`: the 8 positions of one request on one index of ctx are distinct. `block_mask`: every query block may see itself and those of the first 4 blocks not after it; no block sees a later one.
All inputs are finite; a program needn't handle non-finite values.
Results may differ from a plain program's by a relative error of at most 0.023.
Values may be sent and summed in bfloat16 or wider, within the bound.
No kernel may reach another device: no remote copies, remote signals or barrier semaphores. Data moves between devices by JAX's collectives and lax.ppermute only.
A program may use at most 128 MiB of HBM per device.

v0:
```python
import jax
import jax.numpy as jnp
from jax import lax
from jax.sharding import PartitionSpec as P

QH = 32
KVH = 4
HD = 128
BLK = 128
NBD = 8
RCP = 8
SLOTS = 8
CAP = 4
CTX_DEV = 1024


def passed_along(shard, axis, by):
    peers = lax.axis_size(axis)
    return lax.ppermute(shard, axis, [(i, (i + by) % peers) for i in range(peers)])


def absorb(
    query_rows,
    query_pos,
    numerator,
    running,
    totals_now,
    key_rows,
    value_rows,
    key_pos,
    key_in_use,
    mask_cols,
):
    row_count = query_rows.shape[0]
    per_group = QH // KVH
    allowed = jnp.take(mask_cols, query_pos // BLK, axis=0)
    visible = jnp.repeat(allowed, BLK, axis=1) > 0
    visible = visible & key_in_use[None, :] & (key_pos[None, :] <= query_pos[:, None])
    grouped = query_rows.reshape(row_count, KVH, per_group, HD)
    scores = jnp.einsum(
        "rkgd,tkd->kgrt", grouped, key_rows, preferred_element_type=jnp.float32
    ) * HD ** (-0.5)
    scores = jnp.where(visible[None, None], scores, -1e30)
    running = running.reshape(KVH, per_group, row_count)
    newest = jnp.maximum(running, jnp.max(scores, axis=3))
    weights = jnp.where(visible[None, None], jnp.exp(scores - newest[..., None]), 0.0)
    factor = jnp.exp(running - newest)
    totals_now = totals_now.reshape(KVH, per_group, row_count) * factor + jnp.sum(weights, axis=3)
    weighted = jnp.einsum(
        "kgrt,tkd->rkgd",
        weights.astype(jnp.bfloat16),
        value_rows,
        preferred_element_type=jnp.float32,
    )
    numerator = (
        numerator.reshape(row_count, KVH, per_group, HD)
        * jnp.transpose(factor, (2, 0, 1))[..., None]
        + weighted
    )
    return (
        numerator.reshape(row_count, QH * HD),
        newest.reshape(QH, row_count),
        totals_now.reshape(QH, row_count),
    )


def on_device(span_cache, retrieval, counts, recompute_pos, hidden, kv_weight, queries, block_mask):
    owner_count = lax.axis_size("owner")
    cycle_size = lax.axis_size("ctx")
    my_owner = lax.axis_index("owner")
    my_ctx = lax.axis_index("ctx")
    feature_count = span_cache.shape[2]
    positions = jnp.arange(NBD, dtype=jnp.int32)
    block_ids = my_ctx * NBD + positions
    in_use = block_ids[None, :] < counts[:, None]
    holder = retrieval // (cycle_size * SLOTS)
    outbound = in_use & (holder == my_owner)
    slot_rank = jnp.cumsum(outbound.astype(jnp.int32), axis=1) - 1
    picked = outbound[:, None, :] & (
        slot_rank[:, None, :] == jnp.arange(CAP, dtype=jnp.int32)[None, :, None]
    )
    chosen = jnp.sum(jnp.where(picked, (retrieval % SLOTS)[:, None, :], 0), axis=2)
    filled = jnp.any(picked, axis=2)
    outgoing = jnp.where(
        filled[:, :, None, None], jnp.take(span_cache, chosen, axis=0), jnp.zeros((), jnp.bfloat16)
    )
    arrived = lax.all_to_all(outgoing, "owner", split_axis=0, concat_axis=0, tiled=True)
    wanted = lax.dynamic_index_in_dim(retrieval, my_owner, 0, keepdims=False)
    my_count = lax.dynamic_index_in_dim(counts, my_owner, 0, keepdims=False)
    my_in_use = block_ids < my_count
    source = wanted // (cycle_size * SLOTS)
    earlier = (
        (source[:, None] == source[None, :])
        & my_in_use[None, :]
        & (positions[None, :] < positions[:, None])
    )
    ordinal = jnp.sum(earlier.astype(jnp.int32), axis=1)
    flattened = arrived.reshape(owner_count * CAP, BLK, feature_count)
    blocks = jnp.take(flattened, source * CAP + ordinal, axis=0, mode="clip")
    blocks = jnp.where(my_in_use[:, None, None], blocks, jnp.zeros((), jnp.bfloat16))
    context = blocks.reshape(CTX_DEV, feature_count)
    local_rows = hidden[0]
    recomputed = lax.psum_scatter(
        jnp.dot(local_rows, kv_weight, preferred_element_type=jnp.float32).astype(jnp.bfloat16),
        "ctx",
        scatter_dimension=0,
        tiled=True,
    )
    every_pos = recompute_pos[0]
    own_pos = lax.dynamic_slice_in_dim(every_pos, my_ctx * RCP, RCP)
    matches = jnp.arange(CTX_DEV, dtype=jnp.int32)[:, None] == own_pos[None, :]
    placed = jnp.dot(
        matches.astype(jnp.bfloat16), recomputed, preferred_element_type=jnp.float32
    ).astype(jnp.bfloat16)
    context = jnp.where(jnp.any(matches, axis=1)[:, None], placed, context)
    key_width = KVH * HD
    key_rows = context[:, :key_width].reshape(CTX_DEV, KVH, HD)
    value_rows = context[:, key_width:].reshape(CTX_DEV, KVH, HD)
    key_pos = my_ctx * CTX_DEV + jnp.arange(CTX_DEV, dtype=jnp.int32)
    key_in_use = key_pos // BLK < my_count
    mask_cols = block_mask[0]
    query_starts = jnp.arange(cycle_size * RCP, dtype=jnp.int32) // RCP * CTX_DEV + every_pos
    numerator_zero = jnp.zeros((RCP, QH * HD), jnp.float32)
    running_zero = jnp.full((QH, RCP), -1e30, jnp.float32)
    totals_zero = jnp.zeros((QH, RCP), jnp.float32)

    def visit_keys(query_rows, offset, numerator, running, totals_now):
        query_pos = lax.dynamic_slice_in_dim(query_starts, offset, query_rows.shape[0])
        return absorb(
            query_rows,
            query_pos,
            numerator,
            running,
            totals_now,
            key_rows,
            value_rows,
            key_pos,
            key_in_use,
            mask_cols,
        )

    def pass_state(carried):
        return passed_along(carried, "ctx", 1)

    def cycle_turn(turn_index, carry):
        visiting, numerator, running, totals_now = carry
        source_index = (my_ctx - turn_index) % cycle_size
        carried = visit_keys(visiting, source_index * RCP, numerator, running, totals_now)
        visiting = passed_along(visiting, "ctx", 1)
        numerator, running, totals_now = pass_state(carried)
        return (visiting, numerator, running, totals_now)

    visiting, numerator, running, totals_now = lax.fori_loop(
        0, cycle_size - 1, cycle_turn, (queries[0], numerator_zero, running_zero, totals_zero)
    )
    source_index = (my_ctx - (cycle_size - 1)) % cycle_size
    carried = visit_keys(visiting, source_index * RCP, numerator, running, totals_now)
    numerator, running, totals_now = pass_state(carried)
    result = numerator.reshape(RCP, QH, HD) / jnp.transpose(totals_now)[:, :, None]
    attended = result.reshape(RCP, QH * HD).astype(jnp.bfloat16)
    return (context[None], attended[None])


def solution(mesh):
    in_specs = (
        P(("owner", "ctx"), None, None),
        P(None, "ctx"),
        P(),
        P("owner", None),
        P("owner", None, "ctx"),
        P("ctx", None),
        P("owner", "ctx", None),
        P("owner", None, "ctx"),
    )
    out_specs = (P("owner", "ctx", None), P("owner", "ctx", None))
    return jax.shard_map(
        on_device, mesh=mesh, in_specs=in_specs, out_specs=out_specs, check_vma=False
    )
```

profile of v0, /device:TPU:6, one launch (start us, length us, event | category | flops | bytes accessed | tf_op | source)
XLA Modules:
  0.0 836.1 jit_solution(330683902792057110)
XLA Ops:
  9.7 4.7 gather_fusion.1
  14.4 7.6 select_select_fusion
  22.0 11.8 %all-to-all-start = ((bf16[8,4,128,1024]{3,2,1,0:T(8,128)(2,1)}), bf16[8,4,128,1024]{3,2,1,0:T(8,128)(2,1)}, u32[]{:S(2)}, u32[]{:S(2)}) async-start(bf16[8,4,128,1024]{3,2,1,0:T(8,128)(2,1)} %select_select_fusion), calls=%async_computation.1 | async-start | bytes 16777216 | tf_op jit(solution)/shard_map/all_to_all | solution.py:87
  43.9 109.6 %all-to-all-done = bf16[8,4,128,1024]{3,2,1,0:T(8,128)(2,1)} async-done(((bf16[8,4,128,1024]{3,2,1,0:T(8,128)(2,1)}), bf16[8,4,128,1024]{3,2,1,0:T(8,128)(2,1)}, u32[]{:S(2)}, u32[]{:S(2)}) %all-to-all-start) | async-done | bytes 8388640 | tf_op jit(solution)/shard_map/all_to_all | solution.py:87
  153.5 5.4 gather_fusion.2
  158.9 3.9 copy.136
  162.8 92.4 %reduce-scatter.2.cloned.1.call-done = bf16[8,1024]{1,0:T(8,128)(2,1)} async-done(((bf16[256,1024]{1,0:T(8,128)(2,1)}), bf16[8,1024]{1,0:T(8,128)(2,1)}) %reduce-scatter.2.cloned.1.call-update) | async-done | bytes 16400 | tf_op jit(solution)/shard_map/reduce_scatter | solution.py:103
  255.2 2.4 select_select_fusion.1
  257.6 1.7 fusion.54
  259.6 1.6 copy.118
  261.2 2.3 copy.119
  264.7 549.3 %while.23 = (s32[]{:T(128)}, bf16[8,4096]{1,0:T(8,128)(2,1)S(1)}, f32[8,4096]{1,0:T(8,128)S(1)}, f32[32,8]{0,1:T(8,128)}, f32[32,8]{0,1:T(8,128)}, /*index=5*/s3...) while((s32[]{:T(128)}, bf16[8,4096]{1,0:T(8,128)(2,1)S(1)}, ...), condition=%wide.region_9.11_spmd.clone.clone, body=%wide.region_6.10_spmd.clone.clone.sunk | while | flops 136687936 | bytes 7099112 | solution.py:153
  274.9 7.0 collective-permute-done.2
  292.6 7.0 collective-permute-done.2
  304.7 1.6 fusion.72
  310.3 7.0 collective-permute-done.2
  328.1 7.0 collective-permute-done.2
  340.1 1.6 fusion.72
  345.8 7.0 collective-permute-done.2
  357.8 1.6 fusion.72
  363.5 7.0 collective-permute-done.2
  381.2 7.0 collective-permute-done.2
  393.3 1.6 fusion.72
  398.9 7.0 collective-permute-done.2
  411.0 1.6 fusion.72
  416.6 7.0 collective-permute-done.2
  434.3 7.0 collective-permute-done.2
  446.4 1.6 fusion.72
  452.1 7.0 collective-permute-done.2
  464.1 1.6 fusion.72
  469.8 7.0 collective-permute-done.2
  487.5 7.0 collective-permute-done.2
  499.6 1.6 fusion.72
  505.2 7.0 collective-permute-done.2
  517.3 1.6 fusion.72
  522.9 7.0 collective-permute-done.2
  540.6 7.0 collective-permute-done.2
  552.7 1.6 fusion.72
  558.4 7.0 collective-permute-done.2
  570.4 1.6 fusion.72
  576.1 7.0 collective-permute-done.2
  593.8 7.0 collective-permute-done.2
  605.8 1.6 fusion.72
  611.5 7.0 collective-permute-done.2
  623.6 1.6 fusion.72
  629.2 7.0 collective-permute-done.2
  646.9 7.0 collective-permute-done.2
  659.0 1.6 fusion.72
  664.6 7.0 collective-permute-done.2
  676.7 1.6 fusion.72
  682.4 7.0 collective-permute-done.2
  700.1 7.0 collective-permute-done.2
  712.1 1.6 fusion.72
  717.8 7.0 collective-permute-done.2
  729.8 1.6 fusion.72
  735.5 7.0 collective-permute-done.2
  753.2 7.0 collective-permute-done.2
  770.9 7.0 collective-permute-done.2
  788.7 7.0 collective-permute-done.2
  806.4 7.0 collective-permute-done.2
  814.8 1.6 fusion.55
  816.4 1.8 fusion.25
  820.8 3.9 copy.131
  824.8 3.7 collective-permute-done.5
  (986 shorter events, 320.9 us)
Async XLA Ops:
  22.0 131.5 %all-to-all-start = ((bf16[8,4,128,1024]{3,2,1,0:T(8,128)(2,1)}), bf16[8,4,128,1024]{3,2,1,0:T(8,128)(2,1)}, u32[]{:S(2)}, u32[]{:S(2)}) async-start(bf16[8,4,128,1024]{3,2,1,0:T(8,128)(2,1)} %select_select_fusion), calls=%async_computation.1 | async-start | bytes 16777216 | tf_op jit(solution)/shard_map/all_to_all | solution.py:87
  33.8 221.4 %reduce-scatter.2.cloned.1.call-start = ((), (), s32[]{:S(2)}) async-start(), calls=%async_computation.2 | async-start | bytes 540672 | tf_op jit(solution)/shard_map/reduce_scatter | solution.py:103
  264.7 17.2 %collective-permute-start = (bf16[8,4096]{1,0:T(8,128)(2,1)S(1)}, bf16[8,4096]{1,0:T(8,128)(2,1)S(1)}, u32[]{:S(2)}, u32[]{:S(2)}) collective-permute-start(bf16[8,4096]{1,0:T(8,128)(2,1)S(1)} %copy.194), channel_id=1, source_target_pairs={{0,1},{1,2},{2,3},{3,4},{4,5},{5,6},{6,7},{7,8},{8,9},{9,10},{10,1... | collective-permute-start | bytes 196616 | tf_op jit(solution)/shard_map/while/body/eval_jaxpr/ppermute | solution.py:19
  271.0 10.9 %collective-permute-start.1 = (f32[8,4096]{1,0:T(8,128)S(1)}, f32[8,4096]{1,0:T(8,128)S(1)}, u32[]{:S(2)}, u32[]{:S(2)}) collective-permute-start(f32[8,4096]{1,0:T(8,128)S(1)} %bitcast.167), channel_id=1, source_target_pairs={{0,1},{1,2},{2,3},{3,4},{4,5},{5,6},{6,7},{7,8},{8,9},{9,10},{10,1... | collective-permute-start | bytes 393224 | tf_op jit(solution)/shard_map/while/body/eval_jaxpr/ppermute | solution.py:19
  282.5 17.1 %collective-permute-start = (bf16[8,4096]{1,0:T(8,128)(2,1)S(1)}, bf16[8,4096]{1,0:T(8,128)(2,1)S(1)}, u32[]{:S(2)}, u32[]{:S(2)}) collective-permute-start(bf16[8,4096]{1,0:T(8,128)(2,1)S(1)} %copy.194), channel_id=1, source_target_pairs={{0,1},{1,2},{2,3},{3,4},{4,5},{5,6},{6,7},{7,8},{8,9},{9,10},{10,1... | collective-permute-start | bytes 196616 | tf_op jit(solution)/shard_map/while/body/eval_jaxpr/ppermute | solution.py:19
  288.7 10.9 %collective-permute-start.1 = (f32[8,4096]{1,0:T(8,128)S(1)}, f32[8,4096]{1,0:T(8,128)S(1)}, u32[]{:S(2)}, u32[]{:S(2)}) collective-permute-start(f32[8,4096]{1,0:T(8,128)S(1)} %bitcast.167), channel_id=1, source_target_pairs={{0,1},{1,2},{2,3},{3,4},{4,5},{5,6},{6,7},{7,8},{8,9},{9,10},{10,1... | collective-permute-start | bytes 393224 | tf_op jit(solution)/shard_map/while/body/eval_jaxpr/ppermute | solution.py:19
  300.2 17.1 %collective-permute-start = (bf16[8,4096]{1,0:T(8,128)(2,1)S(1)}, bf16[8,4096]{1,0:T(8,128)(2,1)S(1)}, u32[]{:S(2)}, u32[]{:S(2)}) collective-permute-start(bf16[8,4096]{1,0:T(8,128)(2,1)S(1)} %copy.194), channel_id=1, source_target_pairs={{0,1},{1,2},{2,3},{3,4},{4,5},{5,6},{6,7},{7,8},{8,9},{9,10},{10,1... | collective-permute-start | bytes 196616 | tf_op jit(solution)/shard_map/while/body/eval_jaxpr/ppermute | solution.py:19
  306.4 10.9 %collective-permute-start.1 = (f32[8,4096]{1,0:T(8,128)S(1)}, f32[8,4096]{1,0:T(8,128)S(1)}, u32[]{:S(2)}, u32[]{:S(2)}) collective-permute-start(f32[8,4096]{1,0:T(8,128)S(1)} %bitcast.167), channel_id=1, source_target_pairs={{0,1},{1,2},{2,3},{3,4},{4,5},{5,6},{6,7},{7,8},{8,9},{9,10},{10,1... | collective-permute-start | bytes 393224 | tf_op jit(solution)/shard_map/while/body/eval_jaxpr/ppermute | solution.py:19
  317.9 17.1 %collective-permute-start = (bf16[8,4096]{1,0:T(8,128)(2,1)S(1)}, bf16[8,4096]{1,0:T(8,128)(2,1)S(1)}, u32[]{:S(2)}, u32[]{:S(2)}) collective-permute-start(bf16[8,4096]{1,0:T(8,128)(2,1)S(1)} %copy.194), channel_id=1, source_target_pairs={{0,1},{1,2},{2,3},{3,4},{4,5},{5,6},{6,7},{7,8},{8,9},{9,10},{10,1... | collective-permute-start | bytes 196616 | tf_op jit(solution)/shard_map/while/body/eval_jaxpr/ppermute | solution.py:19
  324.1 10.9 %collective-permute-start.1 = (f32[8,4096]{1,0:T(8,128)S(1)}, f32[8,4096]{1,0:T(8,128)S(1)}, u32[]{:S(2)}, u32[]{:S(2)}) collective-permute-start(f32[8,4096]{1,0:T(8,128)S(1)} %bitcast.167), channel_id=1, source_target_pairs={{0,1},{1,2},{2,3},{3,4},{4,5},{5,6},{6,7},{7,8},{8,9},{9,10},{10,1... | collective-permute-start | bytes 393224 | tf_op jit(solution)/shard_map/while/body/eval_jaxpr/ppermute | solution.py:19
  335.6 17.1 %collective-permute-start = (bf16[8,4096]{1,0:T(8,128)(2,1)S(1)}, bf16[8,4096]{1,0:T(8,128)(2,1)S(1)}, u32[]{:S(2)}, u32[]{:S(2)}) collective-permute-start(bf16[8,4096]{1,0:T(8,128)(2,1)S(1)} %copy.194), channel_id=1, source_target_pairs={{0,1},{1,2},{2,3},{3,4},{4,5},{5,6},{6,7},{7,8},{8,9},{9,10},{10,1... | collective-permute-start | bytes 196616 | tf_op jit(solution)/shard_map/while/body/eval_jaxpr/ppermute | solution.py:19
  341.8 10.9 %collective-permute-start.1 = (f32[8,4096]{1,0:T(8,128)S(1)}, f32[8,4096]{1,0:T(8,128)S(1)}, u32[]{:S(2)}, u32[]{:S(2)}) collective-permute-start(f32[8,4096]{1,0:T(8,128)S(1)} %bitcast.167), channel_id=1, source_target_pairs={{0,1},{1,2},{2,3},{3,4},{4,5},{5,6},{6,7},{7,8},{8,9},{9,10},{10,1... | collective-permute-start | bytes 393224 | tf_op jit(solution)/shard_map/while/body/eval_jaxpr/ppermute | solution.py:19
  353.3 17.1 %collective-permute-start = (bf16[8,4096]{1,0:T(8,128)(2,1)S(1)}, bf16[8,4096]{1,0:T(8,128)(2,1)S(1)}, u32[]{:S(2)}, u32[]{:S(2)}) collective-permute-start(bf16[8,4096]{1,0:T(8,128)(2,1)S(1)} %copy.194), channel_id=1, source_target_pairs={{0,1},{1,2},{2,3},{3,4},{4,5},{5,6},{6,7},{7,8},{8,9},{9,10},{10,1... | collective-permute-start | bytes 196616 | tf_op jit(solution)/shard_map/while/body/eval_jaxpr/ppermute | solution.py:19
  359.6 10.9 %collective-permute-start.1 = (f32[8,4096]{1,0:T(8,128)S(1)}, f32[8,4096]{1,0:T(8,128)S(1)}, u32[]{:S(2)}, u32[]{:S(2)}) collective-permute-start(f32[8,4096]{1,0:T(8,128)S(1)} %bitcast.167), channel_id=1, source_target_pairs={{0,1},{1,2},{2,3},{3,4},{4,5},{5,6},{6,7},{7,8},{8,9},{9,10},{10,1... | collective-permute-start | bytes 393224 | tf_op jit(solution)/shard_map/while/body/eval_jaxpr/ppermute | solution.py:19
  371.0 17.1 %collective-permute-start = (bf16[8,4096]{1,0:T(8,128)(2,1)S(1)}, bf16[8,4096]{1,0:T(8,128)(2,1)S(1)}, u32[]{:S(2)}, u32[]{:S(2)}) collective-permute-start(bf16[8,4096]{1,0:T(8,128)(2,1)S(1)} %copy.194), channel_id=1, source_target_pairs={{0,1},{1,2},{2,3},{3,4},{4,5},{5,6},{6,7},{7,8},{8,9},{9,10},{10,1... | collective-permute-start | bytes 196616 | tf_op jit(solution)/shard_map/while/body/eval_jaxpr/ppermute | solution.py:19
  377.3 10.9 %collective-permute-start.1 = (f32[8,4096]{1,0:T(8,128)S(1)}, f32[8,4096]{1,0:T(8,128)S(1)}, u32[]{:S(2)}, u32[]{:S(2)}) collective-permute-start(f32[8,4096]{1,0:T(8,128)S(1)} %bitcast.167), channel_id=1, source_target_pairs={{0,1},{1,2},{2,3},{3,4},{4,5},{5,6},{6,7},{7,8},{8,9},{9,10},{10,1... | collective-permute-start | bytes 393224 | tf_op jit(solution)/shard_map/while/body/eval_jaxpr/ppermute | solution.py:19
  388.8 17.1 %collective-permute-start = (bf16[8,4096]{1,0:T(8,128)(2,1)S(1)}, bf16[8,4096]{1,0:T(8,128)(2,1)S(1)}, u32[]{:S(2)}, u32[]{:S(2)}) collective-permute-start(bf16[8,4096]{1,0:T(8,128)(2,1)S(1)} %copy.194), channel_id=1, source_target_pairs={{0,1},{1,2},{2,3},{3,4},{4,5},{5,6},{6,7},{7,8},{8,9},{9,10},{10,1... | collective-permute-start | bytes 196616 | tf_op jit(solution)/shard_map/while/body/eval_jaxpr/ppermute | solution.py:19
  395.0 10.9 %collective-permute-start.1 = (f32[8,4096]{1,0:T(8,128)S(1)}, f32[8,4096]{1,0:T(8,128)S(1)}, u32[]{:S(2)}, u32[]{:S(2)}) collective-permute-start(f32[8,4096]{1,0:T(8,128)S(1)} %bitcast.167), channel_id=1, source_target_pairs={{0,1},{1,2},{2,3},{3,4},{4,5},{5,6},{6,7},{7,8},{8,9},{9,10},{10,1... | collective-permute-start | bytes 393224 | tf_op jit(solution)/shard_map/while/body/eval_jaxpr/ppermute | solution.py:19
  406.5 17.1 %collective-permute-start = (bf16[8,4096]{1,0:T(8,128)(2,1)S(1)}, bf16[8,4096]{1,0:T(8,128)(2,1)S(1)}, u32[]{:S(2)}, u32[]{:S(2)}) collective-permute-start(bf16[8,4096]{1,0:T(8,128)(2,1)S(1)} %copy.194), channel_id=1, source_target_pairs={{0,1},{1,2},{2,3},{3,4},{4,5},{5,6},{6,7},{7,8},{8,9},{9,10},{10,1... | collective-permute-start | bytes 196616 | tf_op jit(solution)/shard_map/while/body/eval_jaxpr/ppermute | solution.py:19
  412.7 10.9 %collective-permute-start.1 = (f32[8,4096]{1,0:T(8,128)S(1)}, f32[8,4096]{1,0:T(8,128)S(1)}, u32[]{:S(2)}, u32[]{:S(2)}) collective-permute-start(f32[8,4096]{1,0:T(8,128)S(1)} %bitcast.167), channel_id=1, source_target_pairs={{0,1},{1,2},{2,3},{3,4},{4,5},{5,6},{6,7},{7,8},{8,9},{9,10},{10,1... | collective-permute-start | bytes 393224 | tf_op jit(solution)/shard_map/while/body/eval_jaxpr/ppermute | solution.py:19
  424.2 17.1 %collective-permute-start = (bf16[8,4096]{1,0:T(8,128)(2,1)S(1)}, bf16[8,4096]{1,0:T(8,128)(2,1)S(1)}, u32[]{:S(2)}, u32[]{:S(2)}) collective-permute-start(bf16[8,4096]{1,0:T(8,128)(2,1)S(1)} %copy.194), channel_id=1, source_target_pairs={{0,1},{1,2},{2,3},{3,4},{4,5},{5,6},{6,7},{7,8},{8,9},{9,10},{10,1... | collective-permute-start | bytes 196616 | tf_op jit(solution)/shard_map/while/body/eval_jaxpr/ppermute | solution.py:19
  430.4 10.9 %collective-permute-start.1 = (f32[8,4096]{1,0:T(8,128)S(1)}, f32[8,4096]{1,0:T(8,128)S(1)}, u32[]{:S(2)}, u32[]{:S(2)}) collective-permute-start(f32[8,4096]{1,0:T(8,128)S(1)} %bitcast.167), channel_id=1, source_target_pairs={{0,1},{1,2},{2,3},{3,4},{4,5},{5,6},{6,7},{7,8},{8,9},{9,10},{10,1... | collective-permute-start | bytes 393224 | tf_op jit(solution)/shard_map/while/body/eval_jaxpr/ppermute | solution.py:19
  441.9 17.1 %collective-permute-start = (bf16[8,4096]{1,0:T(8,128)(2,1)S(1)}, bf16[8,4096]{1,0:T(8,128)(2,1)S(1)}, u32[]{:S(2)}, u32[]{:S(2)}) collective-permute-start(bf16[8,4096]{1,0:T(8,128)(2,1)S(1)} %copy.194), channel_id=1, source_target_pairs={{0,1},{1,2},{2,3},{3,4},{4,5},{5,6},{6,7},{7,8},{8,9},{9,10},{10,1... | collective-permute-start | bytes 196616 | tf_op jit(solution)/shard_map/while/body/eval_jaxpr/ppermute | solution.py:19
  448.1 10.9 %collective-permute-start.1 = (f32[8,4096]{1,0:T(8,128)S(1)}, f32[8,4096]{1,0:T(8,128)S(1)}, u32[]{:S(2)}, u32[]{:S(2)}) collective-permute-start(f32[8,4096]{1,0:T(8,128)S(1)} %bitcast.167), channel_id=1, source_target_pairs={{0,1},{1,2},{2,3},{3,4},{4,5},{5,6},{6,7},{7,8},{8,9},{9,10},{10,1... | collective-permute-start | bytes 393224 | tf_op jit(solution)/shard_map/while/body/eval_jaxpr/ppermute | solution.py:19
  459.6 17.1 %collective-permute-start = (bf16[8,4096]{1,0:T(8,128)(2,1)S(1)}, bf16[8,4096]{1,0:T(8,128)(2,1)S(1)}, u32[]{:S(2)}, u32[]{:S(2)}) collective-permute-start(bf16[8,4096]{1,0:T(8,128)(2,1)S(1)} %copy.194), channel_id=1, source_target_pairs={{0,1},{1,2},{2,3},{3,4},{4,5},{5,6},{6,7},{7,8},{8,9},{9,10},{10,1... | collective-permute-start | bytes 196616 | tf_op jit(solution)/shard_map/while/body/eval_jaxpr/ppermute | solution.py:19
  465.8 10.9 %collective-permute-start.1 = (f32[8,4096]{1,0:T(8,128)S(1)}, f32[8,4096]{1,0:T(8,128)S(1)}, u32[]{:S(2)}, u32[]{:S(2)}) collective-permute-start(f32[8,4096]{1,0:T(8,128)S(1)} %bitcast.167), channel_id=1, source_target_pairs={{0,1},{1,2},{2,3},{3,4},{4,5},{5,6},{6,7},{7,8},{8,9},{9,10},{10,1... | collective-permute-start | bytes 393224 | tf_op jit(solution)/shard_map/while/body/eval_jaxpr/ppermute | solution.py:19
  477.3 17.1 %collective-permute-start = (bf16[8,4096]{1,0:T(8,128)(2,1)S(1)}, bf16[8,4096]{1,0:T(8,128)(2,1)S(1)}, u32[]{:S(2)}, u32[]{:S(2)}) collective-permute-start(bf16[8,4096]{1,0:T(8,128)(2,1)S(1)} %copy.194), channel_id=1, source_target_pairs={{0,1},{1,2},{2,3},{3,4},{4,5},{5,6},{6,7},{7,8},{8,9},{9,10},{10,1... | collective-permute-start | bytes 196616 | tf_op jit(solution)/shard_map/while/body/eval_jaxpr/ppermute | solution.py:19
  483.6 10.9 %collective-permute-start.1 = (f32[8,4096]{1,0:T(8,128)S(1)}, f32[8,4096]{1,0:T(8,128)S(1)}, u32[]{:S(2)}, u32[]{:S(2)}) collective-permute-start(f32[8,4096]{1,0:T(8,128)S(1)} %bitcast.167), channel_id=1, source_target_pairs={{0,1},{1,2},{2,3},{3,4},{4,5},{5,6},{6,7},{7,8},{8,9},{9,10},{10,1... | collective-permute-start | bytes 393224 | tf_op jit(solution)/shard_map/while/body/eval_jaxpr/ppermute | solution.py:19
  495.0 17.1 %collective-permute-start = (bf16[8,4096]{1,0:T(8,128)(2,1)S(1)}, bf16[8,4096]{1,0:T(8,128)(2,1)S(1)}, u32[]{:S(2)}, u32[]{:S(2)}) collective-permute-start(bf16[8,4096]{1,0:T(8,128)(2,1)S(1)} %copy.194), channel_id=1, source_target_pairs={{0,1},{1,2},{2,3},{3,4},{4,5},{5,6},{6,7},{7,8},{8,9},{9,10},{10,1... | collective-permute-start | bytes 196616 | tf_op jit(solution)/shard_map/while/body/eval_jaxpr/ppermute | solution.py:19
  501.3 10.9 %collective-permute-start.1 = (f32[8,4096]{1,0:T(8,128)S(1)}, f32[8,4096]{1,0:T(8,128)S(1)}, u32[]{:S(2)}, u32[]{:S(2)}) collective-permute-start(f32[8,4096]{1,0:T(8,128)S(1)} %bitcast.167), channel_id=1, source_target_pairs={{0,1},{1,2},{2,3},{3,4},{4,5},{5,6},{6,7},{7,8},{8,9},{9,10},{10,1... | collective-permute-start | bytes 393224 | tf_op jit(solution)/shard_map/while/body/eval_jaxpr/ppermute | solution.py:19
  512.8 17.1 %collective-permute-start = (bf16[8,4096]{1,0:T(8,128)(2,1)S(1)}, bf16[8,4096]{1,0:T(8,128)(2,1)S(1)}, u32[]{:S(2)}, u32[]{:S(2)}) collective-permute-start(bf16[8,4096]{1,0:T(8,128)(2,1)S(1)} %copy.194), channel_id=1, source_target_pairs={{0,1},{1,2},{2,3},{3,4},{4,5},{5,6},{6,7},{7,8},{8,9},{9,10},{10,1... | collective-permute-start | bytes 196616 | tf_op jit(solution)/shard_map/while/body/eval_jaxpr/ppermute | solution.py:19
  519.0 10.9 %collective-permute-start.1 = (f32[8,4096]{1,0:T(8,128)S(1)}, f32[8,4096]{1,0:T(8,128)S(1)}, u32[]{:S(2)}, u32[]{:S(2)}) collective-permute-start(f32[8,4096]{1,0:T(8,128)S(1)} %bitcast.167), channel_id=1, source_target_pairs={{0,1},{1,2},{2,3},{3,4},{4,5},{5,6},{6,7},{7,8},{8,9},{9,10},{10,1... | collective-permute-start | bytes 393224 | tf_op jit(solution)/shard_map/while/body/eval_jaxpr/ppermute | solution.py:19
  530.5 17.1 %collective-permute-start = (bf16[8,4096]{1,0:T(8,128)(2,1)S(1)}, bf16[8,4096]{1,0:T(8,128)(2,1)S(1)}, u32[]{:S(2)}, u32[]{:S(2)}) collective-permute-start(bf16[8,4096]{1,0:T(8,128)(2,1)S(1)} %copy.194), channel_id=1, source_target_pairs={{0,1},{1,2},{2,3},{3,4},{4,5},{5,6},{6,7},{7,8},{8,9},{9,10},{10,1... | collective-permute-start | bytes 196616 | tf_op jit(solution)/shard_map/while/body/eval_jaxpr/ppermute | solution.py:19
  536.7 10.9 %collective-permute-start.1 = (f32[8,4096]{1,0:T(8,128)S(1)}, f32[8,4096]{1,0:T(8,128)S(1)}, u32[]{:S(2)}, u32[]{:S(2)}) collective-permute-start(f32[8,4096]{1,0:T(8,128)S(1)} %bitcast.167), channel_id=1, source_target_pairs={{0,1},{1,2},{2,3},{3,4},{4,5},{5,6},{6,7},{7,8},{8,9},{9,10},{10,1... | collective-permute-start | bytes 393224 | tf_op jit(solution)/shard_map/while/body/eval_jaxpr/ppermute | solution.py:19
  548.2 17.1 %collective-permute-start = (bf16[8,4096]{1,0:T(8,128)(2,1)S(1)}, bf16[8,4096]{1,0:T(8,128)(2,1)S(1)}, u32[]{:S(2)}, u32[]{:S(2)}) collective-permute-start(bf16[8,4096]{1,0:T(8,128)(2,1)S(1)} %copy.194), channel_id=1, source_target_pairs={{0,1},{1,2},{2,3},{3,4},{4,5},{5,6},{6,7},{7,8},{8,9},{9,10},{10,1... | collective-permute-start | bytes 196616 | tf_op jit(solution)/shard_map/while/body/eval_jaxpr/ppermute | solution.py:19
  554.4 10.9 %collective-permute-start.1 = (f32[8,4096]{1,0:T(8,128)S(1)}, f32[8,4096]{1,0:T(8,128)S(1)}, u32[]{:S(2)}, u32[]{:S(2)}) collective-permute-start(f32[8,4096]{1,0:T(8,128)S(1)} %bitcast.167), channel_id=1, source_target_pairs={{0,1},{1,2},{2,3},{3,4},{4,5},{5,6},{6,7},{7,8},{8,9},{9,10},{10,1... | collective-permute-start | bytes 393224 | tf_op jit(solution)/shard_map/while/body/eval_jaxpr/ppermute | solution.py:19
  565.9 17.1 %collective-permute-start = (bf16[8,4096]{1,0:T(8,128)(2,1)S(1)}, bf16[8,4096]{1,0:T(8,128)(2,1)S(1)}, u32[]{:S(2)}, u32[]{:S(2)}) collective-permute-start(bf16[8,4096]{1,0:T(8,128)(2,1)S(1)} %copy.194), channel_id=1, source_target_pairs={{0,1},{1,2},{2,3},{3,4},{4,5},{5,6},{6,7},{7,8},{8,9},{9,10},{10,1... | collective-permute-start | bytes 196616 | tf_op jit(solution)/shard_map/while/body/eval_jaxpr/ppermute | solution.py:19
  572.1 10.9 %collective-permute-start.1 = (f32[8,4096]{1,0:T(8,128)S(1)}, f32[8,4096]{1,0:T(8,128)S(1)}, u32[]{:S(2)}, u32[]{:S(2)}) collective-permute-start(f32[8,4096]{1,0:T(8,128)S(1)} %bitcast.167), channel_id=1, source_target_pairs={{0,1},{1,2},{2,3},{3,4},{4,5},{5,6},{6,7},{7,8},{8,9},{9,10},{10,1... | collective-permute-start | bytes 393224 | tf_op jit(solution)/shard_map/while/body/eval_jaxpr/ppermute | solution.py:19
  583.6 17.1 %collective-permute-start = (bf16[8,4096]{1,0:T(8,128)(2,1)S(1)}, bf16[8,4096]{1,0:T(8,128)(2,1)S(1)}, u32[]{:S(2)}, u32[]{:S(2)}) collective-permute-start(bf16[8,4096]{1,0:T(8,128)(2,1)S(1)} %copy.194), channel_id=1, source_target_pairs={{0,1},{1,2},{2,3},{3,4},{4,5},{5,6},{6,7},{7,8},{8,9},{9,10},{10,1... | collective-permute-start | bytes 196616 | tf_op jit(solution)/shard_map/while/body/eval_jaxpr/ppermute | solution.py:19
  589.8 10.9 %collective-permute-start.1 = (f32[8,4096]{1,0:T(8,128)S(1)}, f32[8,4096]{1,0:T(8,128)S(1)}, u32[]{:S(2)}, u32[]{:S(2)}) collective-permute-start(f32[8,4096]{1,0:T(8,128)S(1)} %bitcast.167), channel_id=1, source_target_pairs={{0,1},{1,2},{2,3},{3,4},{4,5},{5,6},{6,7},{7,8},{8,9},{9,10},{10,1... | collective-permute-start | bytes 393224 | tf_op jit(solution)/shard_map/while/body/eval_jaxpr/ppermute | solution.py:19
  601.3 17.1 %collective-permute-start = (bf16[8,4096]{1,0:T(8,128)(2,1)S(1)}, bf16[8,4096]{1,0:T(8,128)(2,1)S(1)}, u32[]{:S(2)}, u32[]{:S(2)}) collective-permute-start(bf16[8,4096]{1,0:T(8,128)(2,1)S(1)} %copy.194), channel_id=1, source_target_pairs={{0,1},{1,2},{2,3},{3,4},{4,5},{5,6},{6,7},{7,8},{8,9},{9,10},{10,1... | collective-permute-start | bytes 196616 | tf_op jit(solution)/shard_map/while/body/eval_jaxpr/ppermute | solution.py:19
  607.6 10.9 %collective-permute-start.1 = (f32[8,4096]{1,0:T(8,128)S(1)}, f32[8,4096]{1,0:T(8,128)S(1)}, u32[]{:S(2)}, u32[]{:S(2)}) collective-permute-start(f32[8,4096]{1,0:T(8,128)S(1)} %bitcast.167), channel_id=1, source_target_pairs={{0,1},{1,2},{2,3},{3,4},{4,5},{5,6},{6,7},{7,8},{8,9},{9,10},{10,1... | collective-permute-start | bytes 393224 | tf_op jit(solution)/shard_map/while/body/eval_jaxpr/ppermute | solution.py:19
  619.1 17.1 %collective-permute-start = (bf16[8,4096]{1,0:T(8,128)(2,1)S(1)}, bf16[8,4096]{1,0:T(8,128)(2,1)S(1)}, u32[]{:S(2)}, u32[]{:S(2)}) collective-permute-start(bf16[8,4096]{1,0:T(8,128)(2,1)S(1)} %copy.194), channel_id=1, source_target_pairs={{0,1},{1,2},{2,3},{3,4},{4,5},{5,6},{6,7},{7,8},{8,9},{9,10},{10,1... | collective-permute-start | bytes 196616 | tf_op jit(solution)/shard_map/while/body/eval_jaxpr/ppermute | solution.py:19
  625.3 10.9 %collective-permute-start.1 = (f32[8,4096]{1,0:T(8,128)S(1)}, f32[8,4096]{1,0:T(8,128)S(1)}, u32[]{:S(2)}, u32[]{:S(2)}) collective-permute-start(f32[8,4096]{1,0:T(8,128)S(1)} %bitcast.167), channel_id=1, source_target_pairs={{0,1},{1,2},{2,3},{3,4},{4,5},{5,6},{6,7},{7,8},{8,9},{9,10},{10,1... | collective-permute-start | bytes 393224 | tf_op jit(solution)/shard_map/while/body/eval_jaxpr/ppermute | solution.py:19
  636.8 17.1 %collective-permute-start = (bf16[8,4096]{1,0:T(8,128)(2,1)S(1)}, bf16[8,4096]{1,0:T(8,128)(2,1)S(1)}, u32[]{:S(2)}, u32[]{:S(2)}) collective-permute-start(bf16[8,4096]{1,0:T(8,128)(2,1)S(1)} %copy.194), channel_id=1, source_target_pairs={{0,1},{1,2},{2,3},{3,4},{4,5},{5,6},{6,7},{7,8},{8,9},{9,10},{10,1... | collective-permute-start | bytes 196616 | tf_op jit(solution)/shard_map/while/body/eval_jaxpr/ppermute | solution.py:19
  643.0 10.9 %collective-permute-start.1 = (f32[8,4096]{1,0:T(8,128)S(1)}, f32[8,4096]{1,0:T(8,128)S(1)}, u32[]{:S(2)}, u32[]{:S(2)}) collective-permute-start(f32[8,4096]{1,0:T(8,128)S(1)} %bitcast.167), channel_id=1, source_target_pairs={{0,1},{1,2},{2,3},{3,4},{4,5},{5,6},{6,7},{7,8},{8,9},{9,10},{10,1... | collective-permute-start | bytes 393224 | tf_op jit(solution)/shard_map/while/body/eval_jaxpr/ppermute | solution.py:19
  654.5 17.1 %collective-permute-start = (bf16[8,4096]{1,0:T(8,128)(2,1)S(1)}, bf16[8,4096]{1,0:T(8,128)(2,1)S(1)}, u32[]{:S(2)}, u32[]{:S(2)}) collective-permute-start(bf16[8,4096]{1,0:T(8,128)(2,1)S(1)} %copy.194), channel_id=1, source_target_pairs={{0,1},{1,2},{2,3},{3,4},{4,5},{5,6},{6,7},{7,8},{8,9},{9,10},{10,1... | collective-permute-start | bytes 196616 | tf_op jit(solution)/shard_map/while/body/eval_jaxpr/ppermute | solution.py:19
  660.7 10.9 %collective-permute-start.1 = (f32[8,4096]{1,0:T(8,128)S(1)}, f32[8,4096]{1,0:T(8,128)S(1)}, u32[]{:S(2)}, u32[]{:S(2)}) collective-permute-start(f32[8,4096]{1,0:T(8,128)S(1)} %bitcast.167), channel_id=1, source_target_pairs={{0,1},{1,2},{2,3},{3,4},{4,5},{5,6},{6,7},{7,8},{8,9},{9,10},{10,1... | collective-permute-start | bytes 393224 | tf_op jit(solution)/shard_map/while/body/eval_jaxpr/ppermute | solution.py:19
  672.2 17.1 %collective-permute-start = (bf16[8,4096]{1,0:T(8,128)(2,1)S(1)}, bf16[8,4096]{1,0:T(8,128)(2,1)S(1)}, u32[]{:S(2)}, u32[]{:S(2)}) collective-permute-start(bf16[8,4096]{1,0:T(8,128)(2,1)S(1)} %copy.194), channel_id=1, source_target_pairs={{0,1},{1,2},{2,3},{3,4},{4,5},{5,6},{6,7},{7,8},{8,9},{9,10},{10,1... | collective-permute-start | bytes 196616 | tf_op jit(solution)/shard_map/while/body/eval_jaxpr/ppermute | solution.py:19
  678.4 10.9 %collective-permute-start.1 = (f32[8,4096]{1,0:T(8,128)S(1)}, f32[8,4096]{1,0:T(8,128)S(1)}, u32[]{:S(2)}, u32[]{:S(2)}) collective-permute-start(f32[8,4096]{1,0:T(8,128)S(1)} %bitcast.167), channel_id=1, source_target_pairs={{0,1},{1,2},{2,3},{3,4},{4,5},{5,6},{6,7},{7,8},{8,9},{9,10},{10,1... | collective-permute-start | bytes 393224 | tf_op jit(solution)/shard_map/while/body/eval_jaxpr/ppermute | solution.py:19
  689.9 17.1 %collective-permute-start = (bf16[8,4096]{1,0:T(8,128)(2,1)S(1)}, bf16[8,4096]{1,0:T(8,128)(2,1)S(1)}, u32[]{:S(2)}, u32[]{:S(2)}) collective-permute-start(bf16[8,4096]{1,0:T(8,128)(2,1)S(1)} %copy.194), channel_id=1, source_target_pairs={{0,1},{1,2},{2,3},{3,4},{4,5},{5,6},{6,7},{7,8},{8,9},{9,10},{10,1... | collective-permute-start | bytes 196616 | tf_op jit(solution)/shard_map/while/body/eval_jaxpr/ppermute | solution.py:19
  696.1 10.9 %collective-permute-start.1 = (f32[8,4096]{1,0:T(8,128)S(1)}, f32[8,4096]{1,0:T(8,128)S(1)}, u32[]{:S(2)}, u32[]{:S(2)}) collective-permute-start(f32[8,4096]{1,0:T(8,128)S(1)} %bitcast.167), channel_id=1, source_target_pairs={{0,1},{1,2},{2,3},{3,4},{4,5},{5,6},{6,7},{7,8},{8,9},{9,10},{10,1... | collective-permute-start | bytes 393224 | tf_op jit(solution)/shard_map/while/body/eval_jaxpr/ppermute | solution.py:19
  707.6 17.1 %collective-permute-start = (bf16[8,4096]{1,0:T(8,128)(2,1)S(1)}, bf16[8,4096]{1,0:T(8,128)(2,1)S(1)}, u32[]{:S(2)}, u32[]{:S(2)}) collective-permute-start(bf16[8,4096]{1,0:T(8,128)(2,1)S(1)} %copy.194), channel_id=1, source_target_pairs={{0,1},{1,2},{2,3},{3,4},{4,5},{5,6},{6,7},{7,8},{8,9},{9,10},{10,1... | collective-permute-start | bytes 196616 | tf_op jit(solution)/shard_map/while/body/eval_jaxpr/ppermute | solution.py:19
  713.9 10.9 %collective-permute-start.1 = (f32[8,4096]{1,0:T(8,128)S(1)}, f32[8,4096]{1,0:T(8,128)S(1)}, u32[]{:S(2)}, u32[]{:S(2)}) collective-permute-start(f32[8,4096]{1,0:T(8,128)S(1)} %bitcast.167), channel_id=1, source_target_pairs={{0,1},{1,2},{2,3},{3,4},{4,5},{5,6},{6,7},{7,8},{8,9},{9,10},{10,1... | collective-permute-start | bytes 393224 | tf_op jit(solution)/shard_map/while/body/eval_jaxpr/ppermute | solution.py:19
  725.3 17.1 %collective-permute-start = (bf16[8,4096]{1,0:T(8,128)(2,1)S(1)}, bf16[8,4096]{1,0:T(8,128)(2,1)S(1)}, u32[]{:S(2)}, u32[]{:S(2)}) collective-permute-start(bf16[8,4096]{1,0:T(8,128)(2,1)S(1)} %copy.194), channel_id=1, source_target_pairs={{0,1},{1,2},{2,3},{3,4},{4,5},{5,6},{6,7},{7,8},{8,9},{9,10},{10,1... | collective-permute-start | bytes 196616 | tf_op jit(solution)/shard_map/while/body/eval_jaxpr/ppermute | solution.py:19
  731.6 10.9 %collective-permute-start.1 = (f32[8,4096]{1,0:T(8,128)S(1)}, f32[8,4096]{1,0:T(8,128)S(1)}, u32[]{:S(2)}, u32[]{:S(2)}) collective-permute-start(f32[8,4096]{1,0:T(8,128)S(1)} %bitcast.167), channel_id=1, source_target_pairs={{0,1},{1,2},{2,3},{3,4},{4,5},{5,6},{6,7},{7,8},{8,9},{9,10},{10,1... | collective-permute-start | bytes 393224 | tf_op jit(solution)/shard_map/while/body/eval_jaxpr/ppermute | solution.py:19
  743.1 17.1 %collective-permute-start = (bf16[8,4096]{1,0:T(8,128)(2,1)S(1)}, bf16[8,4096]{1,0:T(8,128)(2,1)S(1)}, u32[]{:S(2)}, u32[]{:S(2)}) collective-permute-start(bf16[8,4096]{1,0:T(8,128)(2,1)S(1)} %copy.194), channel_id=1, source_target_pairs={{0,1},{1,2},{2,3},{3,4},{4,5},{5,6},{6,7},{7,8},{8,9},{9,10},{10,1... | collective-permute-start | bytes 196616 | tf_op jit(solution)/shard_map/while/body/eval_jaxpr/ppermute | solution.py:19
  749.3 10.9 %collective-permute-start.1 = (f32[8,4096]{1,0:T(8,128)S(1)}, f32[8,4096]{1,0:T(8,128)S(1)}, u32[]{:S(2)}, u32[]{:S(2)}) collective-permute-start(f32[8,4096]{1,0:T(8,128)S(1)} %bitcast.167), channel_id=1, source_target_pairs={{0,1},{1,2},{2,3},{3,4},{4,5},{5,6},{6,7},{7,8},{8,9},{9,10},{10,1... | collective-permute-start | bytes 393224 | tf_op jit(solution)/shard_map/while/body/eval_jaxpr/ppermute | solution.py:19
  760.8 17.1 %collective-permute-start = (bf16[8,4096]{1,0:T(8,128)(2,1)S(1)}, bf16[8,4096]{1,0:T(8,128)(2,1)S(1)}, u32[]{:S(2)}, u32[]{:S(2)}) collective-permute-start(bf16[8,4096]{1,0:T(8,128)(2,1)S(1)} %copy.194), channel_id=1, source_target_pairs={{0,1},{1,2},{2,3},{3,4},{4,5},{5,6},{6,7},{7,8},{8,9},{9,10},{10,1... | collective-permute-start | bytes 196616 | tf_op jit(solution)/shard_map/while/body/eval_jaxpr/ppermute | solution.py:19
  767.0 10.9 %collective-permute-start.1 = (f32[8,4096]{1,0:T(8,128)S(1)}, f32[8,4096]{1,0:T(8,128)S(1)}, u32[]{:S(2)}, u32[]{:S(2)}) collective-permute-start(f32[8,4096]{1,0:T(8,128)S(1)} %bitcast.167), channel_id=1, source_target_pairs={{0,1},{1,2},{2,3},{3,4},{4,5},{5,6},{6,7},{7,8},{8,9},{9,10},{10,1... | collective-permute-start | bytes 393224 | tf_op jit(solution)/shard_map/while/body/eval_jaxpr/ppermute | solution.py:19
  778.5 17.1 %collective-permute-start = (bf16[8,4096]{1,0:T(8,128)(2,1)S(1)}, bf16[8,4096]{1,0:T(8,128)(2,1)S(1)}, u32[]{:S(2)}, u32[]{:S(2)}) collective-permute-start(bf16[8,4096]{1,0:T(8,128)(2,1)S(1)} %copy.194), channel_id=1, source_target_pairs={{0,1},{1,2},{2,3},{3,4},{4,5},{5,6},{6,7},{7,8},{8,9},{9,10},{10,1... | collective-permute-start | bytes 196616 | tf_op jit(solution)/shard_map/while/body/eval_jaxpr/ppermute | solution.py:19
  784.7 10.9 %collective-permute-start.1 = (f32[8,4096]{1,0:T(8,128)S(1)}, f32[8,4096]{1,0:T(8,128)S(1)}, u32[]{:S(2)}, u32[]{:S(2)}) collective-permute-start(f32[8,4096]{1,0:T(8,128)S(1)} %bitcast.167), channel_id=1, source_target_pairs={{0,1},{1,2},{2,3},{3,4},{4,5},{5,6},{6,7},{7,8},{8,9},{9,10},{10,1... | collective-permute-start | bytes 393224 | tf_op jit(solution)/shard_map/while/body/eval_jaxpr/ppermute | solution.py:19
  796.2 17.1 %collective-permute-start = (bf16[8,4096]{1,0:T(8,128)(2,1)S(1)}, bf16[8,4096]{1,0:T(8,128)(2,1)S(1)}, u32[]{:S(2)}, u32[]{:S(2)}) collective-permute-start(bf16[8,4096]{1,0:T(8,128)(2,1)S(1)} %copy.194), channel_id=1, source_target_pairs={{0,1},{1,2},{2,3},{3,4},{4,5},{5,6},{6,7},{7,8},{8,9},{9,10},{10,1... | collective-permute-start | bytes 196616 | tf_op jit(solution)/shard_map/while/body/eval_jaxpr/ppermute | solution.py:19
  802.4 10.9 %collective-permute-start.1 = (f32[8,4096]{1,0:T(8,128)S(1)}, f32[8,4096]{1,0:T(8,128)S(1)}, u32[]{:S(2)}, u32[]{:S(2)}) collective-permute-start(f32[8,4096]{1,0:T(8,128)S(1)} %bitcast.167), channel_id=1, source_target_pairs={{0,1},{1,2},{2,3},{3,4},{4,5},{5,6},{6,7},{7,8},{8,9},{9,10},{10,1... | collective-permute-start | bytes 393224 | tf_op jit(solution)/shard_map/while/body/eval_jaxpr/ppermute | solution.py:19
  (105 other events, 558.6 us)
Sparse Core Ops, SparseCore 0:
  37.0 218.1 reduce-scatter.1
where the time goes:
time: 843 us; the launch traced here: 836 us
  waiting for transfers between devices  421 us (50%)
  local copies, waits for them, and re-layouts  205 us (24%)
  other arithmetic  101 us (12%)
  matrix products  73.9 us (9%)
  starting transfers between devices  17.3 us (2%)
  between operations  14.3 us (2%)
    ppermute x126, waiting for transfers between devices, passed_along(): lax.ppermute(shard, axis, [(i, (i + by) % peers) for i in range(peers)])  219 us
    all_to_all x1, waiting for transfers between devices, on_device(): lax.all_to_all(outgoing, 'owner', split_axis=0, concat_axis=0, tiled=True)  110 us
    reduce_scatter x1, waiting for transfers between devices, on_device(): lax.psum_scatter(jnp.dot(local_rows, kv_weight, preferred_element_type=jn...  92.4 us
    reduce_sum x64, local copies, waits for them, and re-layouts, absorb(): jnp.sum(weights, axis=3)  62 us
    dot_general x32, matrix products, absorb(): jnp.einsum('kgrt,tkd->rkgd', weights.astype(jnp.bfloat16), value_rows, pr...  51.5 us
    gather x32, local copies, waits for them, and re-layouts, absorb(): allowed = jnp.take(mask_cols, query_pos // BLK, axis=0)  46.7 us
    reshape x32, local copies, waits for them, and re-layouts, absorb(): running = running.reshape(KVH, per_group, row_count)  24.3 us
    and x32, other arithmetic, absorb(): allowed = jnp.take(mask_cols, query_pos // BLK, axis=0)  24 us
  transfers between devices with their start and end apart: 128, of which 34 were waited for; matrix products, arithmetic and copies ran while one was open for 40% of the time, Pallas kernels for 0%

commit v1 on v0

v1 whole, which is shorter than its diff:
```python
import jax
import jax.numpy as jnp
from jax import lax
from jax.sharding import PartitionSpec as P

QH = 32
KVH = 4
HD = 128
BLK = 128
NBD = 8
RCP = 8
SLOTS = 8
CAP = 4
CTX_DEV = 1024


def on_device(span_cache, retrieval, counts, recompute_pos, hidden, kv_weight, queries, block_mask):
    owner_count = lax.axis_size("owner")
    cycle_size = lax.axis_size("ctx")
    my_owner = lax.axis_index("owner")
    my_ctx = lax.axis_index("ctx")
    feature_count = span_cache.shape[2]
    positions = jnp.arange(NBD, dtype=jnp.int32)
    block_ids = my_ctx * NBD + positions
    in_use = block_ids[None, :] < counts[:, None]
    holder = retrieval // (cycle_size * SLOTS)
    outbound = in_use & (holder == my_owner)
    slot_rank = jnp.cumsum(outbound.astype(jnp.int32), axis=1) - 1
    picked = outbound[:, None, :] & (
        slot_rank[:, None, :] == jnp.arange(CAP, dtype=jnp.int32)[None, :, None]
    )
    chosen = jnp.sum(jnp.where(picked, (retrieval % SLOTS)[:, None, :], 0), axis=2)
    filled = jnp.any(picked, axis=2)
    outgoing = jnp.where(
        filled[:, :, None, None], jnp.take(span_cache, chosen, axis=0), jnp.zeros((), jnp.bfloat16)
    )
    arrived = lax.all_to_all(outgoing, "owner", split_axis=0, concat_axis=0, tiled=True)
    wanted = lax.dynamic_index_in_dim(retrieval, my_owner, 0, keepdims=False)
    my_count = lax.dynamic_index_in_dim(counts, my_owner, 0, keepdims=False)
    my_in_use = block_ids < my_count
    source = wanted // (cycle_size * SLOTS)
    earlier = (
        (source[:, None] == source[None, :])
        & my_in_use[None, :]
        & (positions[None, :] < positions[:, None])
    )
    ordinal = jnp.sum(earlier.astype(jnp.int32), axis=1)
    flattened = arrived.reshape(owner_count * CAP, BLK, feature_count)
    blocks = jnp.take(flattened, source * CAP + ordinal, axis=0, mode="clip")
    blocks = jnp.where(my_in_use[:, None, None], blocks, jnp.zeros((), jnp.bfloat16))
    context = blocks.reshape(CTX_DEV, feature_count)
    local_rows = hidden[0]
    recomputed = lax.psum_scatter(
        jnp.dot(local_rows, kv_weight, preferred_element_type=jnp.float32).astype(jnp.bfloat16),
        "ctx",
        scatter_dimension=0,
        tiled=True,
    )
    every_pos = recompute_pos[0]
    own_pos = lax.dynamic_slice_in_dim(every_pos, my_ctx * RCP, RCP)
    matches = jnp.arange(CTX_DEV, dtype=jnp.int32)[:, None] == own_pos[None, :]
    placed = jnp.dot(
        matches.astype(jnp.bfloat16), recomputed, preferred_element_type=jnp.float32
    ).astype(jnp.bfloat16)
    context = jnp.where(jnp.any(matches, axis=1)[:, None], placed, context)
    key_width = KVH * HD
    key_rows = context[:, :key_width].reshape(CTX_DEV, KVH, HD)
    value_rows = context[:, key_width:].reshape(CTX_DEV, KVH, HD)
    key_pos = my_ctx * CTX_DEV + jnp.arange(CTX_DEV, dtype=jnp.int32)
    key_in_use = key_pos // BLK < my_count
    mask_cols = block_mask[0]
    query_count = cycle_size * RCP
    query_pos = jnp.arange(query_count, dtype=jnp.int32) // RCP * CTX_DEV + every_pos
    all_queries = lax.all_gather(queries[0], "ctx", axis=0, tiled=True)
    per_group = QH // KVH
    allowed = jnp.take(mask_cols, query_pos // BLK, axis=0)
    visible = jnp.repeat(allowed, BLK, axis=1) > 0
    visible = visible & key_in_use[None, :] & (key_pos[None, :] <= query_pos[:, None])
    grouped = all_queries.reshape(query_count, KVH, per_group, HD)
    scores = jnp.einsum(
        "rkgd,tkd->kgrt", grouped, key_rows, preferred_element_type=jnp.float32
    ) * HD ** (-0.5)
    scores = jnp.where(visible[None, None], scores, -1e30)
    local_max = jnp.max(scores, axis=3)
    weights = jnp.where(visible[None, None], jnp.exp(scores - local_max[..., None]), 0.0)
    local_sum = jnp.sum(weights, axis=3)
    weighted = jnp.einsum(
        "kgrt,tkd->rkgd",
        weights.astype(jnp.bfloat16),
        value_rows,
        preferred_element_type=jnp.float32,
    )
    global_max = lax.pmax(local_max, "ctx")
    factor = jnp.exp(local_max - global_max)
    numerator = weighted * jnp.transpose(factor, (2, 0, 1))[..., None]
    totals = jnp.transpose(local_sum * factor, (2, 0, 1)).reshape(query_count, QH)
    reduced = lax.psum_scatter(numerator.reshape(query_count, QH * HD), "ctx", scatter_dimension=0, tiled=True)
    reduced_totals = lax.psum_scatter(totals, "ctx", scatter_dimension=0, tiled=True)
    result = reduced.reshape(RCP, QH, HD) / reduced_totals[:, :, None]
    attended = result.reshape(RCP, QH * HD).astype(jnp.bfloat16)
    return (context[None], attended[None])


def solution(mesh):
    in_specs = (
        P(("owner", "ctx"), None, None),
        P(None, "ctx"),
        P(),
        P("owner", None),
        P("owner", None, "ctx"),
        P("ctx", None),
        P("owner", "ctx", None),
        P("owner", None, "ctx"),
    )
    out_specs = (P("owner", "ctx", None), P("owner", "ctx", None))
    return jax.shard_map(
        on_device, mesh=mesh, in_specs=in_specs, out_specs=out_specs, check_vma=False
    )
```

time: 843 us -> 758 us (0.90)
  blocking collectives: 0 us -> 267 us
  local copies, waits for them, and re-layouts: 205 us -> 32 us
  other arithmetic: 101 us -> 30.4 us
  waiting for transfers between devices: 421 us -> 368 us
  matrix products: 73.9 us -> 34.5 us
    all_gather x0 -> x1, waiting for transfers between devices: none -> 222 us  [on_device(): all_queries = lax.all_gather(queries[0], 'ctx', axis=0, tiled=True)]
    ppermute x126 -> x0, waiting for transfers between devices: 219 us -> none  [passed_along(): lax.ppermute(shard, axis, [(i, (i + by) % peers) for i in range(peers)])]
    unnamed x0 -> x1, blocking collectives: none -> 134 us
    pmax x0 -> x1, blocking collectives: none -> 133 us  [on_device(): global_max = lax.pmax(local_max, 'ctx')]
    all_to_all x1, waiting for transfers between devices: 110 us -> 0.01 us  [on_device(): lax.all_to_all(outgoing, 'owner', split_axis=0, concat_axis=0, tiled=True)]
    reduce_sum x64 -> x0, local copies, waits for them, and re-layouts: 62 us -> none  [absorb(): jnp.sum(weights, axis=3)]
    gather x32 -> x2, local copies, waits for them, and re-layouts: 46.7 us -> 0.78 us  [on_device(): allowed = jnp.take(mask_cols, query_pos // BLK, axis=0)]
    dot_general x64 -> x2, matrix products: 70.4 us -> 31.1 us  [the longest x1 16 us: on_device(): jnp.einsum('kgrt,tkd->rkgd', weights.astype(jnp.bfloat16), value_rows, pr...]
  transfers between devices with their start and end apart: 128 -> 4, of which waited for: 34 -> 3; matrix products, arithmetic and copies ran while one was open for 40% -> 3% of each run, Pallas kernels for 0% -> 0%
where the time goes in v1:
time: 758 us; the launch traced here: 759 us
  waiting for transfers between devices  368 us (49%)
  blocking collectives  267 us (35%)
  matrix products  34.5 us (5%)
  local copies, waits for them, and re-layouts  32 us (4%)
  other arithmetic  30.4 us (4%)
  between operations  14.6 us (2%)
  starting transfers between devices  11.6 us (2%)
    all_gather x1, waiting for transfers between devices, on_device(): all_queries = lax.all_gather(queries[0], 'ctx', axis=0, tiled=True)  222 us
    unnamed x1, blocking collectives  134 us
    pmax x1, blocking collectives, on_device(): global_max = lax.pmax(local_max, 'ctx')  133 us
    reduce_scatter x1, waiting for transfers between devices, on_device(): lax.psum_scatter(jnp.dot(local_rows, kv_weight, preferred_element_type=jn...  131 us
    dot_general x1, matrix products, on_device(): jnp.einsum('kgrt,tkd->rkgd', weights.astype(jnp.bfloat16), value_rows, pr...  16 us
  transfers between devices with their start and end apart: 4, of which 3 were waited for; matrix products, arithmetic and copies ran while one was open for 3% of the time, Pallas kernels for 0%

profile of v1, /device:TPU:6, one launch (start us, length us, event | category | flops | bytes accessed | tf_op | source)
XLA Modules:
  0.0 758.9 jit_solution(11337647794066189962)
XLA Ops:
  7.2 0.0 copy-start
  7.2 0.9 fusion.35
  8.1 0.2 reduce_window_sum.11
  8.3 0.7 add_select_fusion.1
  9.0 0.1 select_reduce_fusion
  9.1 0.1 fusion.15
  9.3 0.1 copy.54
  9.4 0.1 reshape.358
  9.5 0.1 copy.53
  9.6 0.1 copy.52
  9.7 0.0 copy-done
  9.7 4.7 gather_fusion
  14.4 7.6 select_select_fusion
  22.0 0.0 copy-start.6
  22.0 11.5 %all-to-all-start = ((bf16[8,4,128,1024]{3,2,1,0:T(8,128)(2,1)}), bf16[8,4,128,1024]{3,2,1,0:T(8,128)(2,1)}, u32[]{:S(2)}, u32[]{:S(2)}) async-start(bf16[8,4,128,1024]{3,2,1,0:T(8,128)(2,1)} %select_select_fusion), calls=%async_computation.1 | async-start | bytes 16777216 | tf_op jit(solution)/shard_map/all_to_all | solution.py:37
  33.5 0.0 all-gather.3.cloned.1.call-start
  33.5 0.7 all-gather.3.cloned.1.call-update
  34.2 0.0 reduce-scatter.4.cloned.1.call-start
  34.3 0.0 copy-done.3
  34.3 0.0 copy-done.4
  34.3 1.1 convolution_convert_fusion
  35.4 0.0 reduce-scatter.4.cloned.1.call-update
  35.4 0.0 reduce-scatter.6.cloned.1.call-start
  35.5 0.0 copy-done.7
  35.5 0.6 dynamic_slice.12
  36.1 0.0 copy-done.5
  36.1 0.1 copy.56
  36.2 0.0 copy-done.6
  36.3 0.7 gather_fusion.2
  37.0 0.1 copy.57
  37.0 0.7 broadcast_compare_fusion
  37.7 0.7 fusion.20
  38.4 0.7 and_select_fusion.5
  39.1 0.3 fusion.8
  39.5 0.7 fusion.30
  40.2 0.1 dynamic-slice_bitcast_fusion
  40.2 0.2 convert_reduce_fusion
  40.4 0.7 fusion.29
  41.1 0.1 fusion.12
  41.2 0.1 broadcast_bitcast_fusion
  41.3 222.5 %all-gather.3.cloned.1.call-done = bf16[1,256,4096]{2,1,0:T(8,128)(2,1)} async-done(((bf16[1,8,4096]{2,1,0:T(8,128)(2,1)}), bf16[1,256,4096]{2,1,0:T(8,128)(2,1)}) %all-gather.3.cloned.1.call-update) | async-done | bytes 2097168 | tf_op jit(solution)/shard_map/all_gather | solution.py:74
  263.8 4.1 copy.58
  267.8 0.0 all-to-all-done
  267.8 5.4 gather_fusion.1
  273.2 4.0 copy.68
  277.2 130.9 %reduce-scatter.4.cloned.1.call-done = bf16[8,1024]{1,0:T(8,128)(2,1)} async-done(((bf16[256,1024]{1,0:T(8,128)(2,1)}), bf16[8,1024]{1,0:T(8,128)(2,1)}) %reduce-scatter.4.cloned.1.call-update) | async-done | bytes 16400 | tf_op jit(solution)/shard_map/reduce_scatter | solution.py:53
  408.0 2.4 select_select_fusion.1
  410.4 0.0 copy-start.2
  410.4 1.3 copy-done.2
  411.7 0.2 fusion.36
  411.9 15.1 %fusion = (f32[4,8,256]{2,1,0:T(8,128)S(1)}, f32[4,1024,256,8]{2,1,3,0:T(8,128)}) fusion(pred[256,1024]{0,1:T(8,128)(4,1)S(1)} %fusion.8, bf16[1024,4,128,1]{0,2,3,1:T(8,128)(2,1)S(1)} %bitcast.110, bf16[256,4,8,128]{0,3,2,1:T(8,128)(2,1)} %bitcast.108), kind=kOutput, calls=%fused_computation.5 | convolution fusion | flops 2172641280 | bytes 36995072 | tf_op jit(solution)/shard_map/rkgd,tkd->kgrt/dot_general | solution.py:80
  426.9 133.5 %pmax.7 = f32[4,8,256]{2,1,0:T(8,128)S(1)} all-reduce(f32[4,8,256]{2,1,0:T(8,128)S(1)} %get-tuple-element.20), channel_id=1, replica_groups=mesh['owner'=8,'ctx'=32] {'ctx'}, use_global_device_ids=true, to_apply=%region_7.8 | all-reduce | flops 8192 | bytes 65536 | tf_op jit(solution)/shard_map/pmax | solution.py:93
  560.4 15.0 %fusion.1 = f32[4,8,256]{2,1,0:T(8,128)S(1)} fusion(f32[4,1024,256,8]{2,1,3,0:T(8,128)} %get-tuple-element.21, f32[4,8,256]{2,1,0:T(8,128)S(1)} %get-tuple-element.20, pred[256,1024]{0,1:T(8,128)(4,1)S(1)} %fusion.8), kind=kLoop, calls=%fused_computation.6 | loop fusion | flops 41934848 | bytes 33882112 | tf_op jit(solution)/shard_map/reduce_sum | solution.py:86
  575.4 16.0 %bitcast_multiply_fusion = f32[256,4,8,128]{0,3,2,1:T(8,128)} fusion(bf16[1024,4,128,1]{0,2,3,1:T(8,128)(2,1)S(1)} %bitcast.111, f32[4,1024,256,8]{2,1,3,0:T(8,128)} %get-tuple-element.21, f32[4,8,256]{2,1,0:T(8,128)S(1)} %get-tuple-element.20, pred[256,1024]{0,1:T(8,128)(4,1)S(1)} %fusion.8, f32[256,4,8]{0,2,1:T(8,128)S(1)} %get-tuple-element.19), kind=kOutput, calls=%fused_computation.11 | convolution fusion | flops 2190475264 | bytes 39124992 | tf_op jit(solution)/shard_map/kgrt,tkd->rkgd/dot_general | solution.py:87
  591.5 5.8 copy.62
  597.2 0.0 reduce-scatter.6.cloned.1.call-update
  597.3 0.0 copy-done.8
  597.3 0.6 dynamic-slice.1
  598.5 3.9 copy.63
  602.4 133.8 %all-reduce = f32[256,32]{0,1:T(8,128)S(1)} all-reduce(f32[256,32]{0,1:T(8,128)S(1)} %get-tuple-element.18), channel_id=5, replica_groups=mesh['owner'=8,'ctx'=32] {'ctx'}, use_global_device_ids=true, to_apply=%region_10.11.clone | all-reduce | flops 8192 | bytes 65536
  736.3 0.1 constant_dynamic-slice_fusion
  736.4 14.4 %reduce-scatter.6.cloned.1.call-done = f32[8,4096]{1,0:T(8,128)} async-done(((f32[256,4096]{1,0:T(8,128)}), f32[8,4096]{1,0:T(8,128)}) %reduce-scatter.6.cloned.1.call-update) | async-done | bytes 131088 | tf_op jit(solution)/shard_map/reduce_scatter | solution.py:97
  750.7 1.6 fusion.11
  752.4 0.0 copy-done.1
  (17 shorter events, 0.1 us)
Async XLA Ops:
  7.2 2.5 copy-start
  21.9 12.3 %copy-start.3 = (bf16[256,1024]{1,0:T(8,128)(2,1)S(1)}, bf16[256,1024]{1,0:T(8,128)(2,1)}, u32[]{:S(2)}) copy-start(bf16[256,1024]{1,0:T(8,128)(2,1)} %param.13) | copy-start | bytes 1572868
  22.0 12.3 %copy-start.4 = (bf16[1,256,256]{2,1,0:T(8,128)(2,1)S(1)}, bf16[1,256,256]{2,1,0:T(8,128)(2,1)}, u32[]{:S(2)}) copy-start(bf16[1,256,256]{2,1,0:T(8,128)(2,1)} %param.12) | copy-start | bytes 393220
  22.0 13.5 %copy-start.7 = (s32[8]{0:T(128)S(1)}, s32[8]{0:T(128)}, u32[]{:S(2)}) copy-start(s32[8]{0:T(128)} %param.10) | copy-start | bytes 100
  22.0 14.1 %copy-start.5 = (s32[1,256,8]{1,2,0:T(8,128)S(1)}, s32[1,256,8]{1,2,0:T(8,128)}, u32[]{:S(2)}) copy-start(s32[1,256,8]{1,2,0:T(8,128)} %param.15) | copy-start | bytes 24580
  22.0 14.2 %copy-start.6 = (s32[1,256]{1,0:T(1,128)S(1)}, s32[1,256]{1,0:T(1,128)}, u32[]{:S(2)}) copy-start(s32[1,256]{1,0:T(1,128)} %param.11) | copy-start | bytes 3076
  22.0 245.9 %all-to-all-start = ((bf16[8,4,128,1024]{3,2,1,0:T(8,128)(2,1)}), bf16[8,4,128,1024]{3,2,1,0:T(8,128)(2,1)}, u32[]{:S(2)}, u32[]{:S(2)}) async-start(bf16[8,4,128,1024]{3,2,1,0:T(8,128)(2,1)} %select_select_fusion), calls=%async_computation.1 | async-start | bytes 16777216 | tf_op jit(solution)/shard_map/all_to_all | solution.py:37
  33.5 230.2 %all-gather.3.cloned.1.call-start = ((), (), s32[]{:S(2)}) async-start(), calls=%async_computation.5 | async-start | bytes 2162688 | tf_op jit(solution)/shard_map/all_gather | solution.py:74
  34.2 373.8 %reduce-scatter.4.cloned.1.call-start = ((), (), s32[]{:S(2)}) async-start(), calls=%async_computation.3 | async-start | bytes 540672 | tf_op jit(solution)/shard_map/reduce_scatter | solution.py:53
  35.4 715.3 %reduce-scatter.6.cloned.1.call-start = ((), (), s32[]{:S(2)}) async-start(), calls=%async_computation.4 | async-start | bytes 4325376 | tf_op jit(solution)/shard_map/reduce_scatter | solution.py:97
  410.4 1.3 copy-start.2
  591.5 5.8 copy-start.8
  591.5 160.9 %copy-start.1 = (bf16[8,128,1024]{2,1,0:T(8,128)(2,1)S(1)}, bf16[8,128,1024]{2,1,0:T(8,128)(2,1)}, u32[]{:S(2)}) copy-start(bf16[8,128,1024]{2,1,0:T(8,128)(2,1)} %param.8) | copy-start | bytes 6291460
Sparse Core Ops, SparseCore 0:
  36.2 227.5 all-gather.2
  266.3 141.7 reduce-scatter.3
  597.4 153.3 reduce-scatter.5

commit v2 on v1

--- a/solution.py
+++ b/solution.py
@@ -13,6 +13,52 @@
 CAP = 4
 CTX_DEV = 1024
 
+
+def exchange(shard, bit):
+    peers = lax.axis_size("ctx")
+    return lax.ppermute(shard, "ctx", [(i, i ^ bit) for i in range(peers)])
+
+
+def gather_rows(block, my_ctx):
+    peers = lax.axis_size("ctx")
+    held = block
+    bit = 1
+    while bit < peers:
+        other = exchange(held, bit)
+        upper = (my_ctx // bit) % 2 == 1
+        held = jnp.where(
+            upper, jnp.concatenate([other, held]), jnp.concatenate([held, other])
+        )
+        bit *= 2
+    return held
+
+
+def scatter_rows(parts, my_ctx, merge):
+    peers = lax.axis_size("ctx")
+    held = parts
+    bit = 1
+    while bit < peers:
+        half = jax.tree.map(lambda a: a.reshape((a.shape[0] // 2, 2) + a.shape[1:]), held)
+        upper = (my_ctx // bit) % 2 == 1
+        keep = jax.tree.map(lambda a: jnp.where(upper, a[:, 1], a[:, 0]), half)
+        send = jax.tree.map(lambda a: jnp.where(upper, a[:, 0], a[:, 1]), half)
+        held = merge(keep, exchange(send, bit))
+        bit *= 2
+    return jax.tree.map(lambda a: a[0], held)
+
+
+def add_parts(a, b):
+    return a + b
+
+
+def merge_softmax(a, b):
+    numerator_a, running_a, totals_a = a
+    numerator_b, running_b, totals_b = b
+    newest = jnp.maximum(running_a, running_b)
+    factor_a = jnp.exp(running_a - newest)
+    factor_b = jnp.exp(running_b - newest)
+    numerator = numerator_a * factor_a[..., None] + numerator_b * factor_b[..., None]
+    return (numerator, newest, totals_a * factor_a + totals_b * factor_b)
 
 def on_device(span_cache, retrieval, counts, recompute_pos, hidden, kv_weight, queries, block_mask):
     owner_count = lax.axis_size("owner")
@@ -50,12 +96,10 @@
     blocks = jnp.where(my_in_use[:, None, None], blocks, jnp.zeros((), jnp.bfloat16))
     context = blocks.reshape(CTX_DEV, feature_count)
     local_rows = hidden[0]
-    recomputed = lax.psum_scatter(
-        jnp.dot(local_rows, kv_weight, preferred_element_type=jnp.float32).astype(jnp.bfloat16),
-        "ctx",
-        scatter_dimension=0,
-        tiled=True,
-    )
+    partial = jnp.dot(local_rows, kv_weight, preferred_element_type=jnp.float32)
+    recomputed = scatter_rows(
+        partial.reshape(cycle_size, RCP, feature_count), my_ctx, add_parts
+    ).astype(jnp.bfloat16)
     every_pos = recompute_pos[0]
     own_pos = lax.dynamic_slice_in_dim(every_pos, my_ctx * RCP, RCP)
     matches = jnp.arange(CTX_DEV, dtype=jnp.int32)[:, None] == own_pos[None, :]
@@ -71,7 +115,7 @@
     mask_cols = block_mask[0]
     query_count = cycle_size * RCP
     query_pos = jnp.arange(query_count, dtype=jnp.int32) // RCP * CTX_DEV + every_pos
-    all_queries = lax.all_gather(queries[0], "ctx", axis=0, tiled=True)
+    all_queries = gather_rows(queries[0], my_ctx)
     per_group = QH // KVH
     allowed = jnp.take(mask_cols, query_pos // BLK, axis=0)
     visible = jnp.repeat(allowed, BLK, axis=1) > 0
@@ -90,13 +134,19 @@
         value_rows,
         preferred_element_type=jnp.float32,
     )
-    global_max = lax.pmax(local_max, "ctx")
-    factor = jnp.exp(local_max - global_max)
-    numerator = weighted * jnp.transpose(factor, (2, 0, 1))[..., None]
-    totals = jnp.transpose(local_sum * factor, (2, 0, 1)).reshape(query_count, QH)
-    reduced = lax.psum_scatter(numerator.reshape(query_count, QH * HD), "ctx", scatter_dimension=0, tiled=True)
-    reduced_totals = lax.psum_scatter(totals, "ctx", scatter_dimension=0, tiled=True)
-    result = reduced.reshape(RCP, QH, HD) / reduced_totals[:, :, None]
+    running = jnp.transpose(local_max, (2, 0, 1)).reshape(query_count, QH)
+    totals = jnp.transpose(local_sum, (2, 0, 1)).reshape(query_count, QH)
+    numerator = weighted.reshape(query_count, QH, HD)
+    numerator, running, totals = scatter_rows(
+        (
+            numerator.reshape(cycle_size, RCP, QH, HD),
+            running.reshape(cycle_size, RCP, QH),
+            totals.reshape(cycle_size, RCP, QH),
+        ),
+        my_ctx,
+        merge_softmax,
+    )
+    result = numerator / totals[:, :, None]
     attended = result.reshape(RCP, QH * HD).astype(jnp.bfloat16)
     return (context[None], attended[None])
 

time: 758 us -> 421 us (0.56)
  blocking collectives: 267 us -> 0 us
  waiting for transfers between devices: 368 us -> 273 us
  starting transfers between devices: 11.6 us -> 42.9 us
  between operations: 14.6 us -> 1.38 us
  other arithmetic: 30.4 us -> 40.9 us
    ppermute x0 -> x25, waiting for transfers between devices: none -> 273 us  [exchange(): return lax.ppermute(shard, 'ctx', [(i, i ^ bit) for i in range(peers)])]
    all_gather x1 -> x0, waiting for transfers between devices: 222 us -> none  [on_device(): all_queries = lax.all_gather(queries[0], 'ctx', axis=0, tiled=True)]
    reduce_scatter x2 -> x0, waiting for transfers between devices: 145 us -> none  [the longest x1 131 us: on_device(): lax.psum_scatter(jnp.dot(local_rows, kv_weight, preferred_element_type=jn...]
    unnamed x1 -> x0, blocking collectives: 134 us -> none
    pmax x1 -> x0, blocking collectives: 133 us -> none  [on_device(): global_max = lax.pmax(local_max, 'ctx')]
    ppermute x0 -> x25, starting transfers between devices: none -> 31.5 us  [exchange(): return lax.ppermute(shard, 'ctx', [(i, i ^ bit) for i in range(peers)])]
  transfers between devices with their start and end apart: 4 -> 26, of which waited for: 3 -> 14; matrix products, arithmetic and copies ran while one was open for 3% -> 6% of each run, Pallas kernels for 0% -> 0%
where the time goes in v2:
time: 421 us; the launch traced here: 420 us
  waiting for transfers between devices  273 us (65%)
  starting transfers between devices  42.9 us (10%)
  other arithmetic  40.9 us (10%)
  matrix products  32.5 us (8%)
  local copies, waits for them, and re-layouts  28.6 us (7%)
    ppermute x25, waiting for transfers between devices, exchange(): return lax.ppermute(shard, 'ctx', [(i, i ^ bit) for i in range(peers)])  273 us
    ppermute x25, starting transfers between devices, exchange(): return lax.ppermute(shard, 'ctx', [(i, i ^ bit) for i in range(peers)])  31.5 us
    dot_general x1, matrix products, on_device(): jnp.einsum('kgrt,tkd->rkgd', weights.astype(jnp.bfloat16), value_rows, pr...  16 us
    reduce_sum x1, other arithmetic, on_device(): local_sum = jnp.sum(weights, axis=3)  15 us
    dot_general x1, matrix products, on_device(): jnp.einsum('rkgd,tkd->kgrt', grouped, key_rows, preferred_element_type=jn...  13.7 us
    all_to_all x1, starting transfers between devices, on_device(): lax.all_to_all(outgoing, 'owner', split_axis=0, concat_axis=0, tiled=True)  11.4 us
  transfers between devices with their start and end apart: 26, of which 14 were waited for; matrix products, arithmetic and copies ran while one was open for 6% of the time, Pallas kernels for 0%

profile of v2, /device:TPU:6, one launch (start us, length us, event | category | flops | bytes accessed | tf_op | source)
XLA Modules:
  0.0 419.6 jit_solution(9981034902326178602)
XLA Ops:
  0.7 0.9 fusion.88
  1.7 0.7 add_select_fusion.1
  3.1 4.9 %gather_fusion = bf16[32,128,1024]{2,1,0:T(8,128)(2,1)} fusion(bf16[8,128,1024]{2,1,0:T(8,128)(2,1)S(1)} %copy-done, s32[1024]{0:T(1024)S(1)} %pad_clamp_fusion.2), kind=kCustom, calls=%fused_computation | custom fusion | bytes 16777344 | tf_op jit(solution)/shard_map/jit(_take)/gather | solution.py:81
  8.0 7.6 %select_select_fusion = bf16[8,4,128,1024]{3,2,1,0:T(8,128)(2,1)} fusion(bf16[8,4,128,1024]{3,2,1,0:T(8,128)(2,1)} %bitcast.468, pred[8,4]{1,0:T(8,128)(4,1)S(1)} %copy.307, pred[8,4]{1,0:T(8,128)(4,1)S(1)} %copy.306), kind=kLoop, calls=%fused_computation.10 | loop fusion | flops 8388608 | bytes 16777280 | tf_op jit(solution)/shard_map/jit(_where)/select_n | solution.py:80
  15.7 11.4 %all-to-all-start = ((bf16[8,4,128,1024]{3,2,1,0:T(8,128)(2,1)}), bf16[8,4,128,1024]{3,2,1,0:T(8,128)(2,1)}, u32[]{:S(2)}, u32[]{:S(2)}) async-start(bf16[8,4,128,1024]{3,2,1,0:T(8,128)(2,1)} %select_select_fusion), calls=%async_computation | async-start | bytes 16777216 | tf_op jit(solution)/shard_map/all_to_all | solution.py:83
  27.1 0.3 fusion.26
  27.5 0.6 collective-permute-start
  28.1 0.6 dynamic_slice.12
  28.9 0.7 gather_fusion.2
  29.6 0.7 and_select_fusion.5
  30.4 0.7 fusion.78
  31.1 0.7 broadcast_compare_fusion
  32.1 0.7 fusion.77
  32.9 1.1 collective-permute-start.6
  34.0 0.7 fusion.64
  34.8 0.3 fusion.20
  35.2 178.7 %collective-permute-done.6 = bf16[16,4096]{1,0:T(8,128)(2,1)S(1)} collective-permute-done((bf16[16,4096]{1,0:T(8,128)(2,1)S(1)}, bf16[16,4096]{1,0:T(8,128)(2,1)S(1)}, u32[]{:S(2)}, u32[]{:S(2)}) %collective-permute-start.6) | collective-permute-done | bytes 131104 | tf_op jit(solution)/shard_map/ppermute | solution.py:19
  214.0 0.5 collective-permute-start.7
  214.7 2.6 collective-permute-start.1
  217.2 10.7 %collective-permute-done.7 = bf16[32,4096]{1,0:T(8,128)(2,1)S(1)} collective-permute-done((bf16[32,4096]{1,0:T(8,128)(2,1)S(1)}, bf16[32,4096]{1,0:T(8,128)(2,1)S(1)}, u32[]{:S(2)}, u32[]{:S(2)}) %collective-permute-start.7) | collective-permute-done | bytes 262176 | tf_op jit(solution)/shard_map/ppermute | solution.py:19
  228.0 1.3 collective-permute-start.8
  229.7 12.2 %collective-permute-done.8 = bf16[64,4096]{1,0:T(8,128)(2,1)S(1)} collective-permute-done((bf16[64,4096]{1,0:T(8,128)(2,1)S(1)}, bf16[64,4096]{1,0:T(8,128)(2,1)S(1)}, u32[]{:S(2)}, u32[]{:S(2)}) %collective-permute-start.8) | collective-permute-done | bytes 524320 | tf_op jit(solution)/shard_map/ppermute | solution.py:19
  242.1 2.5 collective-permute-start.9
  244.6 1.2 collective-permute-start.3
  246.0 23.2 %collective-permute-done.3 = f32[2,8,1024]{2,1,0:T(8,128)S(1)} collective-permute-done((f32[2,8,1024]{2,1,0:T(8,128)S(1)}, f32[2,8,1024]{2,1,0:T(8,128)S(1)}, u32[]{:S(2)}, u32[]{:S(2)}) %collective-permute-start.3) | collective-permute-done | bytes 65568 | tf_op jit(solution)/shard_map/ppermute | solution.py:19
  269.3 1.7 collective-permute-start.4
  271.3 0.4 maximum_select_fusion.3
  272.0 1.4 copy.320
  273.4 4.1 gather_fusion.1
  277.4 2.6 copy.369
  280.0 2.4 select_select_fusion.1
  282.6 13.7 %fusion = (f32[4,8,256]{2,1,0:T(8,128)S(1)}, f32[4,1024,256,8]{2,1,3,0:T(8,128)}) fusion(pred[256,1024]{0,1:T(8,128)(4,1)S(1)} %fusion.20, bf16[1024,4,128,1]{0,2,3,1:T(8,128)(2,1)S(1)} %bitcast.496, bf16[128,4,8,128]{3,0,2,1:T(8,128)(2,1)S(1)} %maximum_select_fusion.3, bf16[128,4,8,128]{3,0,2,1:T(8,128)(2,1)S(1)} %copy-done.3, pred[]{:T(512)S(6)} %eq.96), kind=kOutput, calls=%fused_computation.5 | convolution fusion | flops 2182078464 | bytes 36995072 | tf_op jit(solution)/shard_map/rkgd,tkd->kgrt/dot_general | solution.py:124
  296.4 15.0 %fusion.1 = f32[4,8,256]{2,1,0:T(8,128)S(1)} fusion(f32[4,1024,256,8]{2,1,3,0:T(8,128)} %get-tuple-element.48, f32[4,8,256]{2,1,0:T(8,128)S(1)} %get-tuple-element.47, pred[256,1024]{0,1:T(8,128)(4,1)S(1)} %fusion.20), kind=kLoop, calls=%fused_computation.6 | loop fusion | flops 41934848 | bytes 33882112 | tf_op jit(solution)/shard_map/reduce_sum | solution.py:130
  311.4 16.0 %fusion.6 = f32[256,4,8,128]{0,3,2,1:T(8,128)} fusion(bf16[1024,4,128,1]{0,2,3,1:T(8,128)(2,1)S(1)} %bitcast.495, f32[4,1024,256,8]{2,1,3,0:T(8,128)} %get-tuple-element.48, f32[4,8,256]{2,1,0:T(8,128)S(1)} %get-tuple-element.47, pred[256,1024]{0,1:T(8,128)(4,1)S(1)} %fusion.20), kind=kOutput, calls=%fused_computation.11 | convolution fusion | flops 2189426688 | bytes 39092224 | tf_op jit(solution)/shard_map/kgrt,tkd->rkgd/dot_general | solution.py:131
  327.4 5.5 %copy.324 = f32[256,4,8,128]{3,2,1,0:T(8,128)} copy(f32[256,4,8,128]{0,3,2,1:T(8,128)} %fusion.6) | data formatting | bytes 8388608 | tf_op jit(solution)/shard_map/kgrt,tkd->rkgd/transpose | solution.py:131
  332.9 0.8 reshape_reshape_reshape.11
  333.7 4.1 select_bitcast_fusion
  337.8 0.4 fusion.90
  338.3 0.6 collective-permute-start.20
  338.8 0.8 reshape_reshape_reshape.10
  339.7 0.5 broadcast_select_fusion
  340.2 2.3 collective-permute-done.20
  342.5 0.4 collective-permute-done.10
  344.0 2.1 collective-permute-start.12
  346.4 1.1 collective-permute-done.21
  347.5 0.5 collective-permute-done.12
  348.0 3.5 fusion.17
  351.5 0.3 select_bitcast_fusion.1
  351.8 2.1 collective-permute-start.13
  353.9 1.4 collective-permute-start.14
  355.3 1.6 collective-permute-start.22
  356.9 18.8 %collective-permute-done.14 = f32[4,8,32]{2,1,0:T(8,128)S(1)} collective-permute-done((f32[4,8,32]{2,1,0:T(8,128)S(1)}, f32[4,8,32]{2,1,0:T(8,128)S(1)}, u32[]{:S(2)}, u32[]{:S(2)}) %collective-permute-start.14) | collective-permute-done | bytes 4128 | tf_op jit(solution)/shard_map/ppermute | solution.py:19
  376.0 2.0 collective-permute-start.23
  378.0 0.7 fusion.19
  378.8 3.5 collective-permute-start.15
  382.3 20.3 %collective-permute-done.15 = f32[4,8,32,128]{3,2,1,0:T(8,128)S(1)} collective-permute-done((f32[4,8,32,128]{3,2,1,0:T(8,128)S(1)}, f32[4,8,32,128]{3,2,1,0:T(8,128)S(1)}, u32[]{:S(2)}, u32[]{:S(2)}) %collective-permute-start.15) | collective-permute-done | bytes 524320 | tf_op jit(solution)/shard_map/ppermute | solution.py:19
  402.6 0.3 fusion.23
  403.0 0.5 collective-permute-start.17
  403.4 3.3 collective-permute-start.24
  407.0 3.9 copy.364
  411.1 0.7 collective-permute-done.18
  412.2 2.4 collective-permute-start.19
  414.6 4.1 collective-permute-done.19
  418.9 0.7 fusion.38
  (120 shorter events, 6.5 us)
Async XLA Ops:
  0.6 2.5 copy-start
  15.6 11.5 %copy-start.6 = (bf16[1,8,4096]{2,1,0:T(8,128)(2,1)S(1)}, bf16[1,8,4096]{2,1,0:T(8,128)(2,1)}, u32[]{:S(2)}) copy-start(bf16[1,8,4096]{2,1,0:T(8,128)(2,1)} %param.14) | copy-start | bytes 196612
  15.7 11.5 %copy-start.4 = (bf16[256,1024]{1,0:T(8,128)(2,1)S(1)}, bf16[256,1024]{1,0:T(8,128)(2,1)}, u32[]{:S(2)}) copy-start(bf16[256,1024]{1,0:T(8,128)(2,1)} %param.13) | copy-start | bytes 1572868
  15.7 11.5 %copy-start.5 = (bf16[1,256,256]{2,1,0:T(8,128)(2,1)S(1)}, bf16[1,256,256]{2,1,0:T(8,128)(2,1)}, u32[]{:S(2)}) copy-start(bf16[1,256,256]{2,1,0:T(8,128)(2,1)} %param.12) | copy-start | bytes 393220
  15.7 12.4 %copy-start.9 = (s32[8]{0:T(128)S(1)}, s32[8]{0:T(128)}, u32[]{:S(2)}) copy-start(s32[8]{0:T(128)} %param.10) | copy-start | bytes 100
  15.7 13.0 %copy-start.7 = (s32[1,256,8]{1,2,0:T(8,128)S(1)}, s32[1,256,8]{1,2,0:T(8,128)}, u32[]{:S(2)}) copy-start(s32[1,256,8]{1,2,0:T(8,128)} %param.15) | copy-start | bytes 24580
  15.7 13.1 %copy-start.8 = (s32[1,256]{1,0:T(1,128)S(1)}, s32[1,256]{1,0:T(1,128)}, u32[]{:S(2)}) copy-start(s32[1,256]{1,0:T(1,128)} %param.11) | copy-start | bytes 3076
  15.7 257.7 %all-to-all-start = ((bf16[8,4,128,1024]{3,2,1,0:T(8,128)(2,1)}), bf16[8,4,128,1024]{3,2,1,0:T(8,128)(2,1)}, u32[]{:S(2)}, u32[]{:S(2)}) async-start(bf16[8,4,128,1024]{3,2,1,0:T(8,128)(2,1)} %select_select_fusion), calls=%async_computation | async-start | bytes 16777216 | tf_op jit(solution)/shard_map/all_to_all | solution.py:83
  27.1 5.8 %collective-permute-start.5 = (bf16[8,4096]{1,0:T(8,128)(2,1)S(1)}, bf16[8,4096]{1,0:T(8,128)(2,1)S(1)}, u32[]{:S(2)}, u32[]{:S(2)}) collective-permute-start(bf16[8,4096]{1,0:T(8,128)(2,1)S(1)} %bitcast.516), channel_id=1, source_target_pairs={{0,1},{1,0},{2,3},{3,2},{4,5},{5,4},{6,7},{7,6},{8,9},{9,8},{10,11... | collective-permute-start | bytes 196616 | tf_op jit(solution)/shard_map/ppermute | solution.py:19
  27.5 187.0 %collective-permute-start = (f32[16,8,1024]{2,1,0:T(8,128)S(1)}, f32[16,8,1024]{2,1,0:T(8,128)S(1)}, u32[]{:S(2)}, u32[]{:S(2)}) collective-permute-start(f32[16,8,1024]{2,1,0:T(8,128)S(1)} %select_bitcast_fusion.3), channel_id=1, source_target_pairs={{0,1},{1,0},{2,3},{3,2},{4,5},{5,4},{6,7},{7,6},{8,9},{9,8},{10,11... | collective-permute-start | bytes 1572872 | tf_op jit(solution)/shard_map/ppermute | solution.py:19
  32.9 181.0 %collective-permute-start.6 = (bf16[16,4096]{1,0:T(8,128)(2,1)S(1)}, bf16[16,4096]{1,0:T(8,128)(2,1)S(1)}, u32[]{:S(2)}, u32[]{:S(2)}) collective-permute-start(bf16[16,4096]{1,0:T(8,128)(2,1)S(1)} %maximum_select_fusion.8), channel_id=1, source_target_pairs={{0,2},{1,3},{2,0},{3,1},{4,6},{5,7},{6,4},{7,5},{8,10},{9,11},{10,... | collective-permute-start | bytes 393224 | tf_op jit(solution)/shard_map/ppermute | solution.py:19
  214.0 13.9 %collective-permute-start.7 = (bf16[32,4096]{1,0:T(8,128)(2,1)S(1)}, bf16[32,4096]{1,0:T(8,128)(2,1)S(1)}, u32[]{:S(2)}, u32[]{:S(2)}) collective-permute-start(bf16[32,4096]{1,0:T(8,128)(2,1)S(1)} %maximum_select_fusion.6), channel_id=1, source_target_pairs={{0,4},{1,5},{2,6},{3,7},{4,0},{5,1},{6,2},{7,3},{8,12},{9,13},{10,... | collective-permute-start | bytes 786440 | tf_op jit(solution)/shard_map/ppermute | solution.py:19
  214.7 14.9 %collective-permute-start.1 = (f32[8,8,1024]{2,1,0:T(8,128)S(1)}, f32[8,8,1024]{2,1,0:T(8,128)S(1)}, u32[]{:S(2)}, u32[]{:S(2)}) collective-permute-start(f32[8,8,1024]{2,1,0:T(8,128)S(1)} %select_bitcast_fusion.6), channel_id=1, source_target_pairs={{0,2},{1,3},{2,0},{3,1},{4,6},{5,7},{6,4},{7,5},{8,10},{9,11},{10,... | collective-permute-start | bytes 786440 | tf_op jit(solution)/shard_map/ppermute | solution.py:19
  228.0 13.9 %collective-permute-start.8 = (bf16[64,4096]{1,0:T(8,128)(2,1)S(1)}, bf16[64,4096]{1,0:T(8,128)(2,1)S(1)}, u32[]{:S(2)}, u32[]{:S(2)}) collective-permute-start(bf16[64,4096]{1,0:T(8,128)(2,1)S(1)} %maximum_select_fusion.4), channel_id=1, source_target_pairs={{0,8},{1,9},{2,10},{3,11},{4,12},{5,13},{6,14},{7,15},{8,0},{9,1},... | collective-permute-start | bytes 1572872 | tf_op jit(solution)/shard_map/ppermute | solution.py:19
  229.6 14.9 %collective-permute-start.2 = (f32[4,8,1024]{2,1,0:T(8,128)S(1)}, f32[4,8,1024]{2,1,0:T(8,128)S(1)}, u32[]{:S(2)}, u32[]{:S(2)}) collective-permute-start(f32[4,8,1024]{2,1,0:T(8,128)S(1)} %select_bitcast_fusion.8), channel_id=1, source_target_pairs={{0,4},{1,5},{2,6},{3,7},{4,0},{5,1},{6,2},{7,3},{8,12},{9,13},{10,... | collective-permute-start | bytes 393224 | tf_op jit(solution)/shard_map/ppermute | solution.py:19
  242.1 29.6 %collective-permute-start.9 = (bf16[128,4096]{1,0:T(8,128)(2,1)S(1)}, bf16[128,4096]{1,0:T(8,128)(2,1)S(1)}, u32[]{:S(2)}, u32[]{:S(2)}) collective-permute-start(bf16[128,4096]{1,0:T(8,128)(2,1)S(1)} %maximum_select_fusion.2), channel_id=1, source_target_pairs={{0,16},{1,17},{2,18},{3,19},{4,20},{5,21},{6,22},{7,23},{8,24},{9,... | collective-permute-start | bytes 3145736 | tf_op jit(solution)/shard_map/ppermute | solution.py:19
  244.6 24.6 %collective-permute-start.3 = (f32[2,8,1024]{2,1,0:T(8,128)S(1)}, f32[2,8,1024]{2,1,0:T(8,128)S(1)}, u32[]{:S(2)}, u32[]{:S(2)}) collective-permute-start(f32[2,8,1024]{2,1,0:T(8,128)S(1)} %select_bitcast_fusion.9), channel_id=1, source_target_pairs={{0,8},{1,9},{2,10},{3,11},{4,12},{5,13},{6,14},{7,15},{8,0},{9,1},... | collective-permute-start | bytes 196616 | tf_op jit(solution)/shard_map/ppermute | solution.py:19
  269.3 10.7 %collective-permute-start.4 = (f32[1,8,1024]{2,1,0:T(8,128)S(1)}, f32[1,8,1024]{2,1,0:T(8,128)S(1)}, u32[]{:S(2)}, u32[]{:S(2)}) collective-permute-start(f32[1,8,1024]{2,1,0:T(8,128)S(1)} %select_bitcast_fusion.12), channel_id=1, source_target_pairs={{0,16},{1,17},{2,18},{3,19},{4,20},{5,21},{6,22},{7,23},{8,24},{9,... | collective-permute-start | bytes 98312 | tf_op jit(solution)/shard_map/ppermute | solution.py:19
  280.0 2.6 copy-start.3
  282.4 13.9 %copy-start.2 = (bf16[1024,1024]{0,1:T(8,128)(2,1)}, bf16[1024,1024]{0,1:T(8,128)(2,1)S(1)}, u32[]{:S(2)}) copy-start(bf16[1024,1024]{0,1:T(8,128)(2,1)S(1)} %select_select_fusion.1) | copy-start | bytes 6291460
  337.8 10.2 %collective-permute-start.11 = (f32[16,8,32,128]{3,2,1,0:T(8,128)}, f32[16,8,32,128]{3,2,1,0:T(8,128)}, u32[]{:S(2)}, u32[]{:S(2)}) collective-permute-start(f32[16,8,32,128]{3,2,1,0:T(8,128)} %select_bitcast_fusion), channel_id=1, source_target_pairs={{0,1},{1,0},{2,3},{3,2},{4,5},{5,4},{6,7},{7,6},{8,9},{9,8},{10,11... | collective-permute-start | bytes 6291464 | tf_op jit(solution)/shard_map/ppermute | solution.py:19
  338.3 4.3 %collective-permute-start.20 = (f32[16,8,32]{1,0,2:T(8,128)S(1)}, f32[16,8,32]{1,0,2:T(8,128)S(1)}, u32[]{:S(2)}, u32[]{:S(2)}) collective-permute-start(f32[16,8,32]{1,0,2:T(8,128)S(1)} %select_bitcast_fusion.4), channel_id=1, source_target_pairs={{0,1},{1,0},{2,3},{3,2},{4,5},{5,4},{6,7},{7,6},{8,9},{9,8},{10,11... | collective-permute-start | bytes 49160 | tf_op jit(solution)/shard_map/ppermute | solution.py:19
  340.1 2.8 collective-permute-start.10
  343.5 4.0 collective-permute-start.21
  344.0 4.0 collective-permute-start.12
  351.8 26.2 %collective-permute-start.13 = (f32[8,8,32,128]{3,2,1,0:T(8,128)S(1)}, f32[8,8,32,128]{3,2,1,0:T(8,128)S(1)}, u32[]{:S(2)}, u32[]{:S(2)}) collective-permute-start(f32[8,8,32,128]{3,2,1,0:T(8,128)S(1)} %select_bitcast_fusion.1), channel_id=1, source_target_pairs={{0,2},{1,3},{2,0},{3,1},{4,6},{5,7},{6,4},{7,5},{8,10},{9,11},{10,... | collective-permute-start | bytes 3145736 | tf_op jit(solution)/shard_map/ppermute | solution.py:19
  353.9 21.8 %collective-permute-start.14 = (f32[4,8,32]{2,1,0:T(8,128)S(1)}, f32[4,8,32]{2,1,0:T(8,128)S(1)}, u32[]{:S(2)}, u32[]{:S(2)}) collective-permute-start(f32[4,8,32]{2,1,0:T(8,128)S(1)} %select_bitcast_fusion.14), channel_id=1, source_target_pairs={{0,4},{1,5},{2,6},{3,7},{4,0},{5,1},{6,2},{7,3},{8,12},{9,13},{10,... | collective-permute-start | bytes 12296 | tf_op jit(solution)/shard_map/ppermute | solution.py:19
  355.3 20.6 %collective-permute-start.22 = (f32[4,8,32]{2,1,0:T(8,128)S(1)}, f32[4,8,32]{2,1,0:T(8,128)S(1)}, u32[]{:S(2)}, u32[]{:S(2)}) collective-permute-start(f32[4,8,32]{2,1,0:T(8,128)S(1)} %select_bitcast_fusion.13), channel_id=1, source_target_pairs={{0,4},{1,5},{2,6},{3,7},{4,0},{5,1},{6,2},{7,3},{8,12},{9,13},{10,... | collective-permute-start | bytes 12296 | tf_op jit(solution)/shard_map/ppermute | solution.py:19
  375.9 6.4 %collective-permute-start.16 = (f32[2,8,32]{2,1,0:T(8,128)S(1)}, f32[2,8,32]{2,1,0:T(8,128)S(1)}, u32[]{:S(2)}, u32[]{:S(2)}) collective-permute-start(f32[2,8,32]{2,1,0:T(8,128)S(1)} %select_bitcast_fusion.16), channel_id=1, source_target_pairs={{0,8},{1,9},{2,10},{3,11},{4,12},{5,13},{6,14},{7,15},{8,0},{9,1},... | collective-permute-start | bytes 6152 | tf_op jit(solution)/shard_map/ppermute | solution.py:19
  376.0 6.3 %collective-permute-start.23 = (f32[2,8,32]{2,1,0:T(8,128)S(1)}, f32[2,8,32]{2,1,0:T(8,128)S(1)}, u32[]{:S(2)}, u32[]{:S(2)}) collective-permute-start(f32[2,8,32]{2,1,0:T(8,128)S(1)} %select_bitcast_fusion.15), channel_id=1, source_target_pairs={{0,8},{1,9},{2,10},{3,11},{4,12},{5,13},{6,14},{7,15},{8,0},{9,1},... | collective-permute-start | bytes 6152 | tf_op jit(solution)/shard_map/ppermute | solution.py:19
  378.8 23.8 %collective-permute-start.15 = (f32[4,8,32,128]{3,2,1,0:T(8,128)S(1)}, f32[4,8,32,128]{3,2,1,0:T(8,128)S(1)}, u32[]{:S(2)}, u32[]{:S(2)}) collective-permute-start(f32[4,8,32,128]{3,2,1,0:T(8,128)S(1)} %select_bitcast_fusion.2), channel_id=1, source_target_pairs={{0,4},{1,5},{2,6},{3,7},{4,0},{5,1},{6,2},{7,3},{8,12},{9,13},{10,... | collective-permute-start | bytes 1572872 | tf_op jit(solution)/shard_map/ppermute | solution.py:19
  402.6 17.1 %copy-start.1 = (bf16[8,128,1024]{2,1,0:T(8,128)(2,1)S(1)}, bf16[8,128,1024]{2,1,0:T(8,128)(2,1)}, u32[]{:S(2)}) copy-start(bf16[8,128,1024]{2,1,0:T(8,128)(2,1)} %param.8) | copy-start | bytes 6291460
  403.0 9.0 %collective-permute-start.17 = (f32[2,8,32,128]{3,2,1,0:T(8,128)S(1)}, f32[2,8,32,128]{3,2,1,0:T(8,128)S(1)}, u32[]{:S(2)}, u32[]{:S(2)}) collective-permute-start(f32[2,8,32,128]{3,2,1,0:T(8,128)S(1)} %select_bitcast_fusion.5), channel_id=1, source_target_pairs={{0,8},{1,9},{2,10},{3,11},{4,12},{5,13},{6,14},{7,15},{8,0},{9,1},... | collective-permute-start | bytes 786440 | tf_op jit(solution)/shard_map/ppermute | solution.py:19
  403.4 7.7 %collective-permute-start.24 = (f32[1,8,32]{2,1,0:T(8,128)S(1)}, f32[1,8,32]{2,1,0:T(8,128)S(1)}, u32[]{:S(2)}, u32[]{:S(2)}) collective-permute-start(f32[1,8,32]{2,1,0:T(8,128)S(1)} %select_bitcast_fusion.17), channel_id=1, source_target_pairs={{0,16},{1,17},{2,18},{3,19},{4,20},{5,21},{6,22},{7,23},{8,24},{9,... | collective-permute-start | bytes 3080 | tf_op jit(solution)/shard_map/ppermute | solution.py:19
  406.7 5.1 %collective-permute-start.18 = (f32[1,8,32]{2,1,0:T(8,128)S(1)}, f32[1,8,32]{2,1,0:T(8,128)S(1)}, u32[]{:S(2)}, u32[]{:S(2)}) collective-permute-start(f32[1,8,32]{2,1,0:T(8,128)S(1)} %select_bitcast_fusion.18), channel_id=1, source_target_pairs={{0,16},{1,17},{2,18},{3,19},{4,20},{5,21},{6,22},{7,23},{8,24},{9,... | collective-permute-start | bytes 3080 | tf_op jit(solution)/shard_map/ppermute | solution.py:19
  412.2 6.6 %collective-permute-start.19 = (f32[1,8,32,128]{3,2,1,0:T(8,128)S(1)}, f32[1,8,32,128]{3,2,1,0:T(8,128)S(1)}, u32[]{:S(2)}, u32[]{:S(2)}) collective-permute-start(f32[1,8,32,128]{3,2,1,0:T(8,128)S(1)} %select_bitcast_fusion.7), channel_id=1, source_target_pairs={{0,16},{1,17},{2,18},{3,19},{4,20},{5,21},{6,22},{7,23},{8,24},{9,... | collective-permute-start | bytes 393224 | tf_op jit(solution)/shard_map/ppermute | solution.py:19

commit v3 on v2

--- a/solution.py
+++ b/solution.py
@@ -77,10 +77,21 @@
     )
     chosen = jnp.sum(jnp.where(picked, (retrieval % SLOTS)[:, None, :], 0), axis=2)
     filled = jnp.any(picked, axis=2)
-    outgoing = jnp.where(
-        filled[:, :, None, None], jnp.take(span_cache, chosen, axis=0), jnp.zeros((), jnp.bfloat16)
-    )
-    arrived = lax.all_to_all(outgoing, "owner", split_axis=0, concat_axis=0, tiled=True)
+    pieces = []
+    for shift in range(owner_count):
+        target = (my_owner + shift) % owner_count
+        chosen_here = lax.dynamic_index_in_dim(chosen, target, 0, keepdims=False)
+        filled_here = lax.dynamic_index_in_dim(filled, target, 0, keepdims=False)
+        piece = jnp.where(
+            filled_here[:, None, None],
+            jnp.take(span_cache, chosen_here, axis=0),
+            jnp.zeros((), jnp.bfloat16),
+        )
+        if shift:
+            piece = lax.ppermute(
+                piece, "owner", [(i, (i + shift) % owner_count) for i in range(owner_count)]
+            )
+        pieces.append(piece)
     wanted = lax.dynamic_index_in_dim(retrieval, my_owner, 0, keepdims=False)
     my_count = lax.dynamic_index_in_dim(counts, my_owner, 0, keepdims=False)
     my_in_use = block_ids < my_count
@@ -91,8 +102,9 @@
         & (positions[None, :] < positions[:, None])
     )
     ordinal = jnp.sum(earlier.astype(jnp.int32), axis=1)
-    flattened = arrived.reshape(owner_count * CAP, BLK, feature_count)
-    blocks = jnp.take(flattened, source * CAP + ordinal, axis=0, mode="clip")
+    flattened = jnp.concatenate(pieces, axis=0)
+    shift_of_source = (my_owner - source) % owner_count
+    blocks = jnp.take(flattened, shift_of_source * CAP + ordinal, axis=0, mode="clip")
     blocks = jnp.where(my_in_use[:, None, None], blocks, jnp.zeros((), jnp.bfloat16))
     context = blocks.reshape(CTX_DEV, feature_count)
     local_rows = hidden[0]

time: 421 us -> 514 us (1.22); the launches traced: 420 us -> 504 us
  starting transfers between devices: 42.9 us -> 79.4 us
  local copies, waits for them, and re-layouts: 28.6 us -> 51 us
  other arithmetic: 40.9 us -> 59.8 us
  waiting for transfers between devices: 273 us -> 279 us
    ppermute x0 -> x7, waiting for transfers between devices: none -> 78.1 us  [on_device(): lax.ppermute(piece, 'owner', [(i, (i + shift) % owner_count) for i in ran...]
    ppermute x25, waiting for transfers between devices: 273 us -> 201 us  [exchange(): return lax.ppermute(shard, 'ctx', [(i, i ^ bit) for i in range(peers)])]
    ppermute x25, starting transfers between devices: 31.5 us -> 63.6 us  [exchange(): return lax.ppermute(shard, 'ctx', [(i, i ^ bit) for i in range(peers)])]
    ppermute x0 -> x7, starting transfers between devices: none -> 15.8 us  [on_device(): lax.ppermute(piece, 'owner', [(i, (i + shift) % owner_count) for i in ran...]
    unnamed x31 -> x63, local copies, waits for them, and re-layouts: 4.92 us -> 17.9 us
    all_to_all x1 -> x0, starting transfers between devices: 11.4 us -> none  [on_device(): lax.all_to_all(outgoing, 'owner', split_axis=0, concat_axis=0, tiled=True)]
    select_n x2 -> x16, other arithmetic: 7.63 us -> 17 us  [the longest x7 14.5 us: on_device(): jnp.where(filled_here[:, None, None], jnp.take(span_cache, chosen_here, a...]
    gather x3 -> x10, local copies, waits for them, and re-layouts: 11.5 us -> 19.3 us  [the longest x8 12.7 us: on_device(): jnp.take(span_cache, chosen_here, axis=0)]
  transfers between devices with their start and end apart: 26 -> 32, of which waited for: 14 -> 18; matrix products, arithmetic and copies ran while one was open for 6% -> 16% of each run, Pallas kernels for 0% -> 0%
where the time goes in v3:
time: 514 us; the launch traced here: 504 us
  waiting for transfers between devices  279 us (54%)
  starting transfers between devices  79.4 us (15%)
  other arithmetic  59.8 us (12%)
  local copies, waits for them, and re-layouts  51 us (10%)
  matrix products  33.4 us (6%)
    ppermute x25, waiting for transfers between devices, exchange(): return lax.ppermute(shard, 'ctx', [(i, i ^ bit) for i in range(peers)])  201 us
    ppermute x7, waiting for transfers between devices, on_device(): lax.ppermute(piece, 'owner', [(i, (i + shift) % owner_count) for i in ran...  78.1 us
    ppermute x25, starting transfers between devices, exchange(): return lax.ppermute(shard, 'ctx', [(i, i ^ bit) for i in range(peers)])  63.6 us
    unnamed x63, local copies, waits for them, and re-layouts  17.9 us
    dot_general x1, matrix products, on_device(): jnp.einsum('kgrt,tkd->rkgd', weights.astype(jnp.bfloat16), value_rows, pr...  16 us
    ppermute x7, starting transfers between devices, on_device(): lax.ppermute(piece, 'owner', [(i, (i + shift) % owner_count) for i in ran...  15.8 us
    reduce_sum x1, other arithmetic, on_device(): local_sum = jnp.sum(weights, axis=3)  15 us
    select_n x7, other arithmetic, on_device(): jnp.where(filled_here[:, None, None], jnp.take(span_cache, chosen_here, a...  14.5 us
  transfers between devices with their start and end apart: 32, of which 18 were waited for; matrix products, arithmetic and copies ran while one was open for 16% of the time, Pallas kernels for 0%

profile of v3, /device:TPU:6, one launch (start us, length us, event | category | flops | bytes accessed | tf_op | source)
XLA Modules:
  0.0 504.4 jit_solution(11100160201409552460)
XLA Ops:
  0.8 1.5 fusion.27
  6.7 1.6 gather_fusion.3
  8.3 2.4 select_select_fusion.7
  10.6 7.1 %collective-permute-start.5 = (bf16[4,128,1024]{2,1,0:T(8,128)(2,1)}, bf16[4,128,1024]{2,1,0:T(8,128)(2,1)}, u32[]{:S(2)}, u32[]{:S(2)}) collective-permute-start(bf16[4,128,1024]{2,1,0:T(8,128)(2,1)} %select_select_fusion.7), channel_id=1, source_target_pairs={{0,32},{32,64},{64,96},{96,128},{128,160},{160,192},{192,224},{224... | collective-permute-start | bytes 3145736 | tf_op jit(solution)/shard_map/ppermute | solution.py:91
  17.8 1.6 gather_fusion.4
  19.4 2.5 select_select_fusion.6
  21.8 2.4 collective-permute-start.6
  24.3 1.6 gather_fusion.5
  25.9 2.4 select_select_fusion.5
  36.6 1.6 gather_fusion.9
  38.2 1.6 gather_fusion.8
  39.8 1.6 gather_fusion.7
  41.4 1.6 gather_fusion.6
  43.0 2.6 select_select_fusion.1
  45.6 2.4 select_select_fusion.2
  47.9 1.2 select_select_fusion.3
  49.1 1.2 select_select_fusion.4
  50.3 1.3 fusion.66
  51.6 1.6 gather_fusion.2
  54.9 2.6 fusion.20
  57.4 1.1 fusion.26
  58.7 1.1 collective-permute-start.1
  59.8 1.1 collective-permute-start.13
  61.0 140.1 %collective-permute-done.1 = f32[8,8,1024]{2,1,0:T(8,128)S(1)} collective-permute-done((f32[8,8,1024]{2,1,0:T(8,128)S(1)}, f32[8,8,1024]{2,1,0:T(8,128)S(1)}, u32[]{:S(2)}, u32[]{:S(2)}) %collective-permute-start.1) | collective-permute-done | bytes 262176 | tf_op jit(solution)/shard_map/ppermute | solution.py:19
  201.1 2.0 collective-permute-start.2
  204.0 1.2 collective-permute-start.14
  205.3 11.0 %collective-permute-done.2 = f32[4,8,1024]{2,1,0:T(8,128)S(1)} collective-permute-done((f32[4,8,1024]{2,1,0:T(8,128)S(1)}, f32[4,8,1024]{2,1,0:T(8,128)S(1)}, u32[]{:S(2)}, u32[]{:S(2)}) %collective-permute-start.2) | collective-permute-done | bytes 131104 | tf_op jit(solution)/shard_map/ppermute | solution.py:19
  217.3 3.2 collective-permute-done.14
  221.8 3.2 collective-permute-start.4
  225.2 8.6 %collective-permute-done.15 = bf16[64,4096]{1,0:T(8,128)(2,1)S(1)} collective-permute-done((bf16[64,4096]{1,0:T(8,128)(2,1)S(1)}, bf16[64,4096]{1,0:T(8,128)(2,1)S(1)}, u32[]{:S(2)}, u32[]{:S(2)}) %collective-permute-start.15) | collective-permute-done | bytes 524320 | tf_op jit(solution)/shard_map/ppermute | solution.py:19
  234.8 1.2 collective-permute-done.4
  236.6 1.4 maximum_select_fusion.3
  238.0 5.2 %collective-permute-start.11 = (bf16[4,128,1024]{2,1,0:T(8,128)(2,1)S(1)}, bf16[4,128,1024]{2,1,0:T(8,128)(2,1)S(1)}, u32[]{:S(2)}, u32[]{:S(2)}) collective-permute-start(bf16[4,128,1024]{2,1,0:T(8,128)(2,1)S(1)} %copy-done.8), channel_id=1, source_target_pairs={{0,224},{32,0},{64,32},{96,64},{128,96},{160,128},{192,160},{224,1... | collective-permute-start | bytes 3145736 | tf_op jit(solution)/shard_map/ppermute | solution.py:91
  243.3 2.1 fusion.47
  245.4 2.3 constant_dynamic-update-slice_fusion.6
  247.7 2.3 constant_dynamic-update-slice_fusion.5
  250.0 3.0 collective-permute-start.16
  252.9 2.3 constant_dynamic-update-slice_fusion.4
  255.2 25.5 %collective-permute-done.8 = bf16[4,128,1024]{2,1,0:T(8,128)(2,1)S(1)} collective-permute-done((bf16[4,128,1024]{2,1,0:T(8,128)(2,1)S(1)}, bf16[4,128,1024]{2,1,0:T(8,128)(2,1)S(1)}, u32[]{:S(2)}, u32[]{:S(2)}) %collective-permute-start.8) | collective-permute-done | bytes 1048608 | tf_op jit(solution)/shard_map/ppermute | solution.py:91
  283.9 52.5 %collective-permute-done.11 = bf16[4,128,1024]{2,1,0:T(8,128)(2,1)S(1)} collective-permute-done((bf16[4,128,1024]{2,1,0:T(8,128)(2,1)S(1)}, bf16[4,128,1024]{2,1,0:T(8,128)(2,1)S(1)}, u32[]{:S(2)}, u32[]{:S(2)}) %collective-permute-start.11) | collective-permute-done | bytes 1048608 | tf_op jit(solution)/shard_map/ppermute | solution.py:91
  337.5 4.1 gather_fusion
  341.6 2.6 copy.430
  344.2 2.4 select_select_fusion
  346.8 2.3 copy.455
  349.6 13.7 %fusion = (f32[4,8,256]{2,1,0:T(8,128)S(1)}, f32[4,1024,256,8]{2,1,3,0:T(8,128)}) fusion(pred[256,1024]{0,1:T(8,128)(4,1)S(1)} %fusion.21, bf16[1024,4,128,1]{0,2,3,1:T(8,128)(2,1)S(1)} %bitcast.490, bf16[128,4,8,128]{3,0,2,1:T(8,128)(2,1)S(1)} %copy-done.7, bf16[128,4,8,128]{3,0,2,1:T(8,128)(2,1)S(1)} %copy.381, pred[]{:T(512)S(6)} %eq.106), kind=kOutput, calls=%fused_computation.12 | convolution fusion | flops 2182078464 | bytes 36995072 | tf_op jit(solution)/shard_map/rkgd,tkd->kgrt/dot_general | solution.py:136
  363.3 15.0 %fusion.1 = f32[4,8,256]{2,1,0:T(8,128)S(1)} fusion(f32[4,1024,256,8]{2,1,3,0:T(8,128)} %get-tuple-element.67, f32[4,8,256]{2,1,0:T(8,128)S(1)} %get-tuple-element.66, pred[256,1024]{0,1:T(8,128)(4,1)S(1)} %fusion.21), kind=kLoop, calls=%fused_computation.13 | loop fusion | flops 41934848 | bytes 33882112 | tf_op jit(solution)/shard_map/reduce_sum | solution.py:142
  378.3 16.0 %fusion.6 = f32[256,4,8,128]{0,3,2,1:T(8,128)} fusion(bf16[1024,4,128,1]{0,2,3,1:T(8,128)(2,1)S(1)} %bitcast.489, f32[4,1024,256,8]{2,1,3,0:T(8,128)} %get-tuple-element.67, f32[4,8,256]{2,1,0:T(8,128)S(1)} %get-tuple-element.66, pred[256,1024]{0,1:T(8,128)(4,1)S(1)} %fusion.21), kind=kOutput, calls=%fused_computation.17 | convolution fusion | flops 2189426688 | bytes 39092224 | tf_op jit(solution)/shard_map/kgrt,tkd->rkgd/dot_general | solution.py:143
  394.3 5.5 %copy.385 = f32[256,4,8,128]{3,2,1,0:T(8,128)} copy(f32[256,4,8,128]{0,3,2,1:T(8,128)} %fusion.6) | data formatting | bytes 8388608 | tf_op jit(solution)/shard_map/kgrt,tkd->rkgd/transpose | solution.py:143
  400.6 2.8 select_bitcast_fusion
  406.1 2.2 collective-permute-done.27
  410.6 2.1 collective-permute-start.19
  413.0 1.1 collective-permute-done.28
  414.6 3.5 fusion.17
  418.3 2.1 collective-permute-start.20
  420.4 16.0 %collective-permute-start.21 = (f32[4,8,32]{2,1,0:T(8,128)S(1)}, f32[4,8,32]{2,1,0:T(8,128)S(1)}, u32[]{:S(2)}, u32[]{:S(2)}) collective-permute-start(f32[4,8,32]{2,1,0:T(8,128)S(1)} %select_bitcast_fusion.14), channel_id=1, source_target_pairs={{0,4},{1,5},{2,6},{3,7},{4,0},{5,1},{6,2},{7,3},{8,12},{9,13},{10,... | collective-permute-start | bytes 12296 | tf_op jit(solution)/shard_map/ppermute | solution.py:19
  436.5 5.7 %collective-permute-done.21 = f32[4,8,32]{2,1,0:T(8,128)S(1)} collective-permute-done((f32[4,8,32]{2,1,0:T(8,128)S(1)}, f32[4,8,32]{2,1,0:T(8,128)S(1)}, u32[]{:S(2)}, u32[]{:S(2)}) %collective-permute-start.21) | collective-permute-done | bytes 4128 | tf_op jit(solution)/shard_map/ppermute | solution.py:19
  442.4 2.0 collective-permute-start.23
  445.4 16.0 %collective-permute-start.22 = (f32[4,8,32,128]{3,2,1,0:T(8,128)S(1)}, f32[4,8,32,128]{3,2,1,0:T(8,128)S(1)}, u32[]{:S(2)}, u32[]{:S(2)}) collective-permute-start(f32[4,8,32,128]{3,2,1,0:T(8,128)S(1)} %select_bitcast_fusion.2), channel_id=1, source_target_pairs={{0,4},{1,5},{2,6},{3,7},{4,0},{5,1},{6,2},{7,3},{8,12},{9,13},{10,... | collective-permute-start | bytes 1572872 | tf_op jit(solution)/shard_map/ppermute | solution.py:19
  461.4 21.1 %collective-permute-done.22 = f32[4,8,32,128]{3,2,1,0:T(8,128)S(1)} collective-permute-done((f32[4,8,32,128]{3,2,1,0:T(8,128)S(1)}, f32[4,8,32,128]{3,2,1,0:T(8,128)S(1)}, u32[]{:S(2)}, u32[]{:S(2)}) %collective-permute-start.22) | collective-permute-done | bytes 524320 | tf_op jit(solution)/shard_map/ppermute | solution.py:19
  483.7 3.3 collective-permute-start.24
  487.0 4.4 collective-permute-start.31
  491.4 3.9 copy.425
  496.8 2.4 collective-permute-start.26
  499.2 4.1 collective-permute-done.26
  (199 shorter events, 36.0 us)
Async XLA Ops:
  0.6 6.0 %copy-start = (bf16[8,128,1024]{2,1,0:T(8,128)(2,1)S(1)}, bf16[8,128,1024]{2,1,0:T(8,128)(2,1)}, u32[]{:S(2)}) copy-start(bf16[8,128,1024]{2,1,0:T(8,128)(2,1)} %param.10) | copy-start | bytes 6291460
  0.6 59.1 %collective-permute-start.12 = (bf16[8,4096]{1,0:T(8,128)(2,1)}, bf16[8,4096]{1,0:T(8,128)(2,1)S(1)}, u32[]{:S(2)}, u32[]{:S(2)}) collective-permute-start(bf16[8,4096]{1,0:T(8,128)(2,1)} %bitcast.510), channel_id=1, source_target_pairs={{0,1},{1,0},{2,3},{3,2},{4,5},{5,4},{6,7},{7,6},{8,9},{9,8},{10,11... | collective-permute-start | bytes 196616 | tf_op jit(solution)/shard_map/ppermute | solution.py:19
  3.2 54.3 %collective-permute-start = (f32[16,8,1024]{2,1,0:T(8,128)}, f32[16,8,1024]{2,1,0:T(8,128)}, u32[]{:S(2)}, u32[]{:S(2)}) collective-permute-start(f32[16,8,1024]{2,1,0:T(8,128)} %select_bitcast_fusion.3), channel_id=1, source_target_pairs={{0,1},{1,0},{2,3},{3,2},{4,5},{5,4},{6,7},{7,6},{8,9},{9,8},{10,11... | collective-permute-start | bytes 1572872 | tf_op jit(solution)/shard_map/ppermute | solution.py:19
  10.6 225.9 %collective-permute-start.5 = (bf16[4,128,1024]{2,1,0:T(8,128)(2,1)}, bf16[4,128,1024]{2,1,0:T(8,128)(2,1)}, u32[]{:S(2)}, u32[]{:S(2)}) collective-permute-start(bf16[4,128,1024]{2,1,0:T(8,128)(2,1)} %select_select_fusion.7), channel_id=1, source_target_pairs={{0,32},{32,64},{64,96},{96,128},{128,160},{160,192},{192,224},{224... | collective-permute-start | bytes 3145736 | tf_op jit(solution)/shard_map/ppermute | solution.py:91
  17.8 10.5 %copy-start.17 = (s32[8]{0:T(128)S(1)}, s32[8]{0:T(128)}, u32[]{:S(2)}) copy-start(s32[8]{0:T(128)} %param.12) | copy-start | bytes 100
  17.8 14.8 %copy-start.14 = (s32[1,256]{1,0:T(1,128)S(1)}, s32[1,256]{1,0:T(1,128)}, u32[]{:S(2)}) copy-start(s32[1,256]{1,0:T(1,128)} %param.13) | copy-start | bytes 3076
  17.8 17.9 %copy-start.13 = (s32[1,256,8]{1,2,0:T(8,128)S(1)}, s32[1,256,8]{1,2,0:T(8,128)}, u32[]{:S(2)}) copy-start(s32[1,256,8]{1,2,0:T(8,128)} %param.17) | copy-start | bytes 24580
  21.8 216.2 %collective-permute-start.6 = (bf16[4,128,1024]{2,1,0:T(8,128)(2,1)}, bf16[4,128,1024]{2,1,0:T(8,128)(2,1)}, u32[]{:S(2)}, u32[]{:S(2)}) collective-permute-start(bf16[4,128,1024]{2,1,0:T(8,128)(2,1)} %select_select_fusion.6), channel_id=1, source_target_pairs={{0,64},{32,96},{64,128},{96,160},{128,192},{160,224},{192,0},{224,... | collective-permute-start | bytes 3145736 | tf_op jit(solution)/shard_map/ppermute | solution.py:91
  28.2 221.7 %collective-permute-start.7 = (bf16[4,128,1024]{2,1,0:T(8,128)(2,1)}, bf16[4,128,1024]{2,1,0:T(8,128)(2,1)}, u32[]{:S(2)}, u32[]{:S(2)}) collective-permute-start(bf16[4,128,1024]{2,1,0:T(8,128)(2,1)} %select_select_fusion.5), channel_id=1, source_target_pairs={{0,96},{32,128},{64,160},{96,192},{128,224},{160,0},{192,32},{224,... | collective-permute-start | bytes 3145736 | tf_op jit(solution)/shard_map/ppermute | solution.py:91
  32.7 10.3 %copy-start.18 = (s32[8]{0:T(128)}, s32[8]{0:T(128)S(1)}, u32[]{:S(2)}) copy-start(s32[8]{0:T(128)S(1)} %fusion.98) | copy-start | bytes 100
  33.4 1.6 copy-start.16
  36.6 6.4 %copy-start.22 = (pred[4]{0:T(512)(128)(4,1)S(1)}, pred[4]{0:T(512)(128)(4,1)}, u32[]{:S(2)}) copy-start(pred[4]{0:T(512)(128)(4,1)} %compare_and_fusion.1) | copy-start | bytes 16
  38.2 7.3 %copy-start.21 = (pred[4]{0:T(512)(128)(4,1)S(1)}, pred[4]{0:T(512)(128)(4,1)}, u32[]{:S(2)}) copy-start(pred[4]{0:T(512)(128)(4,1)} %compare_and_fusion.2) | copy-start | bytes 16
  39.8 8.1 %copy-start.20 = (pred[4]{0:T(512)(128)(4,1)S(1)}, pred[4]{0:T(512)(128)(4,1)}, u32[]{:S(2)}) copy-start(pred[4]{0:T(512)(128)(4,1)} %compare_and_fusion.3) | copy-start | bytes 16
  43.0 5.0 copy-start.6
  43.0 6.2 %copy-start.5 = (bf16[4,128,1024]{2,1,0:T(8,128)(2,1)S(1)}, bf16[4,128,1024]{2,1,0:T(8,128)(2,1)}, u32[]{:S(2)}) copy-start(bf16[4,128,1024]{2,1,0:T(8,128)(2,1)} %gather_fusion.6) | copy-start | bytes 3145732
  50.3 9.5 %copy-start.12 = (bf16[1,8,4096]{2,1,0:T(8,128)(2,1)S(1)}, bf16[1,8,4096]{2,1,0:T(8,128)(2,1)}, u32[]{:S(2)}) copy-start(bf16[1,8,4096]{2,1,0:T(8,128)(2,1)} %param.16) | copy-start | bytes 196612
  58.6 175.2 %copy-start.11 = (bf16[4,128,1024]{2,1,0:T(8,128)(2,1)S(1)}, bf16[4,128,1024]{2,1,0:T(8,128)(2,1)}, u32[]{:S(2)}) copy-start(bf16[4,128,1024]{2,1,0:T(8,128)(2,1)} %select_select_fusion.4) | copy-start | bytes 3145732
  58.6 177.3 %copy-start.10 = (bf16[4,128,1024]{2,1,0:T(8,128)(2,1)S(1)}, bf16[4,128,1024]{2,1,0:T(8,128)(2,1)}, u32[]{:S(2)}) copy-start(bf16[4,128,1024]{2,1,0:T(8,128)(2,1)} %select_select_fusion.3) | copy-start | bytes 3145732
  58.7 142.4 %collective-permute-start.1 = (f32[8,8,1024]{2,1,0:T(8,128)S(1)}, f32[8,8,1024]{2,1,0:T(8,128)S(1)}, u32[]{:S(2)}, u32[]{:S(2)}) collective-permute-start(f32[8,8,1024]{2,1,0:T(8,128)S(1)} %select_bitcast_fusion.6), channel_id=1, source_target_pairs={{0,2},{1,3},{2,0},{3,1},{4,6},{5,7},{6,4},{7,5},{8,10},{9,11},{10,... | collective-permute-start | bytes 786440 | tf_op jit(solution)/shard_map/ppermute | solution.py:19
  59.8 144.1 %collective-permute-start.13 = (bf16[16,4096]{1,0:T(8,128)(2,1)S(1)}, bf16[16,4096]{1,0:T(8,128)(2,1)S(1)}, u32[]{:S(2)}, u32[]{:S(2)}) collective-permute-start(bf16[16,4096]{1,0:T(8,128)(2,1)S(1)} %maximum_select_fusion.8), channel_id=1, source_target_pairs={{0,2},{1,3},{2,0},{3,1},{4,6},{5,7},{6,4},{7,5},{8,10},{9,11},{10,... | collective-permute-start | bytes 393224 | tf_op jit(solution)/shard_map/ppermute | solution.py:19
  201.1 15.2 %collective-permute-start.2 = (f32[4,8,1024]{2,1,0:T(8,128)S(1)}, f32[4,8,1024]{2,1,0:T(8,128)S(1)}, u32[]{:S(2)}, u32[]{:S(2)}) collective-permute-start(f32[4,8,1024]{2,1,0:T(8,128)S(1)} %select_bitcast_fusion.8), channel_id=1, source_target_pairs={{0,4},{1,5},{2,6},{3,7},{4,0},{5,1},{6,2},{7,3},{8,12},{9,13},{10,... | collective-permute-start | bytes 393224 | tf_op jit(solution)/shard_map/ppermute | solution.py:19
  204.0 16.5 %collective-permute-start.14 = (bf16[32,4096]{1,0:T(8,128)(2,1)S(1)}, bf16[32,4096]{1,0:T(8,128)(2,1)S(1)}, u32[]{:S(2)}, u32[]{:S(2)}) collective-permute-start(bf16[32,4096]{1,0:T(8,128)(2,1)S(1)} %maximum_select_fusion.6), channel_id=1, source_target_pairs={{0,4},{1,5},{2,6},{3,7},{4,0},{5,1},{6,2},{7,3},{8,12},{9,13},{10,... | collective-permute-start | bytes 786440 | tf_op jit(solution)/shard_map/ppermute | solution.py:19
  205.3 31.2 %copy-start.9 = (bf16[4,128,1024]{2,1,0:T(8,128)(2,1)S(1)}, bf16[4,128,1024]{2,1,0:T(8,128)(2,1)}, u32[]{:S(2)}) copy-start(bf16[4,128,1024]{2,1,0:T(8,128)(2,1)} %select_select_fusion.2) | copy-start | bytes 3145732
  216.3 5.5 %collective-permute-start.3 = (f32[2,8,1024]{2,1,0:T(8,128)S(1)}, f32[2,8,1024]{2,1,0:T(8,128)S(1)}, u32[]{:S(2)}, u32[]{:S(2)}) collective-permute-start(f32[2,8,1024]{2,1,0:T(8,128)S(1)} %select_bitcast_fusion.9), channel_id=1, source_target_pairs={{0,8},{1,9},{2,10},{3,11},{4,12},{5,13},{6,14},{7,15},{8,0},{9,1},... | collective-permute-start | bytes 196616 | tf_op jit(solution)/shard_map/ppermute | solution.py:19
  220.7 17.3 %copy-start.8 = (bf16[4,128,1024]{2,1,0:T(8,128)(2,1)S(1)}, bf16[4,128,1024]{2,1,0:T(8,128)(2,1)}, u32[]{:S(2)}) copy-start(bf16[4,128,1024]{2,1,0:T(8,128)(2,1)} %select_select_fusion.1) | copy-start | bytes 3145732
  220.7 22.6 %copy-start.19 = (s32[8]{0:T(128)S(1)}, s32[8]{0:T(128)}, u32[]{:S(2)}) copy-start(s32[8]{0:T(128)} %copy-done.18) | copy-start | bytes 100
  220.8 13.0 %collective-permute-start.15 = (bf16[64,4096]{1,0:T(8,128)(2,1)S(1)}, bf16[64,4096]{1,0:T(8,128)(2,1)S(1)}, u32[]{:S(2)}, u32[]{:S(2)}) collective-permute-start(bf16[64,4096]{1,0:T(8,128)(2,1)S(1)} %maximum_select_fusion.4), channel_id=1, source_target_pairs={{0,8},{1,9},{2,10},{3,11},{4,12},{5,13},{6,14},{7,15},{8,0},{9,1},... | collective-permute-start | bytes 1572872 | tf_op jit(solution)/shard_map/ppermute | solution.py:19
  221.8 14.2 %collective-permute-start.4 = (f32[1,8,1024]{2,1,0:T(8,128)S(1)}, f32[1,8,1024]{2,1,0:T(8,128)S(1)}, u32[]{:S(2)}, u32[]{:S(2)}) collective-permute-start(f32[1,8,1024]{2,1,0:T(8,128)S(1)} %select_bitcast_fusion.12), channel_id=1, source_target_pairs={{0,16},{1,17},{2,18},{3,19},{4,20},{5,21},{6,22},{7,23},{8,24},{9,... | collective-permute-start | bytes 98312 | tf_op jit(solution)/shard_map/ppermute | solution.py:19
  233.8 46.9 %collective-permute-start.8 = (bf16[4,128,1024]{2,1,0:T(8,128)(2,1)S(1)}, bf16[4,128,1024]{2,1,0:T(8,128)(2,1)S(1)}, u32[]{:S(2)}, u32[]{:S(2)}) collective-permute-start(bf16[4,128,1024]{2,1,0:T(8,128)(2,1)S(1)} %copy-done.11), channel_id=1, source_target_pairs={{0,128},{32,160},{64,192},{96,224},{128,0},{160,32},{192,64},{224,... | collective-permute-start | bytes 3145736 | tf_op jit(solution)/shard_map/ppermute | solution.py:91
  236.0 45.8 %collective-permute-start.9 = (bf16[4,128,1024]{2,1,0:T(8,128)(2,1)S(1)}, bf16[4,128,1024]{2,1,0:T(8,128)(2,1)S(1)}, u32[]{:S(2)}, u32[]{:S(2)}) collective-permute-start(bf16[4,128,1024]{2,1,0:T(8,128)(2,1)S(1)} %copy-done.10), channel_id=1, source_target_pairs={{0,160},{32,192},{64,224},{96,0},{128,32},{160,64},{192,96},{224,1... | collective-permute-start | bytes 3145736 | tf_op jit(solution)/shard_map/ppermute | solution.py:91
  236.5 46.3 %collective-permute-start.10 = (bf16[4,128,1024]{2,1,0:T(8,128)(2,1)S(1)}, bf16[4,128,1024]{2,1,0:T(8,128)(2,1)S(1)}, u32[]{:S(2)}, u32[]{:S(2)}) collective-permute-start(bf16[4,128,1024]{2,1,0:T(8,128)(2,1)S(1)} %copy-done.9), channel_id=1, source_target_pairs={{0,192},{32,224},{64,0},{96,32},{128,64},{160,96},{192,128},{224,1... | collective-permute-start | bytes 3145736 | tf_op jit(solution)/shard_map/ppermute | solution.py:91
  238.0 98.4 %collective-permute-start.11 = (bf16[4,128,1024]{2,1,0:T(8,128)(2,1)S(1)}, bf16[4,128,1024]{2,1,0:T(8,128)(2,1)S(1)}, u32[]{:S(2)}, u32[]{:S(2)}) collective-permute-start(bf16[4,128,1024]{2,1,0:T(8,128)(2,1)S(1)} %copy-done.8), channel_id=1, source_target_pairs={{0,224},{32,0},{64,32},{96,64},{128,96},{160,128},{192,160},{224,1... | collective-permute-start | bytes 3145736 | tf_op jit(solution)/shard_map/ppermute | solution.py:91
  250.0 96.9 %collective-permute-start.16 = (bf16[128,4096]{1,0:T(8,128)(2,1)S(1)}, bf16[128,4096]{1,0:T(8,128)(2,1)}, u32[]{:S(2)}, u32[]{:S(2)}) collective-permute-start(bf16[128,4096]{1,0:T(8,128)(2,1)S(1)} %maximum_select_fusion.2), channel_id=1, source_target_pairs={{0,16},{1,17},{2,18},{3,19},{4,20},{5,21},{6,22},{7,23},{8,24},{9,... | collective-permute-start | bytes 3145736 | tf_op jit(solution)/shard_map/ppermute | solution.py:19
  337.5 6.6 %copy-start.15 = (pred[1024]{0:T(1024)(128)(4,1)S(1)}, pred[1024]{0:T(1024)(128)(4,1)}, u32[]{:S(2)}) copy-start(pred[1024]{0:T(1024)(128)(4,1)} %fusion.48) | copy-start | bytes 3076
  346.6 2.9 copy-start.2
  346.6 2.9 copy-start.7
  403.4 11.2 %collective-permute-start.18 = (f32[16,8,32,128]{3,2,1,0:T(8,128)S(1)}, f32[16,8,32,128]{3,2,1,0:T(8,128)}, u32[]{:S(2)}, u32[]{:S(2)}) collective-permute-start(f32[16,8,32,128]{3,2,1,0:T(8,128)S(1)} %select_bitcast_fusion), channel_id=1, source_target_pairs={{0,1},{1,0},{2,3},{3,2},{4,5},{5,4},{6,7},{7,6},{8,9},{9,8},{10,11... | collective-permute-start | bytes 6291464 | tf_op jit(solution)/shard_map/ppermute | solution.py:19
  404.2 4.2 collective-permute-start.27
  406.0 2.6 collective-permute-start.17
  410.1 4.0 collective-permute-start.28
  410.6 4.0 collective-permute-start.19
  418.3 26.2 %collective-permute-start.20 = (f32[8,8,32,128]{3,2,1,0:T(8,128)S(1)}, f32[8,8,32,128]{3,2,1,0:T(8,128)S(1)}, u32[]{:S(2)}, u32[]{:S(2)}) collective-permute-start(f32[8,8,32,128]{3,2,1,0:T(8,128)S(1)} %select_bitcast_fusion.1), channel_id=1, source_target_pairs={{0,2},{1,3},{2,0},{3,1},{4,6},{5,7},{6,4},{7,5},{8,10},{9,11},{10,... | collective-permute-start | bytes 3145736 | tf_op jit(solution)/shard_map/ppermute | solution.py:19
  420.4 21.8 %collective-permute-start.21 = (f32[4,8,32]{2,1,0:T(8,128)S(1)}, f32[4,8,32]{2,1,0:T(8,128)S(1)}, u32[]{:S(2)}, u32[]{:S(2)}) collective-permute-start(f32[4,8,32]{2,1,0:T(8,128)S(1)} %select_bitcast_fusion.14), channel_id=1, source_target_pairs={{0,4},{1,5},{2,6},{3,7},{4,0},{5,1},{6,2},{7,3},{8,12},{9,13},{10,... | collective-permute-start | bytes 12296 | tf_op jit(solution)/shard_map/ppermute | solution.py:19
  436.4 6.0 %collective-permute-start.29 = (f32[4,8,32]{2,1,0:T(8,128)S(1)}, f32[4,8,32]{2,1,0:T(8,128)S(1)}, u32[]{:S(2)}, u32[]{:S(2)}) collective-permute-start(f32[4,8,32]{2,1,0:T(8,128)S(1)} %select_bitcast_fusion.13), channel_id=1, source_target_pairs={{0,4},{1,5},{2,6},{3,7},{4,0},{5,1},{6,2},{7,3},{8,12},{9,13},{10,... | collective-permute-start | bytes 12296 | tf_op jit(solution)/shard_map/ppermute | solution.py:19
  442.4 18.9 %collective-permute-start.23 = (f32[2,8,32]{2,1,0:T(8,128)S(1)}, f32[2,8,32]{2,1,0:T(8,128)S(1)}, u32[]{:S(2)}, u32[]{:S(2)}) collective-permute-start(f32[2,8,32]{2,1,0:T(8,128)S(1)} %select_bitcast_fusion.16), channel_id=1, source_target_pairs={{0,8},{1,9},{2,10},{3,11},{4,12},{5,13},{6,14},{7,15},{8,0},{9,1},... | collective-permute-start | bytes 6152 | tf_op jit(solution)/shard_map/ppermute | solution.py:19
  444.4 16.9 %collective-permute-start.30 = (f32[2,8,32]{2,1,0:T(8,128)S(1)}, f32[2,8,32]{2,1,0:T(8,128)S(1)}, u32[]{:S(2)}, u32[]{:S(2)}) collective-permute-start(f32[2,8,32]{2,1,0:T(8,128)S(1)} %select_bitcast_fusion.15), channel_id=1, source_target_pairs={{0,8},{1,9},{2,10},{3,11},{4,12},{5,13},{6,14},{7,15},{8,0},{9,1},... | collective-permute-start | bytes 6152 | tf_op jit(solution)/shard_map/ppermute | solution.py:19
  445.4 37.1 %collective-permute-start.22 = (f32[4,8,32,128]{3,2,1,0:T(8,128)S(1)}, f32[4,8,32,128]{3,2,1,0:T(8,128)S(1)}, u32[]{:S(2)}, u32[]{:S(2)}) collective-permute-start(f32[4,8,32,128]{3,2,1,0:T(8,128)S(1)} %select_bitcast_fusion.2), channel_id=1, source_target_pairs={{0,4},{1,5},{2,6},{3,7},{4,0},{5,1},{6,2},{7,3},{8,12},{9,13},{10,... | collective-permute-start | bytes 1572872 | tf_op jit(solution)/shard_map/ppermute | solution.py:19
  482.5 21.8 %copy-start.1 = (bf16[8,128,1024]{2,1,0:T(8,128)(2,1)S(1)}, bf16[8,128,1024]{2,1,0:T(8,128)(2,1)}, u32[]{:S(2)}) copy-start(bf16[8,128,1024]{2,1,0:T(8,128)(2,1)} %param.10) | copy-start | bytes 6291460
  482.8 0.8 copy-start.3
  483.7 12.9 %copy-start.4 = (f32[4,8,32,128]{3,2,1,0:T(8,128)S(1)}, f32[4,8,32,128]{3,2,1,0:T(8,128)}, u32[]{:S(2)}) copy-start(f32[4,8,32,128]{3,2,1,0:T(8,128)} %copy-done.3) | copy-start | bytes 1572868
  483.7 12.9 %collective-permute-start.24 = (f32[2,8,32,128]{3,2,1,0:T(8,128)S(1)}, f32[2,8,32,128]{3,2,1,0:T(8,128)S(1)}, u32[]{:S(2)}, u32[]{:S(2)}) collective-permute-start(f32[2,8,32,128]{3,2,1,0:T(8,128)S(1)} %select_bitcast_fusion.5), channel_id=1, source_target_pairs={{0,8},{1,9},{2,10},{3,11},{4,12},{5,13},{6,14},{7,15},{8,0},{9,1},... | collective-permute-start | bytes 786440 | tf_op jit(solution)/shard_map/ppermute | solution.py:19
  487.0 8.8 %collective-permute-start.31 = (f32[1,8,32]{2,1,0:T(8,128)S(1)}, f32[1,8,32]{2,1,0:T(8,128)S(1)}, u32[]{:S(2)}, u32[]{:S(2)}) collective-permute-start(f32[1,8,32]{2,1,0:T(8,128)S(1)} %select_bitcast_fusion.17), channel_id=1, source_target_pairs={{0,16},{1,17},{2,18},{3,19},{4,20},{5,21},{6,22},{7,23},{8,24},{9,... | collective-permute-start | bytes 3080 | tf_op jit(solution)/shard_map/ppermute | solution.py:19
  491.3 5.1 %collective-permute-start.25 = (f32[1,8,32]{2,1,0:T(8,128)S(1)}, f32[1,8,32]{2,1,0:T(8,128)S(1)}, u32[]{:S(2)}, u32[]{:S(2)}) collective-permute-start(f32[1,8,32]{2,1,0:T(8,128)S(1)} %select_bitcast_fusion.18), channel_id=1, source_target_pairs={{0,16},{1,17},{2,18},{3,19},{4,20},{5,21},{6,22},{7,23},{8,24},{9,... | collective-permute-start | bytes 3080 | tf_op jit(solution)/shard_map/ppermute | solution.py:19
  496.8 6.6 %collective-permute-start.26 = (f32[1,8,32,128]{3,2,1,0:T(8,128)S(1)}, f32[1,8,32,128]{3,2,1,0:T(8,128)S(1)}, u32[]{:S(2)}, u32[]{:S(2)}) collective-permute-start(f32[1,8,32,128]{3,2,1,0:T(8,128)S(1)} %select_bitcast_fusion.7), channel_id=1, source_target_pairs={{0,16},{1,17},{2,18},{3,19},{4,20},{5,21},{6,22},{7,23},{8,24},{9,... | collective-permute-start | bytes 393224 | tf_op jit(solution)/shard_map/ppermute | solution.py:19

commit v4 on v2

--- a/solution.py
+++ b/solution.py
@@ -1,6 +1,8 @@
 import jax
 import jax.numpy as jnp
 from jax import lax
+from jax.experimental import pallas as pl
+from jax.experimental.pallas import tpu as pltpu
 from jax.sharding import PartitionSpec as P
 
 QH = 32
@@ -59,6 +61,61 @@
     factor_b = jnp.exp(running_b - newest)
     numerator = numerator_a * factor_a[..., None] + numerator_b * factor_b[..., None]
     return (numerator, newest, totals_a * factor_a + totals_b * factor_b)
+
+
+def attend_kernel(query_ref, key_ref, value_ref, mask_ref, numerator_ref, running_ref, totals_ref):
+    per_group = QH // KVH
+    visible = mask_ref[...] > 0
+    keys = key_ref[...]
+    values = value_ref[...]
+    for head in range(per_group):
+        columns = slice(head * HD, (head + 1) * HD)
+        scores = lax.dot_general(
+            query_ref[:, columns],
+            keys,
+            (((1,), (1,)), ((), ())),
+            preferred_element_type=jnp.float32,
+        ) * HD ** (-0.5)
+        scores = jnp.where(visible, scores, -1e30)
+        highest = jnp.max(scores, axis=1, keepdims=True)
+        weights = jnp.where(visible, jnp.exp(scores - highest), 0.0)
+        numerator_ref[:, columns] = jnp.dot(
+            weights.astype(jnp.bfloat16), values, preferred_element_type=jnp.float32
+        )
+        running_ref[0, :, head : head + 1] = highest
+        totals_ref[0, :, head : head + 1] = jnp.sum(weights, axis=1, keepdims=True)
+
+
+def attend_local(all_queries, key_rows, value_rows, visible):
+    rows = all_queries.shape[0]
+    keys = key_rows.shape[0]
+    per_group = QH // KVH
+    width = per_group * HD
+    return pl.pallas_call(
+        attend_kernel,
+        grid=(KVH,),
+        in_specs=[
+            pl.BlockSpec((rows, width), lambda k: (0, k)),
+            pl.BlockSpec((keys, HD), lambda k: (0, k)),
+            pl.BlockSpec((keys, HD), lambda k: (0, k)),
+            pl.BlockSpec((rows, keys), lambda k: (0, 0)),
+        ],
+        out_specs=[
+            pl.BlockSpec((rows, width), lambda k: (0, k)),
+            pl.BlockSpec((1, rows, per_group), lambda k: (k, 0, 0)),
+            pl.BlockSpec((1, rows, per_group), lambda k: (k, 0, 0)),
+        ],
+        out_shape=[
+            jax.ShapeDtypeStruct((rows, QH * HD), jnp.float32),
+            jax.ShapeDtypeStruct((KVH, rows, per_group), jnp.float32),
+            jax.ShapeDtypeStruct((KVH, rows, per_group), jnp.float32),
+        ],
+        cost_estimate=pl.CostEstimate(
+            flops=4 * rows * keys * QH * HD,
+            transcendentals=rows * keys * QH,
+            bytes_accessed=rows * QH * HD * 6 + keys * KVH * HD * 4 + rows * keys * 4,
+        ),
+    )(all_queries, key_rows, value_rows, visible)
 
 def on_device(span_cache, retrieval, counts, recompute_pos, hidden, kv_weight, queries, block_mask):
     owner_count = lax.axis_size("owner")
@@ -108,8 +165,6 @@
     ).astype(jnp.bfloat16)
     context = jnp.where(jnp.any(matches, axis=1)[:, None], placed, context)
     key_width = KVH * HD
-    key_rows = context[:, :key_width].reshape(CTX_DEV, KVH, HD)
-    value_rows = context[:, key_width:].reshape(CTX_DEV, KVH, HD)
     key_pos = my_ctx * CTX_DEV + jnp.arange(CTX_DEV, dtype=jnp.int32)
     key_in_use = key_pos // BLK < my_count
     mask_cols = block_mask[0]
@@ -120,23 +175,15 @@
     allowed = jnp.take(mask_cols, query_pos // BLK, axis=0)
     visible = jnp.repeat(allowed, BLK, axis=1) > 0
     visible = visible & key_in_use[None, :] & (key_pos[None, :] <= query_pos[:, None])
-    grouped = all_queries.reshape(query_count, KVH, per_group, HD)
-    scores = jnp.einsum(
-        "rkgd,tkd->kgrt", grouped, key_rows, preferred_element_type=jnp.float32
-    ) * HD ** (-0.5)
-    scores = jnp.where(visible[None, None], scores, -1e30)
-    local_max = jnp.max(scores, axis=3)
-    weights = jnp.where(visible[None, None], jnp.exp(scores - local_max[..., None]), 0.0)
-    local_sum = jnp.sum(weights, axis=3)
-    weighted = jnp.einsum(
-        "kgrt,tkd->rkgd",
-        weights.astype(jnp.bfloat16),
-        value_rows,
-        preferred_element_type=jnp.float32,
-    )
-    running = jnp.transpose(local_max, (2, 0, 1)).reshape(query_count, QH)
-    totals = jnp.transpose(local_sum, (2, 0, 1)).reshape(query_count, QH)
-    numerator = weighted.reshape(query_count, QH, HD)
+    numerator, running, totals = attend_local(
+        all_queries,
+        context[:, :key_width],
+        context[:, key_width:],
+        visible.astype(jnp.float32),
+    )
+    running = jnp.transpose(running, (1, 0, 2)).reshape(query_count, QH)
+    totals = jnp.transpose(totals, (1, 0, 2)).reshape(query_count, QH)
+    numerator = numerator.reshape(query_count, QH, HD)
     numerator, running, totals = scatter_rows(
         (
             numerator.reshape(cycle_size, RCP, QH, HD),

time: 421 us -> 393 us (0.933)
  matrix products: 32.5 us -> 2.78 us
  Pallas kernels: 0 us -> 21.5 us
  other arithmetic: 40.9 us -> 26.4 us
  local copies, waits for them, and re-layouts: 28.6 us -> 22 us
    dot_general x2 -> x0, matrix products: 29.8 us -> none  [the longest x1 16 us: on_device(): jnp.einsum('kgrt,tkd->rkgd', weights.astype(jnp.bfloat16), value_rows, pr...]
    pallas_call x0 -> x1, Pallas kernels: none -> 21.5 us  [attend_local(): pl.pallas_call(attend_kernel, grid=(KVH,), in_specs=[pl.BlockSpec((rows,...]
    reduce_sum x1 -> x0, other arithmetic: 15 us -> none  [on_device(): local_sum = jnp.sum(weights, axis=3)]
  transfers between devices with their start and end apart: 26 -> 26, of which waited for: 14 -> 13; matrix products, arithmetic and copies ran while one was open for 6% -> 6% of each run, Pallas kernels for 0% -> 0%
where the time goes in v4:
time: 393 us; the launch traced here: 391 us
  waiting for transfers between devices  274 us (70%)
  starting transfers between devices  43.6 us (11%)
  other arithmetic  26.4 us (7%)
  local copies, waits for them, and re-layouts  22 us (6%)
  Pallas kernels  21.5 us (5%)
    ppermute x25, waiting for transfers between devices, exchange(): return lax.ppermute(shard, 'ctx', [(i, i ^ bit) for i in range(peers)])  274 us
    ppermute x25, starting transfers between devices, exchange(): return lax.ppermute(shard, 'ctx', [(i, i ^ bit) for i in range(peers)])  32.1 us
    pallas_call x1, Pallas kernels, attend_local(): pl.pallas_call(attend_kernel, grid=(KVH,), in_specs=[pl.BlockSpec((rows,...  21.5 us
    all_to_all x1, starting transfers between devices, on_device(): lax.all_to_all(outgoing, 'owner', split_axis=0, concat_axis=0, tiled=True)  11.6 us
  transfers between devices with their start and end apart: 26, of which 13 were waited for; matrix products, arithmetic and copies ran while one was open for 6% of the time, Pallas kernels for 0%

profile of v4, /device:TPU:6, one launch (start us, length us, event | category | flops | bytes accessed | tf_op | source)
XLA Modules:
  0.0 391.3 jit_solution(5010029228263589772)
XLA Ops:
  0.7 0.9 fusion.70
  1.7 0.7 add_select_fusion.1
  3.1 4.8 %gather_fusion = bf16[32,128,1024]{2,1,0:T(8,128)(2,1)} fusion(bf16[8,128,1024]{2,1,0:T(8,128)(2,1)S(1)} %copy-done, s32[1024]{0:T(1024)S(1)} %pad_clamp_fusion.2), kind=kCustom, calls=%fused_computation | custom fusion | bytes 16777344 | tf_op jit(solution)/shard_map/jit(_take)/gather | solution.py:138
  7.9 7.6 %select_select_fusion = bf16[8,4,128,1024]{3,2,1,0:T(8,128)(2,1)} fusion(bf16[8,4,128,1024]{3,2,1,0:T(8,128)(2,1)} %bitcast.418, pred[8,4]{1,0:T(8,128)(4,1)S(1)} %copy.240, pred[8,4]{1,0:T(8,128)(4,1)S(1)} %copy.239), kind=kLoop, calls=%fused_computation.3 | loop fusion | flops 8388608 | bytes 16777280 | tf_op jit(solution)/shard_map/jit(_where)/select_n | solution.py:137
  15.6 11.6 %all-to-all-start = ((bf16[8,4,128,1024]{3,2,1,0:T(8,128)(2,1)}), bf16[8,4,128,1024]{3,2,1,0:T(8,128)(2,1)}, u32[]{:S(2)}, u32[]{:S(2)}) async-start(bf16[8,4,128,1024]{3,2,1,0:T(8,128)(2,1)} %select_select_fusion), calls=%async_computation | async-start | bytes 16777216 | tf_op jit(solution)/shard_map/all_to_all | solution.py:140
  27.2 0.3 fusion.12
  27.7 0.3 copy-done.7
  28.2 0.6 dynamic_slice.12
  28.9 0.7 gather_fusion.2
  29.7 0.7 fusion.64
  30.4 0.7 and_select_fusion.5
  31.1 0.7 broadcast_compare_fusion
  31.7 0.7 fusion.50
  32.6 0.3 broadcast_in_dim.120
  32.9 1.2 fusion.6.mask_ref
  34.4 1.1 collective-permute-start.6
  35.5 0.7 fusion.63
  36.3 177.2 %collective-permute-done.6 = bf16[16,4096]{1,0:T(8,128)(2,1)S(1)} collective-permute-done((bf16[16,4096]{1,0:T(8,128)(2,1)S(1)}, bf16[16,4096]{1,0:T(8,128)(2,1)S(1)}, u32[]{:S(2)}, u32[]{:S(2)}) %collective-permute-start.6) | collective-permute-done | bytes 131104 | tf_op jit(solution)/shard_map/ppermute | solution.py:21
  213.5 0.6 collective-permute-start.7
  214.3 2.6 collective-permute-start.1
  216.9 10.6 %collective-permute-done.7 = bf16[32,4096]{1,0:T(8,128)(2,1)S(1)} collective-permute-done((bf16[32,4096]{1,0:T(8,128)(2,1)S(1)}, bf16[32,4096]{1,0:T(8,128)(2,1)S(1)}, u32[]{:S(2)}, u32[]{:S(2)}) %collective-permute-start.7) | collective-permute-done | bytes 262176 | tf_op jit(solution)/shard_map/ppermute | solution.py:21
  227.6 1.8 collective-permute-start.8
  229.6 11.8 %collective-permute-done.8 = bf16[64,4096]{1,0:T(8,128)(2,1)S(1)} collective-permute-done((bf16[64,4096]{1,0:T(8,128)(2,1)S(1)}, bf16[64,4096]{1,0:T(8,128)(2,1)S(1)}, u32[]{:S(2)}, u32[]{:S(2)}) %collective-permute-start.8) | collective-permute-done | bytes 524320 | tf_op jit(solution)/shard_map/ppermute | solution.py:21
  241.6 2.7 collective-permute-start.9
  244.5 1.2 collective-permute-start.3
  245.7 23.3 %collective-permute-done.3 = f32[2,8,1024]{2,1,0:T(8,128)S(1)} collective-permute-done((f32[2,8,1024]{2,1,0:T(8,128)S(1)}, f32[2,8,1024]{2,1,0:T(8,128)S(1)}, u32[]{:S(2)}, u32[]{:S(2)}) %collective-permute-start.3) | collective-permute-done | bytes 65568 | tf_op jit(solution)/shard_map/ppermute | solution.py:21
  269.0 2.4 collective-permute-start.4
  271.4 1.9 maximum_select_fusion.query_ref
  273.3 5.4 %gather_fusion.1 = bf16[8,128,1024]{2,1,0:T(8,128)(2,1)} fusion(bf16[32,128,1024]{2,1,0:T(8,128)(2,1)} %bitcast.35, s32[1024]{0:T(1024)S(1)} %pad_clamp_fusion.1), kind=kCustom, calls=%fused_computation.1 | custom fusion | bytes 4194336 | tf_op jit(solution)/shard_map/jit(_take)/gather | solution.py:152
  278.7 2.5 fusion.1
  281.2 1.7 fusion.72
  282.9 0.3 copy-done.3
  283.2 21.5 %shard_map.95 = (f32[256,4096]{1,0:T(8,128)}, f32[4,256,8]{2,1,0:T(8,128)}, f32[4,256,8]{2,1,0:T(8,128)}) custom-call(bf16[256,4096]{1,0:T(8,128)(2,1)} %maximum_select_fusion.query_ref, bf16[1024,512]{1,0:T(8,128)(2,1)} %get-tuple-element.33.key_ref, bf16[1024,512]{1,0:T(8,128)(2,1)} %get-tuple-element.32.value_ref, f32[256,1024]{1,0:T(8,128)} %fusion.6.mask_ref), custom_call_target="tpu_custom_call" | custom-call | flops 4294967296 | bytes 9437184 | tf_op jit(solution)/shard_map/pallas_call | solution.py:94
  304.7 2.6 fusion.71
  307.4 2.1 select_bitcast_fusion
  309.6 0.8 reshape_reshape_reshape.11
  310.4 0.4 fusion.73
  310.9 0.6 collective-permute-start.20
  311.5 1.2 copy.245
  312.7 0.8 reshape_reshape_reshape.10
  313.5 0.5 broadcast_select_fusion
  314.3 1.3 collective-permute-done.10
  315.6 1.1 fusion.20
  317.1 0.3 collective-permute-start.21
  317.8 2.1 collective-permute-start.12
  320.2 1.1 collective-permute-done.21
  321.3 0.5 collective-permute-done.12
  321.9 2.8 fusion
  324.9 2.1 collective-permute-start.13
  327.0 1.2 collective-permute-start.22
  328.2 1.8 collective-permute-start.14
  329.9 18.9 %collective-permute-done.22 = f32[4,8,32]{2,1,0:T(8,128)S(1)} collective-permute-done((f32[4,8,32]{2,1,0:T(8,128)S(1)}, f32[4,8,32]{2,1,0:T(8,128)S(1)}, u32[]{:S(2)}, u32[]{:S(2)}) %collective-permute-start.22) | collective-permute-done | bytes 4128 | tf_op jit(solution)/shard_map/ppermute | solution.py:21
  349.1 2.0 collective-permute-start.16
  351.1 0.7 fusion.4
  351.9 3.5 collective-permute-start.15
  355.5 1.5 collective-permute-start.18
  356.9 18.8 %collective-permute-done.15 = f32[4,8,32,128]{3,2,1,0:T(8,128)S(1)} collective-permute-done((f32[4,8,32,128]{3,2,1,0:T(8,128)S(1)}, f32[4,8,32,128]{3,2,1,0:T(8,128)S(1)}, u32[]{:S(2)}, u32[]{:S(2)}) %collective-permute-start.15) | collective-permute-done | bytes 524320 | tf_op jit(solution)/shard_map/ppermute | solution.py:21
  375.7 0.3 fusion.9
  376.1 0.5 collective-permute-start.17
  376.6 2.6 collective-permute-start.24
  379.2 4.4 %collective-permute-done.24 = f32[1,8,32]{2,1,0:T(8,128)S(1)} collective-permute-done((f32[1,8,32]{2,1,0:T(8,128)S(1)}, f32[1,8,32]{2,1,0:T(8,128)S(1)}, u32[]{:S(2)}, u32[]{:S(2)}) %collective-permute-start.24) | collective-permute-done | bytes 1056 | tf_op jit(solution)/shard_map/ppermute | solution.py:21
  383.9 1.1 collective-permute-start.19
  384.9 5.5 %collective-permute-done.19 = f32[1,8,32,128]{3,2,1,0:T(8,128)S(1)} collective-permute-done((f32[1,8,32,128]{3,2,1,0:T(8,128)S(1)}, f32[1,8,32,128]{3,2,1,0:T(8,128)S(1)}, u32[]{:S(2)}, u32[]{:S(2)}) %collective-permute-start.19) | collective-permute-done | bytes 131104 | tf_op jit(solution)/shard_map/ppermute | solution.py:21
  390.6 0.7 fusion.24
  (108 shorter events, 5.5 us)
Async XLA Ops:
  0.6 2.5 copy-start
  15.5 11.6 %copy-start.4 = (bf16[256,1024]{1,0:T(8,128)(2,1)S(1)}, bf16[256,1024]{1,0:T(8,128)(2,1)}, u32[]{:S(2)}) copy-start(bf16[256,1024]{1,0:T(8,128)(2,1)} %param.13) | copy-start | bytes 1572868
  15.6 11.6 %copy-start.6 = (bf16[1,256,256]{2,1,0:T(8,128)(2,1)S(1)}, bf16[1,256,256]{2,1,0:T(8,128)(2,1)}, u32[]{:S(2)}) copy-start(bf16[1,256,256]{2,1,0:T(8,128)(2,1)} %param.12) | copy-start | bytes 393220
  15.6 257.8 %all-to-all-start = ((bf16[8,4,128,1024]{3,2,1,0:T(8,128)(2,1)}), bf16[8,4,128,1024]{3,2,1,0:T(8,128)(2,1)}, u32[]{:S(2)}, u32[]{:S(2)}) async-start(bf16[8,4,128,1024]{3,2,1,0:T(8,128)(2,1)} %select_select_fusion), calls=%async_computation | async-start | bytes 16777216 | tf_op jit(solution)/shard_map/all_to_all | solution.py:140
  27.1 0.8 copy-start.7
  27.1 1.0 copy-start.10
  27.1 1.6 copy-start.8
  27.2 1.7 copy-start.9
  27.6 186.6 %collective-permute-start = (f32[16,8,1024]{2,1,0:T(8,128)S(1)}, f32[16,8,1024]{2,1,0:T(8,128)S(1)}, u32[]{:S(2)}, u32[]{:S(2)}) collective-permute-start(f32[16,8,1024]{2,1,0:T(8,128)S(1)} %select_bitcast_fusion.3), channel_id=1, source_target_pairs={{0,1},{1,0},{2,3},{3,2},{4,5},{5,4},{6,7},{7,6},{8,9},{9,8},{10,11... | collective-permute-start | bytes 1572872 | tf_op jit(solution)/shard_map/ppermute | solution.py:21
  28.0 6.4 %collective-permute-start.5 = (bf16[8,4096]{1,0:T(8,128)(2,1)S(1)}, bf16[8,4096]{1,0:T(8,128)(2,1)S(1)}, u32[]{:S(2)}, u32[]{:S(2)}) collective-permute-start(bf16[8,4096]{1,0:T(8,128)(2,1)S(1)} %bitcast.455), channel_id=1, source_target_pairs={{0,1},{1,0},{2,3},{3,2},{4,5},{5,4},{6,7},{7,6},{8,9},{9,8},{10,11... | collective-permute-start | bytes 196616 | tf_op jit(solution)/shard_map/ppermute | solution.py:21
  34.4 179.1 %collective-permute-start.6 = (bf16[16,4096]{1,0:T(8,128)(2,1)S(1)}, bf16[16,4096]{1,0:T(8,128)(2,1)S(1)}, u32[]{:S(2)}, u32[]{:S(2)}) collective-permute-start(bf16[16,4096]{1,0:T(8,128)(2,1)S(1)} %maximum_select_fusion.4), channel_id=1, source_target_pairs={{0,2},{1,3},{2,0},{3,1},{4,6},{5,7},{6,4},{7,5},{8,10},{9,11},{10,... | collective-permute-start | bytes 393224 | tf_op jit(solution)/shard_map/ppermute | solution.py:21
  213.5 13.9 %collective-permute-start.7 = (bf16[32,4096]{1,0:T(8,128)(2,1)S(1)}, bf16[32,4096]{1,0:T(8,128)(2,1)S(1)}, u32[]{:S(2)}, u32[]{:S(2)}) collective-permute-start(bf16[32,4096]{1,0:T(8,128)(2,1)S(1)} %maximum_select_fusion.3), channel_id=1, source_target_pairs={{0,4},{1,5},{2,6},{3,7},{4,0},{5,1},{6,2},{7,3},{8,12},{9,13},{10,... | collective-permute-start | bytes 786440 | tf_op jit(solution)/shard_map/ppermute | solution.py:21
  214.3 15.1 %collective-permute-start.1 = (f32[8,8,1024]{2,1,0:T(8,128)S(1)}, f32[8,8,1024]{2,1,0:T(8,128)S(1)}, u32[]{:S(2)}, u32[]{:S(2)}) collective-permute-start(f32[8,8,1024]{2,1,0:T(8,128)S(1)} %select_bitcast_fusion.6), channel_id=1, source_target_pairs={{0,2},{1,3},{2,0},{3,1},{4,6},{5,7},{6,4},{7,5},{8,10},{9,11},{10,... | collective-permute-start | bytes 786440 | tf_op jit(solution)/shard_map/ppermute | solution.py:21
  227.6 13.9 %collective-permute-start.8 = (bf16[64,4096]{1,0:T(8,128)(2,1)S(1)}, bf16[64,4096]{1,0:T(8,128)(2,1)S(1)}, u32[]{:S(2)}, u32[]{:S(2)}) collective-permute-start(bf16[64,4096]{1,0:T(8,128)(2,1)S(1)} %maximum_select_fusion.2), channel_id=1, source_target_pairs={{0,8},{1,9},{2,10},{3,11},{4,12},{5,13},{6,14},{7,15},{8,0},{9,1},... | collective-permute-start | bytes 1572872 | tf_op jit(solution)/shard_map/ppermute | solution.py:21
  229.5 14.9 %collective-permute-start.2 = (f32[4,8,1024]{2,1,0:T(8,128)S(1)}, f32[4,8,1024]{2,1,0:T(8,128)S(1)}, u32[]{:S(2)}, u32[]{:S(2)}) collective-permute-start(f32[4,8,1024]{2,1,0:T(8,128)S(1)} %select_bitcast_fusion.8), channel_id=1, source_target_pairs={{0,4},{1,5},{2,6},{3,7},{4,0},{5,1},{6,2},{7,3},{8,12},{9,13},{10,... | collective-permute-start | bytes 393224 | tf_op jit(solution)/shard_map/ppermute | solution.py:21
  241.6 29.8 %collective-permute-start.9 = (bf16[128,4096]{1,0:T(8,128)(2,1)S(1)}, bf16[128,4096]{1,0:T(8,128)(2,1)S(1)}, u32[]{:S(2)}, u32[]{:S(2)}) collective-permute-start(bf16[128,4096]{1,0:T(8,128)(2,1)S(1)} %maximum_select_fusion.1), channel_id=1, source_target_pairs={{0,16},{1,17},{2,18},{3,19},{4,20},{5,21},{6,22},{7,23},{8,24},{9,... | collective-permute-start | bytes 3145736 | tf_op jit(solution)/shard_map/ppermute | solution.py:21
  244.5 24.5 %collective-permute-start.3 = (f32[2,8,1024]{2,1,0:T(8,128)S(1)}, f32[2,8,1024]{2,1,0:T(8,128)S(1)}, u32[]{:S(2)}, u32[]{:S(2)}) collective-permute-start(f32[2,8,1024]{2,1,0:T(8,128)S(1)} %select_bitcast_fusion.9), channel_id=1, source_target_pairs={{0,8},{1,9},{2,10},{3,11},{4,12},{5,13},{6,14},{7,15},{8,0},{9,1},... | collective-permute-start | bytes 196616 | tf_op jit(solution)/shard_map/ppermute | solution.py:21
  269.0 9.7 %collective-permute-start.4 = (f32[1,8,1024]{2,1,0:T(8,128)S(1)}, f32[1,8,1024]{2,1,0:T(8,128)S(1)}, u32[]{:S(2)}, u32[]{:S(2)}) collective-permute-start(f32[1,8,1024]{2,1,0:T(8,128)S(1)} %select_bitcast_fusion.12), channel_id=1, source_target_pairs={{0,16},{1,17},{2,18},{3,19},{4,20},{5,21},{6,22},{7,23},{8,24},{9,... | collective-permute-start | bytes 98312 | tf_op jit(solution)/shard_map/ppermute | solution.py:21
  281.2 2.0 copy-start.3
  307.3 2.1 copy-start.2
  307.3 2.1 copy-start.5
  309.4 12.4 %collective-permute-start.11 = (f32[16,8,32,128]{3,2,1,0:T(8,128)}, f32[16,8,32,128]{3,2,1,0:T(8,128)}, u32[]{:S(2)}, u32[]{:S(2)}) collective-permute-start(f32[16,8,32,128]{3,2,1,0:T(8,128)} %select_bitcast_fusion), channel_id=1, source_target_pairs={{0,1},{1,0},{2,3},{3,2},{4,5},{5,4},{6,7},{7,6},{8,9},{9,8},{10,11... | collective-permute-start | bytes 6291464 | tf_op jit(solution)/shard_map/ppermute | solution.py:21
  310.9 3.4 collective-permute-start.20
  314.0 1.6 collective-permute-start.10
  317.1 4.3 %collective-permute-start.21 = (f32[8,8,32]{2,1,0:T(8,128)S(1)}, f32[8,8,32]{2,1,0:T(8,128)S(1)}, u32[]{:S(2)}, u32[]{:S(2)}) collective-permute-start(f32[8,8,32]{2,1,0:T(8,128)S(1)} %select_bitcast_fusion.10), channel_id=1, source_target_pairs={{0,2},{1,3},{2,0},{3,1},{4,6},{5,7},{6,4},{7,5},{8,10},{9,11},{10,... | collective-permute-start | bytes 24584 | tf_op jit(solution)/shard_map/ppermute | solution.py:21
  317.8 4.0 %collective-permute-start.12 = (f32[8,8,32]{2,1,0:T(8,128)S(1)}, f32[8,8,32]{2,1,0:T(8,128)S(1)}, u32[]{:S(2)}, u32[]{:S(2)}) collective-permute-start(f32[8,8,32]{2,1,0:T(8,128)S(1)} %select_bitcast_fusion.11), channel_id=1, source_target_pairs={{0,2},{1,3},{2,0},{3,1},{4,6},{5,7},{6,4},{7,5},{8,10},{9,11},{10,... | collective-permute-start | bytes 24584 | tf_op jit(solution)/shard_map/ppermute | solution.py:21
  324.9 26.2 %collective-permute-start.13 = (f32[8,8,32,128]{3,2,1,0:T(8,128)S(1)}, f32[8,8,32,128]{3,2,1,0:T(8,128)S(1)}, u32[]{:S(2)}, u32[]{:S(2)}) collective-permute-start(f32[8,8,32,128]{3,2,1,0:T(8,128)S(1)} %select_bitcast_fusion.1), channel_id=1, source_target_pairs={{0,2},{1,3},{2,0},{3,1},{4,6},{5,7},{6,4},{7,5},{8,10},{9,11},{10,... | collective-permute-start | bytes 3145736 | tf_op jit(solution)/shard_map/ppermute | solution.py:21
  327.0 21.8 %collective-permute-start.22 = (f32[4,8,32]{2,1,0:T(8,128)S(1)}, f32[4,8,32]{2,1,0:T(8,128)S(1)}, u32[]{:S(2)}, u32[]{:S(2)}) collective-permute-start(f32[4,8,32]{2,1,0:T(8,128)S(1)} %select_bitcast_fusion.13), channel_id=1, source_target_pairs={{0,4},{1,5},{2,6},{3,7},{4,0},{5,1},{6,2},{7,3},{8,12},{9,13},{10,... | collective-permute-start | bytes 12296 | tf_op jit(solution)/shard_map/ppermute | solution.py:21
  328.2 20.8 %collective-permute-start.14 = (f32[4,8,32]{2,1,0:T(8,128)S(1)}, f32[4,8,32]{2,1,0:T(8,128)S(1)}, u32[]{:S(2)}, u32[]{:S(2)}) collective-permute-start(f32[4,8,32]{2,1,0:T(8,128)S(1)} %select_bitcast_fusion.14), channel_id=1, source_target_pairs={{0,4},{1,5},{2,6},{3,7},{4,0},{5,1},{6,2},{7,3},{8,12},{9,13},{10,... | collective-permute-start | bytes 12296 | tf_op jit(solution)/shard_map/ppermute | solution.py:21
  349.0 6.4 %collective-permute-start.23 = (f32[2,8,32]{2,1,0:T(8,128)S(1)}, f32[2,8,32]{2,1,0:T(8,128)S(1)}, u32[]{:S(2)}, u32[]{:S(2)}) collective-permute-start(f32[2,8,32]{2,1,0:T(8,128)S(1)} %select_bitcast_fusion.15), channel_id=1, source_target_pairs={{0,8},{1,9},{2,10},{3,11},{4,12},{5,13},{6,14},{7,15},{8,0},{9,1},... | collective-permute-start | bytes 6152 | tf_op jit(solution)/shard_map/ppermute | solution.py:21
  349.1 6.3 %collective-permute-start.16 = (f32[2,8,32]{2,1,0:T(8,128)S(1)}, f32[2,8,32]{2,1,0:T(8,128)S(1)}, u32[]{:S(2)}, u32[]{:S(2)}) collective-permute-start(f32[2,8,32]{2,1,0:T(8,128)S(1)} %select_bitcast_fusion.16), channel_id=1, source_target_pairs={{0,8},{1,9},{2,10},{3,11},{4,12},{5,13},{6,14},{7,15},{8,0},{9,1},... | collective-permute-start | bytes 6152 | tf_op jit(solution)/shard_map/ppermute | solution.py:21
  351.9 23.8 %collective-permute-start.15 = (f32[4,8,32,128]{3,2,1,0:T(8,128)S(1)}, f32[4,8,32,128]{3,2,1,0:T(8,128)S(1)}, u32[]{:S(2)}, u32[]{:S(2)}) collective-permute-start(f32[4,8,32,128]{3,2,1,0:T(8,128)S(1)} %select_bitcast_fusion.2), channel_id=1, source_target_pairs={{0,4},{1,5},{2,6},{3,7},{4,0},{5,1},{6,2},{7,3},{8,12},{9,13},{10,... | collective-permute-start | bytes 1572872 | tf_op jit(solution)/shard_map/ppermute | solution.py:21
  355.5 23.7 %collective-permute-start.18 = (f32[1,8,32]{2,1,0:T(8,128)S(1)}, f32[1,8,32]{2,1,0:T(8,128)S(1)}, u32[]{:S(2)}, u32[]{:S(2)}) collective-permute-start(f32[1,8,32]{2,1,0:T(8,128)S(1)} %select_bitcast_fusion.18), channel_id=1, source_target_pairs={{0,16},{1,17},{2,18},{3,19},{4,20},{5,21},{6,22},{7,23},{8,24},{9,... | collective-permute-start | bytes 3080 | tf_op jit(solution)/shard_map/ppermute | solution.py:21
  375.7 15.6 %copy-start.1 = (bf16[8,128,1024]{2,1,0:T(8,128)(2,1)S(1)}, bf16[8,128,1024]{2,1,0:T(8,128)(2,1)}, u32[]{:S(2)}) copy-start(bf16[8,128,1024]{2,1,0:T(8,128)(2,1)} %param.8) | copy-start | bytes 6291460
  376.1 7.5 %collective-permute-start.17 = (f32[2,8,32,128]{3,2,1,0:T(8,128)S(1)}, f32[2,8,32,128]{3,2,1,0:T(8,128)S(1)}, u32[]{:S(2)}, u32[]{:S(2)}) collective-permute-start(f32[2,8,32,128]{3,2,1,0:T(8,128)S(1)} %select_bitcast_fusion.5), channel_id=1, source_target_pairs={{0,8},{1,9},{2,10},{3,11},{4,12},{5,13},{6,14},{7,15},{8,0},{9,1},... | collective-permute-start | bytes 786440 | tf_op jit(solution)/shard_map/ppermute | solution.py:21
  376.6 6.9 %collective-permute-start.24 = (f32[1,8,32]{2,1,0:T(8,128)S(1)}, f32[1,8,32]{2,1,0:T(8,128)S(1)}, u32[]{:S(2)}, u32[]{:S(2)}) collective-permute-start(f32[1,8,32]{2,1,0:T(8,128)S(1)} %select_bitcast_fusion.17), channel_id=1, source_target_pairs={{0,16},{1,17},{2,18},{3,19},{4,20},{5,21},{6,22},{7,23},{8,24},{9,... | collective-permute-start | bytes 3080 | tf_op jit(solution)/shard_map/ppermute | solution.py:21
  383.9 6.6 %collective-permute-start.19 = (f32[1,8,32,128]{3,2,1,0:T(8,128)S(1)}, f32[1,8,32,128]{3,2,1,0:T(8,128)S(1)}, u32[]{:S(2)}, u32[]{:S(2)}) collective-permute-start(f32[1,8,32,128]{3,2,1,0:T(8,128)S(1)} %select_bitcast_fusion.7), channel_id=1, source_target_pairs={{0,16},{1,17},{2,18},{3,19},{4,20},{5,21},{6,22},{7,23},{8,24},{9,... | collective-permute-start | bytes 393224 | tf_op jit(solution)/shard_map/ppermute | solution.py:21

commit v5 on v4

--- a/solution.py
+++ b/solution.py
@@ -35,7 +35,7 @@
     return held
 
 
-def scatter_rows(parts, my_ctx, merge):
+def scatter_rows(parts, my_ctx, merge, narrow=lambda t: t, widen=lambda t: t):
     peers = lax.axis_size("ctx")
     held = parts
     bit = 1
@@ -44,7 +44,7 @@
         upper = (my_ctx // bit) % 2 == 1
         keep = jax.tree.map(lambda a: jnp.where(upper, a[:, 1], a[:, 0]), half)
         send = jax.tree.map(lambda a: jnp.where(upper, a[:, 0], a[:, 1]), half)
-        held = merge(keep, exchange(send, bit))
+        held = merge(keep, widen(exchange(narrow(send), bit)))
         bit *= 2
     return jax.tree.map(lambda a: a[0], held)
 
@@ -192,6 +192,8 @@
         ),
         my_ctx,
         merge_softmax,
+        lambda t: (t[0].astype(jnp.bfloat16),) + t[1:],
+        lambda t: (t[0].astype(jnp.float32),) + t[1:],
     )
     result = numerator / totals[:, :, None]
     attended = result.reshape(RCP, QH * HD).astype(jnp.bfloat16)

time: 393 us -> 376 us (0.957)
  waiting for transfers between devices: 274 us -> 246 us
  other arithmetic: 26.4 us -> 30.9 us
    ppermute x25, waiting for transfers between devices: 274 us -> 246 us  [exchange(): return lax.ppermute(shard, 'ctx', [(i, i ^ bit) for i in range(peers)])]
  transfers between devices with their start and end apart: 26 -> 26, of which waited for: 13 -> 11; matrix products, arithmetic and copies ran while one was open for 6% -> 8% of each run, Pallas kernels for 0% -> 0%
where the time goes in v5:
time: 376 us; the launch traced here: 374 us
  waiting for transfers between devices  246 us (65%)
  starting transfers between devices  45.4 us (12%)
  other arithmetic  30.9 us (8%)
  local copies, waits for them, and re-layouts  25.7 us (7%)
  Pallas kernels  21.5 us (6%)
    ppermute x25, waiting for transfers between devices, exchange(): return lax.ppermute(shard, 'ctx', [(i, i ^ bit) for i in range(peers)])  246 us
    ppermute x25, starting transfers between devices, exchange(): return lax.ppermute(shard, 'ctx', [(i, i ^ bit) for i in range(peers)])  33.7 us
    pallas_call x1, Pallas kernels, attend_local(): pl.pallas_call(attend_kernel, grid=(KVH,), in_specs=[pl.BlockSpec((rows,...  21.5 us
    all_to_all x1, starting transfers between devices, on_device(): lax.all_to_all(outgoing, 'owner', split_axis=0, concat_axis=0, tiled=True)  11.7 us
    select_n x1, other arithmetic, on_device(): jnp.where(filled[:, :, None, None], jnp.take(span_cache, chosen, axis=0),...  7.64 us
  transfers between devices with their start and end apart: 26, of which 11 were waited for; matrix products, arithmetic and copies ran while one was open for 8% of the time, Pallas kernels for 0%

profile of v5, /device:TPU:6, one launch (start us, length us, event | category | flops | bytes accessed | tf_op | source)
XLA Modules:
  0.0 374.0 jit_solution(9198862984064596730)
XLA Ops:
  0.7 0.9 fusion.75
  1.7 0.7 add_select_fusion.1
  3.1 4.7 %gather_fusion = bf16[32,128,1024]{2,1,0:T(8,128)(2,1)} fusion(bf16[8,128,1024]{2,1,0:T(8,128)(2,1)S(1)} %copy-done, s32[1024]{0:T(1024)S(1)} %pad_clamp_fusion.2), kind=kCustom, calls=%fused_computation | custom fusion | bytes 16777344 | tf_op jit(solution)/shard_map/jit(_take)/gather | solution.py:138
  7.9 7.6 %select_select_fusion = bf16[8,4,128,1024]{3,2,1,0:T(8,128)(2,1)} fusion(bf16[8,4,128,1024]{3,2,1,0:T(8,128)(2,1)} %bitcast.424, pred[8,4]{1,0:T(8,128)(4,1)S(1)} %copy.240, pred[8,4]{1,0:T(8,128)(4,1)S(1)} %copy.239), kind=kLoop, calls=%fused_computation.3 | loop fusion | flops 8388608 | bytes 16777280 | tf_op jit(solution)/shard_map/jit(_where)/select_n | solution.py:137
  15.5 11.7 %all-to-all-start = ((bf16[8,4,128,1024]{3,2,1,0:T(8,128)(2,1)}), bf16[8,4,128,1024]{3,2,1,0:T(8,128)(2,1)}, u32[]{:S(2)}, u32[]{:S(2)}) async-start(bf16[8,4,128,1024]{3,2,1,0:T(8,128)(2,1)} %select_select_fusion), calls=%async_computation | async-start | bytes 16777216 | tf_op jit(solution)/shard_map/all_to_all | solution.py:140
  28.2 0.6 dynamic_slice.12
  29.0 0.7 gather_fusion.2
  29.7 0.7 fusion.69
  30.4 0.7 and_select_fusion.5
  31.1 0.7 broadcast_compare_fusion
  31.8 0.7 fusion.55
  33.0 1.3 fusion.7.mask_ref
  34.5 1.1 collective-permute-start.6
  35.6 0.7 fusion.68
  36.4 177.2 %collective-permute-done.6 = bf16[16,4096]{1,0:T(8,128)(2,1)S(1)} collective-permute-done((bf16[16,4096]{1,0:T(8,128)(2,1)S(1)}, bf16[16,4096]{1,0:T(8,128)(2,1)S(1)}, u32[]{:S(2)}, u32[]{:S(2)}) %collective-permute-start.6) | collective-permute-done | bytes 131104 | tf_op jit(solution)/shard_map/ppermute | solution.py:21
  213.6 1.1 collective-permute-start.7
  214.9 2.6 collective-permute-start.1
  217.5 10.3 %collective-permute-done.7 = bf16[32,4096]{1,0:T(8,128)(2,1)S(1)} collective-permute-done((bf16[32,4096]{1,0:T(8,128)(2,1)S(1)}, bf16[32,4096]{1,0:T(8,128)(2,1)S(1)}, u32[]{:S(2)}, u32[]{:S(2)}) %collective-permute-start.7) | collective-permute-done | bytes 262176 | tf_op jit(solution)/shard_map/ppermute | solution.py:21
  227.8 2.2 collective-permute-start.8
  230.3 11.8 %collective-permute-done.8 = bf16[64,4096]{1,0:T(8,128)(2,1)S(1)} collective-permute-done((bf16[64,4096]{1,0:T(8,128)(2,1)S(1)}, bf16[64,4096]{1,0:T(8,128)(2,1)S(1)}, u32[]{:S(2)}, u32[]{:S(2)}) %collective-permute-start.8) | collective-permute-done | bytes 524320 | tf_op jit(solution)/shard_map/ppermute | solution.py:21
  242.3 2.7 collective-permute-start.9
  245.3 22.8 %collective-permute-done.3 = f32[2,8,1024]{2,1,0:T(8,128)S(1)} collective-permute-done((f32[2,8,1024]{2,1,0:T(8,128)S(1)}, f32[2,8,1024]{2,1,0:T(8,128)S(1)}, u32[]{:S(2)}, u32[]{:S(2)}) %collective-permute-start.3) | collective-permute-done | bytes 65568 | tf_op jit(solution)/shard_map/ppermute | solution.py:21
  268.1 4.0 %collective-permute-start.4 = (f32[1,8,1024]{2,1,0:T(8,128)S(1)}, f32[1,8,1024]{2,1,0:T(8,128)S(1)}, u32[]{:S(2)}, u32[]{:S(2)}) collective-permute-start(f32[1,8,1024]{2,1,0:T(8,128)S(1)} %select_bitcast_fusion.7), channel_id=1, source_target_pairs={{0,16},{1,17},{2,18},{3,19},{4,20},{5,21},{6,22},{7,23},{8,24},{9,... | collective-permute-start | bytes 98312 | tf_op jit(solution)/shard_map/ppermute | solution.py:21
  272.1 1.9 maximum_select_fusion.query_ref
  274.0 5.4 %gather_fusion.1 = bf16[8,128,1024]{2,1,0:T(8,128)(2,1)} fusion(bf16[32,128,1024]{2,1,0:T(8,128)(2,1)} %bitcast.35, s32[1024]{0:T(1024)S(1)} %pad_clamp_fusion.1), kind=kCustom, calls=%fused_computation.1 | custom fusion | bytes 4194336 | tf_op jit(solution)/shard_map/jit(_take)/gather | solution.py:152
  279.4 2.5 fusion.1
  281.9 1.7 fusion.77
  283.9 21.5 %shard_map.95 = (f32[256,4096]{1,0:T(8,128)}, f32[4,256,8]{2,1,0:T(8,128)}, f32[4,256,8]{2,1,0:T(8,128)}) custom-call(bf16[256,4096]{1,0:T(8,128)(2,1)} %maximum_select_fusion.query_ref, bf16[1024,512]{1,0:T(8,128)(2,1)} %get-tuple-element.33.key_ref, bf16[1024,512]{1,0:T(8,128)(2,1)} %get-tuple-element.32.value_ref, f32[256,1024]{1,0:T(8,128)} %fusion.7.mask_ref), custom_call_target="tpu_custom_call" | custom-call | flops 4294967296 | bytes 9437184 | tf_op jit(solution)/shard_map/pallas_call | solution.py:94
  305.4 1.3 copy.274
  306.7 0.8 reshape_reshape_reshape.11
  307.5 0.4 fusion.78
  308.2 0.8 reshape_reshape_reshape.10
  309.1 0.5 broadcast_select_fusion
  309.5 0.6 collective-permute-start.10
  310.1 4.1 %fusion.76 = (f32[16,1,8,32,128]{4,2,3,1,0:T(8,128)S(1)}, f32[16,1,8,32,128]{4,2,3,1,0:T(8,128)}) fusion(f32[16,2,8,32,128]{4,2,3,1,0:T(8,128)} %bitcast.432), kind=kLoop, calls=%fused_computation.205 | loop fusion | bytes 8388608 | tf_op jit(solution)/shard_map/slice | solution.py:45
  314.2 0.7 copy-done.7
  314.9 1.8 fusion.23
  317.1 0.6 select_bitcast_fusion.5
  318.1 2.1 collective-permute-start.12
  320.2 2.2 fusion.2
  322.8 1.4 fusion.34
  324.2 0.6 copy-done.5
  324.8 0.6 select_bitcast_fusion.8
  325.4 1.2 collective-permute-start.22
  326.6 0.6 select_bitcast_fusion.9
  327.2 1.7 collective-permute-start.14
  328.9 1.1 copy.251
  330.3 1.9 collective-permute-done.14
  332.2 0.8 fusion.41
  333.3 2.6 fusion
  336.0 0.8 collective-permute-start.13
  336.9 1.9 collective-permute-start.16
  338.7 1.8 collective-permute-done.16
  340.5 7.5 %collective-permute-done.13 = bf16[8,8,32,128]{3,2,1,0:T(8,128)(2,1)S(1)} collective-permute-done((bf16[8,8,32,128]{3,2,1,0:T(8,128)(2,1)S(1)}, bf16[8,8,32,128]{3,2,1,0:T(8,128)(2,1)S(1)}, u32[]{:S(2)}, u32[]{:S(2)}) %collective-permute-start.13) | collective-permute-done | bytes 524320 | tf_op jit(solution)/shard_map/ppermute | solution.py:21
  348.1 0.7 fusion.5
  348.8 2.6 collective-permute-start.15
  351.4 2.7 collective-permute-start.18
  354.1 0.9 collective-permute-start.24
  355.0 6.7 %collective-permute-done.15 = bf16[4,8,32,128]{3,2,1,0:T(8,128)(2,1)S(1)} collective-permute-done((bf16[4,8,32,128]{3,2,1,0:T(8,128)(2,1)S(1)}, bf16[4,8,32,128]{3,2,1,0:T(8,128)(2,1)S(1)}, u32[]{:S(2)}, u32[]{:S(2)}) %collective-permute-start.15) | collective-permute-done | bytes 262176 | tf_op jit(solution)/shard_map/ppermute | solution.py:21
  362.0 1.5 collective-permute-start.17
  363.5 3.5 collective-permute-done.17
  367.3 2.9 collective-permute-start.19
  370.3 2.9 collective-permute-done.19
  373.3 0.7 fusion.28
  (116 shorter events, 7.0 us)
Async XLA Ops:
  0.6 2.5 copy-start
  15.5 11.7 %copy-start.3 = (bf16[256,1024]{1,0:T(8,128)(2,1)S(1)}, bf16[256,1024]{1,0:T(8,128)(2,1)}, u32[]{:S(2)}) copy-start(bf16[256,1024]{1,0:T(8,128)(2,1)} %param.13) | copy-start | bytes 1572868
  15.5 11.7 %copy-start.10 = (bf16[1,256,256]{2,1,0:T(8,128)(2,1)S(1)}, bf16[1,256,256]{2,1,0:T(8,128)(2,1)}, u32[]{:S(2)}) copy-start(bf16[1,256,256]{2,1,0:T(8,128)(2,1)} %param.12) | copy-start | bytes 393220
  15.5 258.5 %all-to-all-start = ((bf16[8,4,128,1024]{3,2,1,0:T(8,128)(2,1)}), bf16[8,4,128,1024]{3,2,1,0:T(8,128)(2,1)}, u32[]{:S(2)}, u32[]{:S(2)}) async-start(bf16[8,4,128,1024]{3,2,1,0:T(8,128)(2,1)} %select_select_fusion), calls=%async_computation | async-start | bytes 16777216 | tf_op jit(solution)/shard_map/all_to_all | solution.py:140
  27.2 0.8 copy-start.11
  27.2 1.0 copy-start.14
  27.2 1.6 copy-start.12
  27.2 1.7 copy-start.13
  27.6 187.1 %collective-permute-start = (f32[16,8,1024]{2,1,0:T(8,128)S(1)}, f32[16,8,1024]{2,1,0:T(8,128)S(1)}, u32[]{:S(2)}, u32[]{:S(2)}) collective-permute-start(f32[16,8,1024]{2,1,0:T(8,128)S(1)} %select_bitcast_fusion), channel_id=1, source_target_pairs={{0,1},{1,0},{2,3},{3,2},{4,5},{5,4},{6,7},{7,6},{8,9},{9,8},{10,11... | collective-permute-start | bytes 1572872 | tf_op jit(solution)/shard_map/ppermute | solution.py:21
  28.0 6.4 %collective-permute-start.5 = (bf16[8,4096]{1,0:T(8,128)(2,1)S(1)}, bf16[8,4096]{1,0:T(8,128)(2,1)S(1)}, u32[]{:S(2)}, u32[]{:S(2)}) collective-permute-start(bf16[8,4096]{1,0:T(8,128)(2,1)S(1)} %bitcast.461), channel_id=1, source_target_pairs={{0,1},{1,0},{2,3},{3,2},{4,5},{5,4},{6,7},{7,6},{8,9},{9,8},{10,11... | collective-permute-start | bytes 196616 | tf_op jit(solution)/shard_map/ppermute | solution.py:21
  34.5 179.1 %collective-permute-start.6 = (bf16[16,4096]{1,0:T(8,128)(2,1)S(1)}, bf16[16,4096]{1,0:T(8,128)(2,1)S(1)}, u32[]{:S(2)}, u32[]{:S(2)}) collective-permute-start(bf16[16,4096]{1,0:T(8,128)(2,1)S(1)} %maximum_select_fusion.4), channel_id=1, source_target_pairs={{0,2},{1,3},{2,0},{3,1},{4,6},{5,7},{6,4},{7,5},{8,10},{9,11},{10,... | collective-permute-start | bytes 393224 | tf_op jit(solution)/shard_map/ppermute | solution.py:21
  213.6 14.1 %collective-permute-start.7 = (bf16[32,4096]{1,0:T(8,128)(2,1)S(1)}, bf16[32,4096]{1,0:T(8,128)(2,1)S(1)}, u32[]{:S(2)}, u32[]{:S(2)}) collective-permute-start(bf16[32,4096]{1,0:T(8,128)(2,1)S(1)} %maximum_select_fusion.3), channel_id=1, source_target_pairs={{0,4},{1,5},{2,6},{3,7},{4,0},{5,1},{6,2},{7,3},{8,12},{9,13},{10,... | collective-permute-start | bytes 786440 | tf_op jit(solution)/shard_map/ppermute | solution.py:21
  214.9 15.2 %collective-permute-start.1 = (f32[8,8,1024]{2,1,0:T(8,128)S(1)}, f32[8,8,1024]{2,1,0:T(8,128)S(1)}, u32[]{:S(2)}, u32[]{:S(2)}) collective-permute-start(f32[8,8,1024]{2,1,0:T(8,128)S(1)} %select_bitcast_fusion.2), channel_id=1, source_target_pairs={{0,2},{1,3},{2,0},{3,1},{4,6},{5,7},{6,4},{7,5},{8,10},{9,11},{10,... | collective-permute-start | bytes 786440 | tf_op jit(solution)/shard_map/ppermute | solution.py:21
  227.8 14.3 %collective-permute-start.8 = (bf16[64,4096]{1,0:T(8,128)(2,1)S(1)}, bf16[64,4096]{1,0:T(8,128)(2,1)S(1)}, u32[]{:S(2)}, u32[]{:S(2)}) collective-permute-start(bf16[64,4096]{1,0:T(8,128)(2,1)S(1)} %maximum_select_fusion.2), channel_id=1, source_target_pairs={{0,8},{1,9},{2,10},{3,11},{4,12},{5,13},{6,14},{7,15},{8,0},{9,1},... | collective-permute-start | bytes 1572872 | tf_op jit(solution)/shard_map/ppermute | solution.py:21
  230.2 14.9 %collective-permute-start.2 = (f32[4,8,1024]{2,1,0:T(8,128)S(1)}, f32[4,8,1024]{2,1,0:T(8,128)S(1)}, u32[]{:S(2)}, u32[]{:S(2)}) collective-permute-start(f32[4,8,1024]{2,1,0:T(8,128)S(1)} %select_bitcast_fusion.3), channel_id=1, source_target_pairs={{0,4},{1,5},{2,6},{3,7},{4,0},{5,1},{6,2},{7,3},{8,12},{9,13},{10,... | collective-permute-start | bytes 393224 | tf_op jit(solution)/shard_map/ppermute | solution.py:21
  242.3 29.8 %collective-permute-start.9 = (bf16[128,4096]{1,0:T(8,128)(2,1)S(1)}, bf16[128,4096]{1,0:T(8,128)(2,1)S(1)}, u32[]{:S(2)}, u32[]{:S(2)}) collective-permute-start(bf16[128,4096]{1,0:T(8,128)(2,1)S(1)} %maximum_select_fusion.1), channel_id=1, source_target_pairs={{0,16},{1,17},{2,18},{3,19},{4,20},{5,21},{6,22},{7,23},{8,24},{9,... | collective-permute-start | bytes 3145736 | tf_op jit(solution)/shard_map/ppermute | solution.py:21
  245.2 22.9 %collective-permute-start.3 = (f32[2,8,1024]{2,1,0:T(8,128)S(1)}, f32[2,8,1024]{2,1,0:T(8,128)S(1)}, u32[]{:S(2)}, u32[]{:S(2)}) collective-permute-start(f32[2,8,1024]{2,1,0:T(8,128)S(1)} %select_bitcast_fusion.4), channel_id=1, source_target_pairs={{0,8},{1,9},{2,10},{3,11},{4,12},{5,13},{6,14},{7,15},{8,0},{9,1},... | collective-permute-start | bytes 196616 | tf_op jit(solution)/shard_map/ppermute | solution.py:21
  268.1 11.3 %collective-permute-start.4 = (f32[1,8,1024]{2,1,0:T(8,128)S(1)}, f32[1,8,1024]{2,1,0:T(8,128)S(1)}, u32[]{:S(2)}, u32[]{:S(2)}) collective-permute-start(f32[1,8,1024]{2,1,0:T(8,128)S(1)} %select_bitcast_fusion.7), channel_id=1, source_target_pairs={{0,16},{1,17},{2,18},{3,19},{4,20},{5,21},{6,22},{7,23},{8,24},{9,... | collective-permute-start | bytes 98312 | tf_op jit(solution)/shard_map/ppermute | solution.py:21
  281.9 2.0 copy-start.2
  305.4 2.6 copy-start.4
  308.0 6.2 %collective-permute-start.20 = (f32[16,8,32]{1,0,2:T(8,128)S(1)}, f32[16,8,32]{1,0,2:T(8,128)S(1)}, u32[]{:S(2)}, u32[]{:S(2)}) collective-permute-start(f32[16,8,32]{1,0,2:T(8,128)S(1)} %select_bitcast_fusion.1), channel_id=1, source_target_pairs={{0,1},{1,0},{2,3},{3,2},{4,5},{5,4},{6,7},{7,6},{8,9},{9,8},{10,11... | collective-permute-start | bytes 49160 | tf_op jit(solution)/shard_map/ppermute | solution.py:21
  309.5 4.6 %collective-permute-start.10 = (f32[16,8,32]{1,0,2:T(8,128)S(1)}, f32[16,8,32]{1,0,2:T(8,128)S(1)}, u32[]{:S(2)}, u32[]{:S(2)}) collective-permute-start(f32[16,8,32]{1,0,2:T(8,128)S(1)} %bitcast.455), channel_id=1, source_target_pairs={{0,1},{1,0},{2,3},{3,2},{4,5},{5,4},{6,7},{7,6},{8,9},{9,8},{10,11... | collective-permute-start | bytes 49160 | tf_op jit(solution)/shard_map/ppermute | solution.py:21
  314.2 0.7 copy-start.7
  317.7 5.1 %collective-permute-start.21 = (f32[8,8,32]{2,1,0:T(8,128)}, f32[8,8,32]{2,1,0:T(8,128)}, u32[]{:S(2)}, u32[]{:S(2)}) collective-permute-start(f32[8,8,32]{2,1,0:T(8,128)} %select_bitcast_fusion.5), channel_id=1, source_target_pairs={{0,2},{1,3},{2,0},{3,1},{4,6},{5,7},{6,4},{7,5},{8,10},{9,11},{10,... | collective-permute-start | bytes 24584 | tf_op jit(solution)/shard_map/ppermute | solution.py:21
  318.1 4.6 %collective-permute-start.12 = (f32[8,8,32]{2,1,0:T(8,128)S(1)}, f32[8,8,32]{2,1,0:T(8,128)S(1)}, u32[]{:S(2)}, u32[]{:S(2)}) collective-permute-start(f32[8,8,32]{2,1,0:T(8,128)S(1)} %select_bitcast_fusion.6), channel_id=1, source_target_pairs={{0,2},{1,3},{2,0},{3,1},{4,6},{5,7},{6,4},{7,5},{8,10},{9,11},{10,... | collective-permute-start | bytes 24584 | tf_op jit(solution)/shard_map/ppermute | solution.py:21
  322.4 10.9 %collective-permute-start.11 = (bf16[16,8,32,128]{3,2,1,0:T(8,128)(2,1)S(1)}, bf16[16,8,32,128]{3,2,1,0:T(8,128)(2,1)}, u32[]{:S(2)}, u32[]{:S(2)}) collective-permute-start(bf16[16,8,32,128]{3,2,1,0:T(8,128)(2,1)S(1)} %fusion.2), channel_id=1, source_target_pairs={{0,1},{1,0},{2,3},{3,2},{4,5},{5,4},{6,7},{7,6},{8,9},{9,8},{10,11... | collective-permute-start | bytes 3145736 | tf_op jit(solution)/shard_map/ppermute | solution.py:21
  324.2 0.6 copy-start.5
  324.2 2.4 copy-start.6
  325.4 4.9 %collective-permute-start.22 = (f32[4,8,32]{2,1,0:T(8,128)}, f32[4,8,32]{2,1,0:T(8,128)S(1)}, u32[]{:S(2)}, u32[]{:S(2)}) collective-permute-start(f32[4,8,32]{2,1,0:T(8,128)} %select_bitcast_fusion.8), channel_id=1, source_target_pairs={{0,4},{1,5},{2,6},{3,7},{4,0},{5,1},{6,2},{7,3},{8,12},{9,13},{10,... | collective-permute-start | bytes 12296 | tf_op jit(solution)/shard_map/ppermute | solution.py:21
  327.2 5.0 %collective-permute-start.14 = (f32[4,8,32]{2,1,0:T(8,128)}, f32[4,8,32]{2,1,0:T(8,128)}, u32[]{:S(2)}, u32[]{:S(2)}) collective-permute-start(f32[4,8,32]{2,1,0:T(8,128)} %select_bitcast_fusion.9), channel_id=1, source_target_pairs={{0,4},{1,5},{2,6},{3,7},{4,0},{5,1},{6,2},{7,3},{8,12},{9,13},{10,... | collective-permute-start | bytes 12296 | tf_op jit(solution)/shard_map/ppermute | solution.py:21
  333.0 15.0 %copy-start.8 = (f32[8,8,32]{2,1,0:T(8,128)S(1)}, f32[8,8,32]{2,1,0:T(8,128)}, u32[]{:S(2)}) copy-start(f32[8,8,32]{2,1,0:T(8,128)} %get-tuple-element.19) | copy-start | bytes 24580
  333.0 15.0 %copy-start.9 = (f32[8,8,32]{2,1,0:T(8,128)S(1)}, f32[8,8,32]{2,1,0:T(8,128)}, u32[]{:S(2)}) copy-start(f32[8,8,32]{2,1,0:T(8,128)} %get-tuple-element.20) | copy-start | bytes 24580
  333.0 5.7 %collective-permute-start.23 = (f32[2,8,32]{2,1,0:T(8,128)S(1)}, f32[2,8,32]{2,1,0:T(8,128)S(1)}, u32[]{:S(2)}, u32[]{:S(2)}) collective-permute-start(f32[2,8,32]{2,1,0:T(8,128)S(1)} %select_bitcast_fusion.10), channel_id=1, source_target_pairs={{0,8},{1,9},{2,10},{3,11},{4,12},{5,13},{6,14},{7,15},{8,0},{9,1},... | collective-permute-start | bytes 6152 | tf_op jit(solution)/shard_map/ppermute | solution.py:21
  336.0 12.0 %collective-permute-start.13 = (bf16[8,8,32,128]{3,2,1,0:T(8,128)(2,1)S(1)}, bf16[8,8,32,128]{3,2,1,0:T(8,128)(2,1)S(1)}, u32[]{:S(2)}, u32[]{:S(2)}) collective-permute-start(bf16[8,8,32,128]{3,2,1,0:T(8,128)(2,1)S(1)} %fusion.8), channel_id=1, source_target_pairs={{0,2},{1,3},{2,0},{3,1},{4,6},{5,7},{6,4},{7,5},{8,10},{9,11},{10,... | collective-permute-start | bytes 1572872 | tf_op jit(solution)/shard_map/ppermute | solution.py:21
  336.9 3.7 collective-permute-start.16
  348.8 12.8 %collective-permute-start.15 = (bf16[4,8,32,128]{3,2,1,0:T(8,128)(2,1)S(1)}, bf16[4,8,32,128]{3,2,1,0:T(8,128)(2,1)S(1)}, u32[]{:S(2)}, u32[]{:S(2)}) collective-permute-start(bf16[4,8,32,128]{3,2,1,0:T(8,128)(2,1)S(1)} %fusion.16), channel_id=1, source_target_pairs={{0,4},{1,5},{2,6},{3,7},{4,0},{5,1},{6,2},{7,3},{8,12},{9,13},{10,... | collective-permute-start | bytes 786440 | tf_op jit(solution)/shard_map/ppermute | solution.py:21
  351.4 12.1 %collective-permute-start.18 = (f32[1,8,32]{2,1,0:T(8,128)S(1)}, f32[1,8,32]{2,1,0:T(8,128)S(1)}, u32[]{:S(2)}, u32[]{:S(2)}) collective-permute-start(f32[1,8,32]{2,1,0:T(8,128)S(1)} %select_bitcast_fusion.13), channel_id=1, source_target_pairs={{0,16},{1,17},{2,18},{3,19},{4,20},{5,21},{6,22},{7,23},{8,24},{9,... | collective-permute-start | bytes 3080 | tf_op jit(solution)/shard_map/ppermute | solution.py:21
  354.1 9.4 %collective-permute-start.24 = (f32[1,8,32]{2,1,0:T(8,128)S(1)}, f32[1,8,32]{2,1,0:T(8,128)S(1)}, u32[]{:S(2)}, u32[]{:S(2)}) collective-permute-start(f32[1,8,32]{2,1,0:T(8,128)S(1)} %select_bitcast_fusion.12), channel_id=1, source_target_pairs={{0,16},{1,17},{2,18},{3,19},{4,20},{5,21},{6,22},{7,23},{8,24},{9,... | collective-permute-start | bytes 3080 | tf_op jit(solution)/shard_map/ppermute | solution.py:21
  361.6 12.4 %copy-start.1 = (bf16[8,128,1024]{2,1,0:T(8,128)(2,1)S(1)}, bf16[8,128,1024]{2,1,0:T(8,128)(2,1)}, u32[]{:S(2)}) copy-start(bf16[8,128,1024]{2,1,0:T(8,128)(2,1)} %param.8) | copy-start | bytes 6291460
  362.0 5.1 %collective-permute-start.17 = (bf16[2,8,32,128]{3,2,1,0:T(8,128)(2,1)S(1)}, bf16[2,8,32,128]{3,2,1,0:T(8,128)(2,1)S(1)}, u32[]{:S(2)}, u32[]{:S(2)}) collective-permute-start(bf16[2,8,32,128]{3,2,1,0:T(8,128)(2,1)S(1)} %fusion.25), channel_id=1, source_target_pairs={{0,8},{1,9},{2,10},{3,11},{4,12},{5,13},{6,14},{7,15},{8,0},{9,1},... | collective-permute-start | bytes 393224 | tf_op jit(solution)/shard_map/ppermute | solution.py:21
  367.3 5.9 %collective-permute-start.19 = (bf16[1,8,32,128]{3,2,1,0:T(8,128)(2,1)S(1)}, bf16[1,8,32,128]{3,2,1,0:T(8,128)(2,1)S(1)}, u32[]{:S(2)}, u32[]{:S(2)}) collective-permute-start(bf16[1,8,32,128]{3,2,1,0:T(8,128)(2,1)S(1)} %fusion.30), channel_id=1, source_target_pairs={{0,16},{1,17},{2,18},{3,19},{4,20},{5,21},{6,22},{7,23},{8,24},{9,... | collective-permute-start | bytes 196616 | tf_op jit(solution)/shard_map/ppermute | solution.py:21

commit v6 on v5

--- a/solution.py
+++ b/solution.py
@@ -137,6 +137,15 @@
     outgoing = jnp.where(
         filled[:, :, None, None], jnp.take(span_cache, chosen, axis=0), jnp.zeros((), jnp.bfloat16)
     )
+    local_rows = hidden[0]
+    partial = jnp.dot(local_rows, kv_weight, preferred_element_type=jnp.float32)
+    recomputed = scatter_rows(
+        partial.reshape(cycle_size, RCP, feature_count), my_ctx, add_parts
+    ).astype(jnp.bfloat16)
+    all_queries = gather_rows(queries[0], my_ctx)
+    outgoing, recomputed, all_queries = lax.optimization_barrier(
+        (outgoing, recomputed, all_queries)
+    )
     arrived = lax.all_to_all(outgoing, "owner", split_axis=0, concat_axis=0, tiled=True)
     wanted = lax.dynamic_index_in_dim(retrieval, my_owner, 0, keepdims=False)
     my_count = lax.dynamic_index_in_dim(counts, my_owner, 0, keepdims=False)
@@ -152,11 +161,6 @@
     blocks = jnp.take(flattened, source * CAP + ordinal, axis=0, mode="clip")
     blocks = jnp.where(my_in_use[:, None, None], blocks, jnp.zeros((), jnp.bfloat16))
     context = blocks.reshape(CTX_DEV, feature_count)
-    local_rows = hidden[0]
-    partial = jnp.dot(local_rows, kv_weight, preferred_element_type=jnp.float32)
-    recomputed = scatter_rows(
-        partial.reshape(cycle_size, RCP, feature_count), my_ctx, add_parts
-    ).astype(jnp.bfloat16)
     every_pos = recompute_pos[0]
     own_pos = lax.dynamic_slice_in_dim(every_pos, my_ctx * RCP, RCP)
     matches = jnp.arange(CTX_DEV, dtype=jnp.int32)[:, None] == own_pos[None, :]
@@ -170,7 +174,6 @@
     mask_cols = block_mask[0]
     query_count = cycle_size * RCP
     query_pos = jnp.arange(query_count, dtype=jnp.int32) // RCP * CTX_DEV + every_pos
-    all_queries = gather_rows(queries[0], my_ctx)
     per_group = QH // KVH
     allowed = jnp.take(mask_cols, query_pos // BLK, axis=0)
     visible = jnp.repeat(allowed, BLK, axis=1) > 0

time: 376 us -> 357 us (0.949)
  waiting for transfers between devices: 246 us -> 234 us
  starting transfers between devices: 45.4 us -> 41.2 us
    ppermute x25, waiting for transfers between devices: 246 us -> 61.3 us  [exchange(): return lax.ppermute(shard, 'ctx', [(i, i ^ bit) for i in range(peers)])]
    all_to_all x1, waiting for transfers between devices: 0.01 us -> 173 us  [on_device(): lax.all_to_all(outgoing, 'owner', split_axis=0, concat_axis=0, tiled=True)]
  transfers between devices with their start and end apart: 26 -> 26, of which waited for: 11 -> 14; matrix products, arithmetic and copies ran while one was open for 8% -> 11% of each run, Pallas kernels for 0% -> 0%
where the time goes in v6:
time: 357 us; the launch traced here: 356 us
  waiting for transfers between devices  234 us (66%)
  starting transfers between devices  41.2 us (12%)
  other arithmetic  29.2 us (8%)
  local copies, waits for them, and re-layouts  24.9 us (7%)
  Pallas kernels  21.5 us (6%)
  matrix products  3.96 us (1%)
    all_to_all x1, waiting for transfers between devices, on_device(): lax.all_to_all(outgoing, 'owner', split_axis=0, concat_axis=0, tiled=True)  173 us
    ppermute x25, waiting for transfers between devices, exchange(): return lax.ppermute(shard, 'ctx', [(i, i ^ bit) for i in range(peers)])  61.3 us
    ppermute x25, starting transfers between devices, exchange(): return lax.ppermute(shard, 'ctx', [(i, i ^ bit) for i in range(peers)])  31.7 us
    pallas_call x1, Pallas kernels, attend_local(): pl.pallas_call(attend_kernel, grid=(KVH,), in_specs=[pl.BlockSpec((rows,...  21.5 us
    all_to_all x1, starting transfers between devices, on_device(): lax.all_to_all(outgoing, 'owner', split_axis=0, concat_axis=0, tiled=True)  9.5 us
    select_n x1, other arithmetic, on_device(): jnp.where(filled[:, :, None, None], jnp.take(span_cache, chosen, axis=0),...  7.65 us
  transfers between devices with their start and end apart: 26, of which 14 were waited for; matrix products, arithmetic and copies ran while one was open for 11% of the time, Pallas kernels for 0%

profile of v6, /device:TPU:6, one launch (start us, length us, event | category | flops | bytes accessed | tf_op | source)
XLA Modules:
  0.0 356.3 jit_solution(14451164583719805959)
XLA Ops:
  0.8 1.5 fusion.14
  2.3 0.9 select_bitcast_fusion
  3.2 0.4 collective-permute-start
  4.6 2.0 collective-permute-start.6
  6.6 1.1 fusion.13
  7.8 0.9 collective-permute-start.1
  8.6 1.9 collective-permute-done.6
  10.5 3.4 collective-permute-start.7
  13.9 6.8 %collective-permute-done.1 = f32[8,8,1024]{2,1,0:T(8,128)S(1)} collective-permute-done((f32[8,8,1024]{2,1,0:T(8,128)S(1)}, f32[8,8,1024]{2,1,0:T(8,128)S(1)}, u32[]{:S(2)}, u32[]{:S(2)}) %collective-permute-start.1) | collective-permute-done | bytes 262176 | tf_op jit(solution)/shard_map/ppermute | solution.py:21
  20.8 8.3 %collective-permute-done.7 = bf16[32,4096]{1,0:T(8,128)(2,1)S(1)} collective-permute-done((bf16[32,4096]{1,0:T(8,128)(2,1)S(1)}, bf16[32,4096]{1,0:T(8,128)(2,1)S(1)}, u32[]{:S(2)}, u32[]{:S(2)}) %collective-permute-start.7) | collective-permute-done | bytes 262176 | tf_op jit(solution)/shard_map/ppermute | solution.py:21
  29.3 1.7 collective-permute-start.8
  31.1 1.7 collective-permute-start.3
  32.7 4.8 %gather_fusion = bf16[32,128,1024]{2,1,0:T(8,128)(2,1)} fusion(bf16[8,128,1024]{2,1,0:T(8,128)(2,1)S(1)} %copy-done, s32[1024]{0:T(1024)S(1)} %pad_clamp_fusion.2), kind=kCustom, calls=%fused_computation | custom fusion | bytes 16777344 | tf_op jit(solution)/shard_map/jit(_take)/gather | solution.py:138
  37.6 2.3 collective-permute-done.3
  39.9 3.6 %collective-permute-start.4 = (f32[1,8,1024]{2,1,0:T(8,128)S(1)}, f32[1,8,1024]{2,1,0:T(8,128)S(1)}, u32[]{:S(2)}, u32[]{:S(2)}) collective-permute-start(f32[1,8,1024]{2,1,0:T(8,128)S(1)} %select_bitcast_fusion.7), channel_id=1, source_target_pairs={{0,16},{1,17},{2,18},{3,19},{4,20},{5,21},{6,22},{7,23},{8,24},{9,... | collective-permute-start | bytes 98312 | tf_op jit(solution)/shard_map/ppermute | solution.py:21
  43.9 7.6 %select_select_fusion = bf16[8,4,128,1024]{3,2,1,0:T(8,128)(2,1)} fusion(bf16[8,4,128,1024]{3,2,1,0:T(8,128)(2,1)} %bitcast.423, pred[8,4]{1,0:T(8,128)(4,1)S(1)} %copy.224, pred[8,4]{1,0:T(8,128)(4,1)S(1)} %copy.223), kind=kLoop, calls=%fused_computation.3 | loop fusion | flops 8388608 | bytes 16777280 | tf_op jit(solution)/shard_map/jit(_where)/select_n | solution.py:137
  51.6 14.9 %collective-permute-done.9 = bf16[128,4096]{1,0:T(8,128)(2,1)S(1)} collective-permute-done((bf16[128,4096]{1,0:T(8,128)(2,1)S(1)}, bf16[128,4096]{1,0:T(8,128)(2,1)S(1)}, u32[]{:S(2)}, u32[]{:S(2)}) %collective-permute-start.9) | collective-permute-done | bytes 1048608 | tf_op jit(solution)/shard_map/ppermute | solution.py:21
  66.5 1.9 maximum_select_fusion.query_ref
  68.4 9.5 %all-to-all-start = ((bf16[8,4,128,1024]{3,2,1,0:T(8,128)(2,1)}), bf16[8,4,128,1024]{3,2,1,0:T(8,128)(2,1)}, u32[]{:S(2)}, u32[]{:S(2)}) async-start(bf16[8,4,128,1024]{3,2,1,0:T(8,128)(2,1)} %select_select_fusion), calls=%async_computation | async-start | bytes 16777216 | tf_op jit(solution)/shard_map/all_to_all | solution.py:149
  77.9 0.6 dynamic_slice.12
  78.7 0.7 gather_fusion.2
  79.4 0.7 broadcast_compare_fusion
  80.2 0.7 fusion.53
  81.7 1.3 fusion.7.mask_ref
  83.0 173.0 %all-to-all-done = bf16[8,4,128,1024]{3,2,1,0:T(8,128)(2,1)} async-done(((bf16[8,4,128,1024]{3,2,1,0:T(8,128)(2,1)}), bf16[8,4,128,1024]{3,2,1,0:T(8,128)(2,1)}, u32[]{:S(2)}, u32[]{:S(2)}) %all-to-all-start) | async-done | bytes 8388640 | tf_op jit(solution)/shard_map/all_to_all | solution.py:149
  256.0 5.4 %gather_fusion.1 = bf16[8,128,1024]{2,1,0:T(8,128)(2,1)} fusion(bf16[32,128,1024]{2,1,0:T(8,128)(2,1)} %bitcast.36, s32[1024]{0:T(1024)S(1)} %pad_clamp_fusion.1), kind=kCustom, calls=%fused_computation.1 | custom fusion | bytes 4194336 | tf_op jit(solution)/shard_map/jit(_take)/gather | solution.py:161
  261.4 2.4 fusion.1
  263.8 1.6 fusion.75
  265.8 21.5 %shard_map.95 = (f32[256,4096]{1,0:T(8,128)}, f32[4,256,8]{2,1,0:T(8,128)}, f32[4,256,8]{2,1,0:T(8,128)}) custom-call(bf16[256,4096]{1,0:T(8,128)(2,1)} %maximum_select_fusion.query_ref, bf16[1024,512]{1,0:T(8,128)(2,1)} %get-tuple-element.39.key_ref, bf16[1024,512]{1,0:T(8,128)(2,1)} %get-tuple-element.38.value_ref, f32[256,1024]{1,0:T(8,128)} %fusion.7.mask_ref), custom_call_target="tpu_custom_call" | custom-call | flops 4294967296 | bytes 9437184 | tf_op jit(solution)/shard_map/pallas_call | solution.py:94
  287.4 1.3 copy.274
  288.6 0.8 reshape_reshape_reshape.11
  289.4 0.4 fusion.76
  290.2 0.8 reshape_reshape_reshape.10
  291.0 0.5 broadcast_select_fusion
  291.5 0.6 collective-permute-start.10
  292.0 4.1 %fusion.74 = (f32[16,1,8,32,128]{4,2,3,1,0:T(8,128)S(1)}, f32[16,1,8,32,128]{4,2,3,1,0:T(8,128)}) fusion(f32[16,2,8,32,128]{4,2,3,1,0:T(8,128)} %bitcast.431), kind=kLoop, calls=%fused_computation.204 | loop fusion | bytes 8388608 | tf_op jit(solution)/shard_map/slice | solution.py:45
  296.1 0.7 copy-done.6
  296.8 1.8 fusion.23
  299.0 0.6 select_bitcast_fusion.6
  300.0 2.3 collective-permute-start.21
  302.4 2.2 fusion.2
  304.7 1.4 fusion.34
  306.1 0.6 select_bitcast_fusion.9
  306.7 2.7 collective-permute-start.14
  309.4 0.6 select_bitcast_fusion.8
  310.3 1.1 copy.250
  311.6 3.4 collective-permute-done.22
  315.0 0.8 fusion.40
  315.9 0.8 collective-permute-start.16
  316.6 2.6 fusion
  319.4 0.5 collective-permute-start.13
  319.9 1.3 collective-permute-start.23
  321.2 2.3 collective-permute-done.23
  323.5 1.9 collective-permute-start.24
  325.4 5.3 %collective-permute-done.13 = bf16[8,8,32,128]{3,2,1,0:T(8,128)(2,1)S(1)} collective-permute-done((bf16[8,8,32,128]{3,2,1,0:T(8,128)(2,1)S(1)}, bf16[8,8,32,128]{3,2,1,0:T(8,128)(2,1)S(1)}, u32[]{:S(2)}, u32[]{:S(2)}) %collective-permute-start.13) | collective-permute-done | bytes 524320 | tf_op jit(solution)/shard_map/ppermute | solution.py:21
  330.7 0.7 fusion.5
  331.5 1.4 collective-permute-start.15
  332.9 3.0 collective-permute-start.18
  335.9 7.5 %collective-permute-done.15 = bf16[4,8,32,128]{3,2,1,0:T(8,128)(2,1)S(1)} collective-permute-done((bf16[4,8,32,128]{3,2,1,0:T(8,128)(2,1)S(1)}, bf16[4,8,32,128]{3,2,1,0:T(8,128)(2,1)S(1)}, u32[]{:S(2)}, u32[]{:S(2)}) %collective-permute-start.15) | collective-permute-done | bytes 262176 | tf_op jit(solution)/shard_map/ppermute | solution.py:21
  343.8 1.4 collective-permute-start.17
  345.3 4.0 %collective-permute-done.17 = bf16[2,8,32,128]{3,2,1,0:T(8,128)(2,1)S(1)} collective-permute-done((bf16[2,8,32,128]{3,2,1,0:T(8,128)(2,1)S(1)}, bf16[2,8,32,128]{3,2,1,0:T(8,128)(2,1)S(1)}, u32[]{:S(2)}, u32[]{:S(2)}) %collective-permute-start.17) | collective-permute-done | bytes 131104 | tf_op jit(solution)/shard_map/ppermute | solution.py:21
  349.5 1.5 collective-permute-start.19
  351.1 4.3 %collective-permute-done.19 = bf16[1,8,32,128]{3,2,1,0:T(8,128)(2,1)S(1)} collective-permute-done((bf16[1,8,32,128]{3,2,1,0:T(8,128)(2,1)S(1)}, bf16[1,8,32,128]{3,2,1,0:T(8,128)(2,1)S(1)}, u32[]{:S(2)}, u32[]{:S(2)}) %collective-permute-start.19) | collective-permute-done | bytes 65568 | tf_op jit(solution)/shard_map/ppermute | solution.py:21
  355.5 0.7 fusion.28
  (115 shorter events, 6.1 us)
Async XLA Ops:
  0.6 32.1 %copy-start = (bf16[8,128,1024]{2,1,0:T(8,128)(2,1)S(1)}, bf16[8,128,1024]{2,1,0:T(8,128)(2,1)}, u32[]{:S(2)}) copy-start(bf16[8,128,1024]{2,1,0:T(8,128)(2,1)} %param.8) | copy-start | bytes 6291460
  0.6 3.9 %copy-start.9 = (bf16[1,8,4096]{2,1,0:T(8,128)(2,1)S(1)}, bf16[1,8,4096]{2,1,0:T(8,128)(2,1)}, u32[]{:S(2)}) copy-start(bf16[1,8,4096]{2,1,0:T(8,128)(2,1)} %param.14) | copy-start | bytes 196612
  0.7 2.9 copy-start.13
  0.7 2.9 copy-start.10
  0.7 3.9 %collective-permute-start.5 = (bf16[8,4096]{1,0:T(8,128)(2,1)}, bf16[8,4096]{1,0:T(8,128)(2,1)S(1)}, u32[]{:S(2)}, u32[]{:S(2)}) collective-permute-start(bf16[8,4096]{1,0:T(8,128)(2,1)} %bitcast.460), channel_id=1, source_target_pairs={{0,1},{1,0},{2,3},{3,2},{4,5},{5,4},{6,7},{7,6},{8,9},{9,8},{10,11... | collective-permute-start | bytes 196616 | tf_op jit(solution)/shard_map/ppermute | solution.py:21
  3.2 3.4 collective-permute-start
  4.6 5.9 %collective-permute-start.6 = (bf16[16,4096]{1,0:T(8,128)(2,1)S(1)}, bf16[16,4096]{1,0:T(8,128)(2,1)S(1)}, u32[]{:S(2)}, u32[]{:S(2)}) collective-permute-start(bf16[16,4096]{1,0:T(8,128)(2,1)S(1)} %maximum_select_fusion.4), channel_id=1, source_target_pairs={{0,2},{1,3},{2,0},{3,1},{4,6},{5,7},{6,4},{7,5},{8,10},{9,11},{10,... | collective-permute-start | bytes 393224 | tf_op jit(solution)/shard_map/ppermute | solution.py:21
  7.8 12.9 %collective-permute-start.1 = (f32[8,8,1024]{2,1,0:T(8,128)S(1)}, f32[8,8,1024]{2,1,0:T(8,128)S(1)}, u32[]{:S(2)}, u32[]{:S(2)}) collective-permute-start(f32[8,8,1024]{2,1,0:T(8,128)S(1)} %select_bitcast_fusion.2), channel_id=1, source_target_pairs={{0,2},{1,3},{2,0},{3,1},{4,6},{5,7},{6,4},{7,5},{8,10},{9,11},{10,... | collective-permute-start | bytes 786440 | tf_op jit(solution)/shard_map/ppermute | solution.py:21
  10.5 18.6 %collective-permute-start.7 = (bf16[32,4096]{1,0:T(8,128)(2,1)S(1)}, bf16[32,4096]{1,0:T(8,128)(2,1)S(1)}, u32[]{:S(2)}, u32[]{:S(2)}) collective-permute-start(bf16[32,4096]{1,0:T(8,128)(2,1)S(1)} %maximum_select_fusion.3), channel_id=1, source_target_pairs={{0,4},{1,5},{2,6},{3,7},{4,0},{5,1},{6,2},{7,3},{8,12},{9,13},{10,... | collective-permute-start | bytes 786440 | tf_op jit(solution)/shard_map/ppermute | solution.py:21
  20.7 10.3 %collective-permute-start.2 = (f32[4,8,1024]{2,1,0:T(8,128)S(1)}, f32[4,8,1024]{2,1,0:T(8,128)S(1)}, u32[]{:S(2)}, u32[]{:S(2)}) collective-permute-start(f32[4,8,1024]{2,1,0:T(8,128)S(1)} %select_bitcast_fusion.3), channel_id=1, source_target_pairs={{0,4},{1,5},{2,6},{3,7},{4,0},{5,1},{6,2},{7,3},{8,12},{9,13},{10,... | collective-permute-start | bytes 393224 | tf_op jit(solution)/shard_map/ppermute | solution.py:21
  29.3 14.3 %collective-permute-start.8 = (bf16[64,4096]{1,0:T(8,128)(2,1)S(1)}, bf16[64,4096]{1,0:T(8,128)(2,1)S(1)}, u32[]{:S(2)}, u32[]{:S(2)}) collective-permute-start(bf16[64,4096]{1,0:T(8,128)(2,1)S(1)} %maximum_select_fusion.2), channel_id=1, source_target_pairs={{0,8},{1,9},{2,10},{3,11},{4,12},{5,13},{6,14},{7,15},{8,0},{9,1},... | collective-permute-start | bytes 1572872 | tf_op jit(solution)/shard_map/ppermute | solution.py:21
  31.1 8.9 %collective-permute-start.3 = (f32[2,8,1024]{2,1,0:T(8,128)S(1)}, f32[2,8,1024]{2,1,0:T(8,128)S(1)}, u32[]{:S(2)}, u32[]{:S(2)}) collective-permute-start(f32[2,8,1024]{2,1,0:T(8,128)S(1)} %select_bitcast_fusion.4), channel_id=1, source_target_pairs={{0,8},{1,9},{2,10},{3,11},{4,12},{5,13},{6,14},{7,15},{8,0},{9,1},... | collective-permute-start | bytes 196616 | tf_op jit(solution)/shard_map/ppermute | solution.py:21
  39.9 11.6 %collective-permute-start.4 = (f32[1,8,1024]{2,1,0:T(8,128)S(1)}, f32[1,8,1024]{2,1,0:T(8,128)S(1)}, u32[]{:S(2)}, u32[]{:S(2)}) collective-permute-start(f32[1,8,1024]{2,1,0:T(8,128)S(1)} %select_bitcast_fusion.7), channel_id=1, source_target_pairs={{0,16},{1,17},{2,18},{3,19},{4,20},{5,21},{6,22},{7,23},{8,24},{9,... | collective-permute-start | bytes 98312 | tf_op jit(solution)/shard_map/ppermute | solution.py:21
  43.8 22.7 %collective-permute-start.9 = (bf16[128,4096]{1,0:T(8,128)(2,1)S(1)}, bf16[128,4096]{1,0:T(8,128)(2,1)S(1)}, u32[]{:S(2)}, u32[]{:S(2)}) collective-permute-start(bf16[128,4096]{1,0:T(8,128)(2,1)S(1)} %maximum_select_fusion.1), channel_id=1, source_target_pairs={{0,16},{1,17},{2,18},{3,19},{4,20},{5,21},{6,22},{7,23},{8,24},{9,... | collective-permute-start | bytes 3145736 | tf_op jit(solution)/shard_map/ppermute | solution.py:21
  68.4 10.1 %copy-start.11 = (s32[1,256,8]{1,2,0:T(8,128)S(1)}, s32[1,256,8]{1,2,0:T(8,128)}, u32[]{:S(2)}) copy-start(s32[1,256,8]{1,2,0:T(8,128)} %param.15) | copy-start | bytes 24580
  68.4 10.2 %copy-start.12 = (s32[1,256]{1,0:T(1,128)S(1)}, s32[1,256]{1,0:T(1,128)}, u32[]{:S(2)}) copy-start(s32[1,256]{1,0:T(1,128)} %param.11) | copy-start | bytes 3076
  68.4 187.6 %all-to-all-start = ((bf16[8,4,128,1024]{3,2,1,0:T(8,128)(2,1)}), bf16[8,4,128,1024]{3,2,1,0:T(8,128)(2,1)}, u32[]{:S(2)}, u32[]{:S(2)}) async-start(bf16[8,4,128,1024]{3,2,1,0:T(8,128)(2,1)} %select_select_fusion), calls=%async_computation | async-start | bytes 16777216 | tf_op jit(solution)/shard_map/all_to_all | solution.py:149
  263.8 2.0 copy-start.2
  287.3 2.6 copy-start.3
  289.9 6.2 %collective-permute-start.20 = (f32[16,8,32]{1,0,2:T(8,128)S(1)}, f32[16,8,32]{1,0,2:T(8,128)S(1)}, u32[]{:S(2)}, u32[]{:S(2)}) collective-permute-start(f32[16,8,32]{1,0,2:T(8,128)S(1)} %select_bitcast_fusion.1), channel_id=1, source_target_pairs={{0,1},{1,0},{2,3},{3,2},{4,5},{5,4},{6,7},{7,6},{8,9},{9,8},{10,11... | collective-permute-start | bytes 49160 | tf_op jit(solution)/shard_map/ppermute | solution.py:21
  291.5 4.6 %collective-permute-start.10 = (f32[16,8,32]{1,0,2:T(8,128)S(1)}, f32[16,8,32]{1,0,2:T(8,128)S(1)}, u32[]{:S(2)}, u32[]{:S(2)}) collective-permute-start(f32[16,8,32]{1,0,2:T(8,128)S(1)} %bitcast.454), channel_id=1, source_target_pairs={{0,1},{1,0},{2,3},{3,2},{4,5},{5,4},{6,7},{7,6},{8,9},{9,8},{10,11... | collective-permute-start | bytes 49160 | tf_op jit(solution)/shard_map/ppermute | solution.py:21
  296.1 0.7 copy-start.6
  299.6 5.1 %collective-permute-start.12 = (f32[8,8,32]{2,1,0:T(8,128)}, f32[8,8,32]{2,1,0:T(8,128)}, u32[]{:S(2)}, u32[]{:S(2)}) collective-permute-start(f32[8,8,32]{2,1,0:T(8,128)} %select_bitcast_fusion.6), channel_id=1, source_target_pairs={{0,2},{1,3},{2,0},{3,1},{4,6},{5,7},{6,4},{7,5},{8,10},{9,11},{10,... | collective-permute-start | bytes 24584 | tf_op jit(solution)/shard_map/ppermute | solution.py:21
  300.0 4.6 %collective-permute-start.21 = (f32[8,8,32]{2,1,0:T(8,128)S(1)}, f32[8,8,32]{2,1,0:T(8,128)S(1)}, u32[]{:S(2)}, u32[]{:S(2)}) collective-permute-start(f32[8,8,32]{2,1,0:T(8,128)S(1)} %select_bitcast_fusion.5), channel_id=1, source_target_pairs={{0,2},{1,3},{2,0},{3,1},{4,6},{5,7},{6,4},{7,5},{8,10},{9,11},{10,... | collective-permute-start | bytes 24584 | tf_op jit(solution)/shard_map/ppermute | solution.py:21
  304.6 12.1 %collective-permute-start.11 = (bf16[16,8,32,128]{3,2,1,0:T(8,128)(2,1)S(1)}, bf16[16,8,32,128]{3,2,1,0:T(8,128)(2,1)}, u32[]{:S(2)}, u32[]{:S(2)}) collective-permute-start(bf16[16,8,32,128]{3,2,1,0:T(8,128)(2,1)S(1)} %fusion.2), channel_id=1, source_target_pairs={{0,1},{1,0},{2,3},{3,2},{4,5},{5,4},{6,7},{7,6},{8,9},{9,8},{10,11... | collective-permute-start | bytes 3145736 | tf_op jit(solution)/shard_map/ppermute | solution.py:21
  306.1 3.3 copy-start.4
  306.1 3.9 %copy-start.5 = (f32[8,8,32]{2,1,0:T(8,128)}, f32[8,8,32]{2,1,0:T(8,128)S(1)}, u32[]{:S(2)}) copy-start(f32[8,8,32]{2,1,0:T(8,128)S(1)} %get-tuple-element.27) | copy-start | bytes 24580
  306.7 4.8 %collective-permute-start.14 = (f32[4,8,32]{2,1,0:T(8,128)}, f32[4,8,32]{2,1,0:T(8,128)S(1)}, u32[]{:S(2)}, u32[]{:S(2)}) collective-permute-start(f32[4,8,32]{2,1,0:T(8,128)} %select_bitcast_fusion.9), channel_id=1, source_target_pairs={{0,4},{1,5},{2,6},{3,7},{4,0},{5,1},{6,2},{7,3},{8,12},{9,13},{10,... | collective-permute-start | bytes 12296 | tf_op jit(solution)/shard_map/ppermute | solution.py:21
  310.0 5.0 %collective-permute-start.22 = (f32[4,8,32]{2,1,0:T(8,128)}, f32[4,8,32]{2,1,0:T(8,128)}, u32[]{:S(2)}, u32[]{:S(2)}) collective-permute-start(f32[4,8,32]{2,1,0:T(8,128)} %select_bitcast_fusion.8), channel_id=1, source_target_pairs={{0,4},{1,5},{2,6},{3,7},{4,0},{5,1},{6,2},{7,3},{8,12},{9,13},{10,... | collective-permute-start | bytes 12296 | tf_op jit(solution)/shard_map/ppermute | solution.py:21
  315.8 14.9 %copy-start.7 = (f32[8,8,32]{2,1,0:T(8,128)S(1)}, f32[8,8,32]{2,1,0:T(8,128)}, u32[]{:S(2)}) copy-start(f32[8,8,32]{2,1,0:T(8,128)} %get-tuple-element.25) | copy-start | bytes 24580
  315.8 14.9 %copy-start.8 = (f32[8,8,32]{2,1,0:T(8,128)S(1)}, f32[8,8,32]{2,1,0:T(8,128)}, u32[]{:S(2)}) copy-start(f32[8,8,32]{2,1,0:T(8,128)} %get-tuple-element.26) | copy-start | bytes 24580
  315.9 5.3 %collective-permute-start.16 = (f32[2,8,32]{2,1,0:T(8,128)S(1)}, f32[2,8,32]{2,1,0:T(8,128)S(1)}, u32[]{:S(2)}, u32[]{:S(2)}) collective-permute-start(f32[2,8,32]{2,1,0:T(8,128)S(1)} %select_bitcast_fusion.11), channel_id=1, source_target_pairs={{0,8},{1,9},{2,10},{3,11},{4,12},{5,13},{6,14},{7,15},{8,0},{9,1},... | collective-permute-start | bytes 6152 | tf_op jit(solution)/shard_map/ppermute | solution.py:21
  319.4 11.3 %collective-permute-start.13 = (bf16[8,8,32,128]{3,2,1,0:T(8,128)(2,1)S(1)}, bf16[8,8,32,128]{3,2,1,0:T(8,128)(2,1)S(1)}, u32[]{:S(2)}, u32[]{:S(2)}) collective-permute-start(bf16[8,8,32,128]{3,2,1,0:T(8,128)(2,1)S(1)} %fusion.8), channel_id=1, source_target_pairs={{0,2},{1,3},{2,0},{3,1},{4,6},{5,7},{6,4},{7,5},{8,10},{9,11},{10,... | collective-permute-start | bytes 1572872 | tf_op jit(solution)/shard_map/ppermute | solution.py:21
  319.9 3.7 %collective-permute-start.23 = (f32[2,8,32]{2,1,0:T(8,128)S(1)}, f32[2,8,32]{2,1,0:T(8,128)S(1)}, u32[]{:S(2)}, u32[]{:S(2)}) collective-permute-start(f32[2,8,32]{2,1,0:T(8,128)S(1)} %select_bitcast_fusion.10), channel_id=1, source_target_pairs={{0,8},{1,9},{2,10},{3,11},{4,12},{5,13},{6,14},{7,15},{8,0},{9,1},... | collective-permute-start | bytes 6152 | tf_op jit(solution)/shard_map/ppermute | solution.py:21
  323.5 21.7 %collective-permute-start.24 = (f32[1,8,32]{2,1,0:T(8,128)S(1)}, f32[1,8,32]{2,1,0:T(8,128)S(1)}, u32[]{:S(2)}, u32[]{:S(2)}) collective-permute-start(f32[1,8,32]{2,1,0:T(8,128)S(1)} %select_bitcast_fusion.12), channel_id=1, source_target_pairs={{0,16},{1,17},{2,18},{3,19},{4,20},{5,21},{6,22},{7,23},{8,24},{9,... | collective-permute-start | bytes 3080 | tf_op jit(solution)/shard_map/ppermute | solution.py:21
  331.5 12.0 %collective-permute-start.15 = (bf16[4,8,32,128]{3,2,1,0:T(8,128)(2,1)S(1)}, bf16[4,8,32,128]{3,2,1,0:T(8,128)(2,1)S(1)}, u32[]{:S(2)}, u32[]{:S(2)}) collective-permute-start(bf16[4,8,32,128]{3,2,1,0:T(8,128)(2,1)S(1)} %fusion.16), channel_id=1, source_target_pairs={{0,4},{1,5},{2,6},{3,7},{4,0},{5,1},{6,2},{7,3},{8,12},{9,13},{10,... | collective-permute-start | bytes 786440 | tf_op jit(solution)/shard_map/ppermute | solution.py:21
  332.9 12.3 %collective-permute-start.18 = (f32[1,8,32]{2,1,0:T(8,128)S(1)}, f32[1,8,32]{2,1,0:T(8,128)S(1)}, u32[]{:S(2)}, u32[]{:S(2)}) collective-permute-start(f32[1,8,32]{2,1,0:T(8,128)S(1)} %select_bitcast_fusion.13), channel_id=1, source_target_pairs={{0,16},{1,17},{2,18},{3,19},{4,20},{5,21},{6,22},{7,23},{8,24},{9,... | collective-permute-start | bytes 3080 | tf_op jit(solution)/shard_map/ppermute | solution.py:21
  343.5 12.8 %copy-start.1 = (bf16[8,128,1024]{2,1,0:T(8,128)(2,1)S(1)}, bf16[8,128,1024]{2,1,0:T(8,128)(2,1)}, u32[]{:S(2)}) copy-start(bf16[8,128,1024]{2,1,0:T(8,128)(2,1)} %param.8) | copy-start | bytes 6291460
  343.8 5.4 %collective-permute-start.17 = (bf16[2,8,32,128]{3,2,1,0:T(8,128)(2,1)S(1)}, bf16[2,8,32,128]{3,2,1,0:T(8,128)(2,1)S(1)}, u32[]{:S(2)}, u32[]{:S(2)}) collective-permute-start(bf16[2,8,32,128]{3,2,1,0:T(8,128)(2,1)S(1)} %fusion.25), channel_id=1, source_target_pairs={{0,8},{1,9},{2,10},{3,11},{4,12},{5,13},{6,14},{7,15},{8,0},{9,1},... | collective-permute-start | bytes 393224 | tf_op jit(solution)/shard_map/ppermute | solution.py:21
  349.5 5.9 %collective-permute-start.19 = (bf16[1,8,32,128]{3,2,1,0:T(8,128)(2,1)S(1)}, bf16[1,8,32,128]{3,2,1,0:T(8,128)(2,1)S(1)}, u32[]{:S(2)}, u32[]{:S(2)}) collective-permute-start(bf16[1,8,32,128]{3,2,1,0:T(8,128)(2,1)S(1)} %fusion.30), channel_id=1, source_target_pairs={{0,16},{1,17},{2,18},{3,19},{4,20},{5,21},{6,22},{7,23},{8,24},{9,... | collective-permute-start | bytes 196616 | tf_op jit(solution)/shard_map/ppermute | solution.py:21

commit v7 on v6

--- a/solution.py
+++ b/solution.py
@@ -54,13 +54,16 @@
 
 
 def merge_softmax(a, b):
-    numerator_a, running_a, totals_a = a
-    numerator_b, running_b, totals_b = b
+    numerator_a, stats_a = a
+    numerator_b, stats_b = b
+    running_a, totals_a = stats_a[..., :QH], stats_a[..., QH:]
+    running_b, totals_b = stats_b[..., :QH], stats_b[..., QH:]
     newest = jnp.maximum(running_a, running_b)
     factor_a = jnp.exp(running_a - newest)
     factor_b = jnp.exp(running_b - newest)
     numerator = numerator_a * factor_a[..., None] + numerator_b * factor_b[..., None]
-    return (numerator, newest, totals_a * factor_a + totals_b * factor_b)
+    totals = totals_a * factor_a + totals_b * factor_b
+    return (numerator, jnp.concatenate([newest, totals], axis=-1))
 
 
 def attend_kernel(query_ref, key_ref, value_ref, mask_ref, numerator_ref, running_ref, totals_ref):
@@ -187,17 +190,17 @@
     running = jnp.transpose(running, (1, 0, 2)).reshape(query_count, QH)
     totals = jnp.transpose(totals, (1, 0, 2)).reshape(query_count, QH)
     numerator = numerator.reshape(query_count, QH, HD)
-    numerator, running, totals = scatter_rows(
+    numerator, stats = scatter_rows(
         (
             numerator.reshape(cycle_size, RCP, QH, HD),
-            running.reshape(cycle_size, RCP, QH),
-            totals.reshape(cycle_size, RCP, QH),
+            jnp.concatenate([running, totals], axis=-1).reshape(cycle_size, RCP, 2 * QH),
         ),
         my_ctx,
         merge_softmax,
-        lambda t: (t[0].astype(jnp.bfloat16),) + t[1:],
-        lambda t: (t[0].astype(jnp.float32),) + t[1:],
-    )
+        lambda t: (t[0].astype(jnp.bfloat16), t[1]),
+        lambda t: (t[0].astype(jnp.float32), t[1]),
+    )
+    totals = stats[:, QH:]
     result = numerator / totals[:, :, None]
     attended = result.reshape(RCP, QH * HD).astype(jnp.bfloat16)
     return (context[None], attended[None])

time: 357 us -> 344 us (0.964)
  other arithmetic: 29.2 us -> 20.8 us
  starting transfers between devices: 41.2 us -> 36.1 us
  waiting for transfers between devices: 234 us -> 239 us
  local copies, waits for them, and re-layouts: 24.9 us -> 20.8 us
    ppermute x25 -> x20, starting transfers between devices: 31.7 us -> 26.6 us  [exchange(): return lax.ppermute(shard, 'ctx', [(i, i ^ bit) for i in range(peers)])]
    ppermute x25 -> x20, waiting for transfers between devices: 61.3 us -> 66 us  [exchange(): return lax.ppermute(shard, 'ctx', [(i, i ^ bit) for i in range(peers)])]
    add x3 -> x5, other arithmetic: 4 us -> 0.42 us  [merge_softmax(): totals = totals_a * factor_a + totals_b * factor_b]
  transfers between devices with their start and end apart: 26 -> 21, of which waited for: 14 -> 14; matrix products, arithmetic and copies ran while one was open for 11% -> 8% of each run, Pallas kernels for 0% -> 0%
where the time goes in v7:
time: 344 us
  waiting for transfers between devices  239 us (69%)
  starting transfers between devices  36.1 us (10%)
  Pallas kernels  21.6 us (6%)
  local copies, waits for them, and re-layouts  20.8 us (6%)
  other arithmetic  20.8 us (6%)
  matrix products  3.96 us (1%)
    all_to_all x1, waiting for transfers between devices, on_device(): lax.all_to_all(outgoing, 'owner', split_axis=0, concat_axis=0, tiled=True)  173 us
    ppermute x20, waiting for transfers between devices, exchange(): return lax.ppermute(shard, 'ctx', [(i, i ^ bit) for i in range(peers)])  66 us
    ppermute x20, starting transfers between devices, exchange(): return lax.ppermute(shard, 'ctx', [(i, i ^ bit) for i in range(peers)])  26.6 us
    pallas_call x1, Pallas kernels, attend_local(): pl.pallas_call(attend_kernel, grid=(KVH,), in_specs=[pl.BlockSpec((rows,...  21.6 us
    all_to_all x1, starting transfers between devices, on_device(): lax.all_to_all(outgoing, 'owner', split_axis=0, concat_axis=0, tiled=True)  9.58 us
    select_n x1, other arithmetic, on_device(): jnp.where(filled[:, :, None, None], jnp.take(span_cache, chosen, axis=0),...  7.64 us
  transfers between devices with their start and end apart: 21, of which 14 were waited for; matrix products, arithmetic and copies ran while one was open for 8% of the time, Pallas kernels for 0%

profile of v7, /device:TPU:6, one launch (start us, length us, event | category | flops | bytes accessed | tf_op | source)
XLA Modules:
  0.0 343.6 jit_solution(3212683713682091684)
XLA Ops:
  0.8 1.5 fusion.14
  2.3 0.9 select_bitcast_fusion
  3.2 0.4 collective-permute-start
  3.6 0.2 reduce_window_sum.11
  3.8 0.1 select_reduce_fusion
  4.3 0.1 fusion.43
  4.6 2.0 collective-permute-start.6
  6.6 1.1 fusion.13
  7.8 0.9 collective-permute-start.1
  8.6 1.9 collective-permute-done.6
  10.5 3.4 collective-permute-start.7
  13.9 6.8 %collective-permute-done.1 = f32[8,8,1024]{2,1,0:T(8,128)S(1)} collective-permute-done((f32[8,8,1024]{2,1,0:T(8,128)S(1)}, f32[8,8,1024]{2,1,0:T(8,128)S(1)}, u32[]{:S(2)}, u32[]{:S(2)}) %collective-permute-start.1) | collective-permute-done | bytes 262176 | tf_op jit(solution)/shard_map/ppermute | solution.py:21
  20.8 8.3 %collective-permute-done.7 = bf16[32,4096]{1,0:T(8,128)(2,1)S(1)} collective-permute-done((bf16[32,4096]{1,0:T(8,128)(2,1)S(1)}, bf16[32,4096]{1,0:T(8,128)(2,1)S(1)}, u32[]{:S(2)}, u32[]{:S(2)}) %collective-permute-start.7) | collective-permute-done | bytes 262176 | tf_op jit(solution)/shard_map/ppermute | solution.py:21
  29.2 1.7 collective-permute-start.8
  31.1 1.7 collective-permute-start.3
  32.7 4.7 %gather_fusion = bf16[32,128,1024]{2,1,0:T(8,128)(2,1)} fusion(bf16[8,128,1024]{2,1,0:T(8,128)(2,1)S(1)} %copy-done, s32[1024]{0:T(1024)S(1)} %pad_clamp_fusion.2), kind=kCustom, calls=%fused_computation | custom fusion | bytes 16777344 | tf_op jit(solution)/shard_map/jit(_take)/gather | solution.py:141
  37.5 2.5 collective-permute-done.3
  39.9 3.6 %collective-permute-start.4 = (f32[1,8,1024]{2,1,0:T(8,128)S(1)}, f32[1,8,1024]{2,1,0:T(8,128)S(1)}, u32[]{:S(2)}, u32[]{:S(2)}) collective-permute-start(f32[1,8,1024]{2,1,0:T(8,128)S(1)} %select_bitcast_fusion.7), channel_id=1, source_target_pairs={{0,16},{1,17},{2,18},{3,19},{4,20},{5,21},{6,22},{7,23},{8,24},{9,... | collective-permute-start | bytes 98312 | tf_op jit(solution)/shard_map/ppermute | solution.py:21
  43.6 0.2 maximum_select_fusion.1
  43.9 7.6 %select_select_fusion = bf16[8,4,128,1024]{3,2,1,0:T(8,128)(2,1)} fusion(bf16[8,4,128,1024]{3,2,1,0:T(8,128)(2,1)} %bitcast.325, pred[8,4]{1,0:T(8,128)(4,1)S(1)} %copy.359, pred[8,4]{1,0:T(8,128)(4,1)S(1)} %copy.358), kind=kLoop, calls=%fused_computation.3 | loop fusion | flops 8388608 | bytes 16777280 | tf_op jit(solution)/shard_map/jit(_where)/select_n | solution.py:140
  51.5 14.7 %collective-permute-done.9 = bf16[128,4096]{1,0:T(8,128)(2,1)S(1)} collective-permute-done((bf16[128,4096]{1,0:T(8,128)(2,1)S(1)}, bf16[128,4096]{1,0:T(8,128)(2,1)S(1)}, u32[]{:S(2)}, u32[]{:S(2)}) %collective-permute-start.9) | collective-permute-done | bytes 1048608 | tf_op jit(solution)/shard_map/ppermute | solution.py:21
  66.3 1.9 maximum_select_fusion.query_ref
  68.2 9.6 %all-to-all-start = ((bf16[8,4,128,1024]{3,2,1,0:T(8,128)(2,1)}), bf16[8,4,128,1024]{3,2,1,0:T(8,128)(2,1)}, u32[]{:S(2)}, u32[]{:S(2)}) async-start(bf16[8,4,128,1024]{3,2,1,0:T(8,128)(2,1)} %select_select_fusion), calls=%async_computation | async-start | bytes 16777216 | tf_op jit(solution)/shard_map/all_to_all | solution.py:152
  77.7 0.6 dynamic_slice.12
  78.5 0.7 gather_fusion.2
  79.3 0.7 broadcast_compare_fusion
  80.0 0.7 fusion.49
  80.7 0.2 convert_reduce_fusion
  81.2 0.3 broadcast_in_dim.121
  81.5 1.3 fusion.7.mask_ref
  82.8 173.2 %all-to-all-done = bf16[8,4,128,1024]{3,2,1,0:T(8,128)(2,1)} async-done(((bf16[8,4,128,1024]{3,2,1,0:T(8,128)(2,1)}), bf16[8,4,128,1024]{3,2,1,0:T(8,128)(2,1)}, u32[]{:S(2)}, u32[]{:S(2)}) %all-to-all-start) | async-done | bytes 8388640 | tf_op jit(solution)/shard_map/all_to_all | solution.py:152
  255.9 5.4 %gather_fusion.1 = bf16[8,128,1024]{2,1,0:T(8,128)(2,1)} fusion(bf16[32,128,1024]{2,1,0:T(8,128)(2,1)} %bitcast.36, s32[1024]{0:T(1024)S(1)} %pad_clamp_fusion.1), kind=kCustom, calls=%fused_computation.1 | custom fusion | bytes 4194336 | tf_op jit(solution)/shard_map/jit(_take)/gather | solution.py:164
  261.3 2.4 fusion.1
  263.8 1.6 fusion.65
  265.4 0.4 copy-done.1
  265.8 21.6 %shard_map.95 = (f32[256,4096]{1,0:T(8,128)}, f32[4,256,8]{2,1,0:T(8,128)}, f32[4,256,8]{2,1,0:T(8,128)}) custom-call(bf16[256,4096]{1,0:T(8,128)(2,1)} %maximum_select_fusion.query_ref, bf16[1024,512]{1,0:T(8,128)(2,1)} %get-tuple-element.41.key_ref, bf16[1024,512]{1,0:T(8,128)(2,1)} %get-tuple-element.40.value_ref, f32[256,1024]{1,0:T(8,128)} %fusion.7.mask_ref), custom_call_target="tpu_custom_call" | custom-call | flops 4294967296 | bytes 9437184 | tf_op jit(solution)/shard_map/pallas_call | solution.py:97
  287.4 1.3 copy.380
  288.6 0.8 concatenate.63
  289.4 0.3 copy.382
  289.8 0.2 copy.381
  289.9 0.8 concatenate.64
  290.8 0.3 copy.383
  291.4 2.5 fusion.64
  293.9 0.6 fusion.2
  294.5 0.6 collective-permute-start.11
  295.3 2.5 collective-permute-start.12
  297.9 1.9 collective-permute-done.12
  299.9 0.4 collective-permute-start.14
  300.4 4.3 %collective-permute-done.14 = f32[4,8,64]{2,1,0:T(8,128)S(1)} collective-permute-done((f32[4,8,64]{2,1,0:T(8,128)S(1)}, f32[4,8,64]{2,1,0:T(8,128)S(1)}, u32[]{:S(2)}, u32[]{:S(2)}) %collective-permute-start.14) | collective-permute-done | bytes 8224 | tf_op jit(solution)/shard_map/ppermute | solution.py:21
  304.8 0.9 collective-permute-start.16
  305.8 1.2 fusion
  307.1 2.1 collective-permute-start.13
  309.4 9.7 %collective-permute-done.13 = bf16[8,8,32,128]{3,2,1,0:T(8,128)(2,1)S(1)} collective-permute-done((bf16[8,8,32,128]{3,2,1,0:T(8,128)(2,1)S(1)}, bf16[8,8,32,128]{3,2,1,0:T(8,128)(2,1)S(1)}, u32[]{:S(2)}, u32[]{:S(2)}) %collective-permute-start.13) | collective-permute-done | bytes 524320 | tf_op jit(solution)/shard_map/ppermute | solution.py:21
  319.1 0.7 fusion.5
  320.0 2.3 collective-permute-start.18
  322.2 2.9 collective-permute-done.18
  325.2 5.9 %collective-permute-done.15 = bf16[4,8,32,128]{3,2,1,0:T(8,128)(2,1)S(1)} collective-permute-done((bf16[4,8,32,128]{3,2,1,0:T(8,128)(2,1)S(1)}, bf16[4,8,32,128]{3,2,1,0:T(8,128)(2,1)S(1)}, u32[]{:S(2)}, u32[]{:S(2)}) %collective-permute-start.15) | collective-permute-done | bytes 262176 | tf_op jit(solution)/shard_map/ppermute | solution.py:21
  331.2 0.3 fusion.11
  331.6 1.4 collective-permute-start.17
  333.0 3.6 %collective-permute-done.17 = bf16[2,8,32,128]{3,2,1,0:T(8,128)(2,1)S(1)} collective-permute-done((bf16[2,8,32,128]{3,2,1,0:T(8,128)(2,1)S(1)}, bf16[2,8,32,128]{3,2,1,0:T(8,128)(2,1)S(1)}, u32[]{:S(2)}, u32[]{:S(2)}) %collective-permute-start.17) | collective-permute-done | bytes 131104 | tf_op jit(solution)/shard_map/ppermute | solution.py:21
  336.6 0.2 fusion.20
  336.9 2.3 collective-permute-start.19
  339.4 3.4 collective-permute-done.19
  342.9 0.7 fusion.26
  (90 shorter events, 3.5 us)
Async XLA Ops:
  0.6 32.1 %copy-start = (bf16[8,128,1024]{2,1,0:T(8,128)(2,1)S(1)}, bf16[8,128,1024]{2,1,0:T(8,128)(2,1)}, u32[]{:S(2)}) copy-start(bf16[8,128,1024]{2,1,0:T(8,128)(2,1)} %param.8) | copy-start | bytes 6291460
  0.6 3.9 %copy-start.3 = (bf16[1,8,4096]{2,1,0:T(8,128)(2,1)S(1)}, bf16[1,8,4096]{2,1,0:T(8,128)(2,1)}, u32[]{:S(2)}) copy-start(bf16[1,8,4096]{2,1,0:T(8,128)(2,1)} %param.14) | copy-start | bytes 196612
  0.7 2.9 copy-start.7
  0.7 2.9 copy-start.4
  0.7 3.9 %collective-permute-start.5 = (bf16[8,4096]{1,0:T(8,128)(2,1)}, bf16[8,4096]{1,0:T(8,128)(2,1)S(1)}, u32[]{:S(2)}, u32[]{:S(2)}) collective-permute-start(bf16[8,4096]{1,0:T(8,128)(2,1)} %bitcast.351), channel_id=1, source_target_pairs={{0,1},{1,0},{2,3},{3,2},{4,5},{5,4},{6,7},{7,6},{8,9},{9,8},{10,11... | collective-permute-start | bytes 196616 | tf_op jit(solution)/shard_map/ppermute | solution.py:21
  3.2 3.4 collective-permute-start
  4.6 5.9 %collective-permute-start.6 = (bf16[16,4096]{1,0:T(8,128)(2,1)S(1)}, bf16[16,4096]{1,0:T(8,128)(2,1)S(1)}, u32[]{:S(2)}, u32[]{:S(2)}) collective-permute-start(bf16[16,4096]{1,0:T(8,128)(2,1)S(1)} %maximum_select_fusion.4), channel_id=1, source_target_pairs={{0,2},{1,3},{2,0},{3,1},{4,6},{5,7},{6,4},{7,5},{8,10},{9,11},{10,... | collective-permute-start | bytes 393224 | tf_op jit(solution)/shard_map/ppermute | solution.py:21
  7.8 12.9 %collective-permute-start.1 = (f32[8,8,1024]{2,1,0:T(8,128)S(1)}, f32[8,8,1024]{2,1,0:T(8,128)S(1)}, u32[]{:S(2)}, u32[]{:S(2)}) collective-permute-start(f32[8,8,1024]{2,1,0:T(8,128)S(1)} %select_bitcast_fusion.1), channel_id=1, source_target_pairs={{0,2},{1,3},{2,0},{3,1},{4,6},{5,7},{6,4},{7,5},{8,10},{9,11},{10,... | collective-permute-start | bytes 786440 | tf_op jit(solution)/shard_map/ppermute | solution.py:21
  10.5 18.6 %collective-permute-start.7 = (bf16[32,4096]{1,0:T(8,128)(2,1)S(1)}, bf16[32,4096]{1,0:T(8,128)(2,1)S(1)}, u32[]{:S(2)}, u32[]{:S(2)}) collective-permute-start(bf16[32,4096]{1,0:T(8,128)(2,1)S(1)} %maximum_select_fusion.3), channel_id=1, source_target_pairs={{0,4},{1,5},{2,6},{3,7},{4,0},{5,1},{6,2},{7,3},{8,12},{9,13},{10,... | collective-permute-start | bytes 786440 | tf_op jit(solution)/shard_map/ppermute | solution.py:21
  20.7 10.3 %collective-permute-start.2 = (f32[4,8,1024]{2,1,0:T(8,128)S(1)}, f32[4,8,1024]{2,1,0:T(8,128)S(1)}, u32[]{:S(2)}, u32[]{:S(2)}) collective-permute-start(f32[4,8,1024]{2,1,0:T(8,128)S(1)} %select_bitcast_fusion.2), channel_id=1, source_target_pairs={{0,4},{1,5},{2,6},{3,7},{4,0},{5,1},{6,2},{7,3},{8,12},{9,13},{10,... | collective-permute-start | bytes 393224 | tf_op jit(solution)/shard_map/ppermute | solution.py:21
  29.2 14.3 %collective-permute-start.8 = (bf16[64,4096]{1,0:T(8,128)(2,1)S(1)}, bf16[64,4096]{1,0:T(8,128)(2,1)S(1)}, u32[]{:S(2)}, u32[]{:S(2)}) collective-permute-start(bf16[64,4096]{1,0:T(8,128)(2,1)S(1)} %maximum_select_fusion.2), channel_id=1, source_target_pairs={{0,8},{1,9},{2,10},{3,11},{4,12},{5,13},{6,14},{7,15},{8,0},{9,1},... | collective-permute-start | bytes 1572872 | tf_op jit(solution)/shard_map/ppermute | solution.py:21
  31.1 8.9 %collective-permute-start.3 = (f32[2,8,1024]{2,1,0:T(8,128)S(1)}, f32[2,8,1024]{2,1,0:T(8,128)S(1)}, u32[]{:S(2)}, u32[]{:S(2)}) collective-permute-start(f32[2,8,1024]{2,1,0:T(8,128)S(1)} %select_bitcast_fusion.5), channel_id=1, source_target_pairs={{0,8},{1,9},{2,10},{3,11},{4,12},{5,13},{6,14},{7,15},{8,0},{9,1},... | collective-permute-start | bytes 196616 | tf_op jit(solution)/shard_map/ppermute | solution.py:21
  39.9 11.6 %collective-permute-start.4 = (f32[1,8,1024]{2,1,0:T(8,128)S(1)}, f32[1,8,1024]{2,1,0:T(8,128)S(1)}, u32[]{:S(2)}, u32[]{:S(2)}) collective-permute-start(f32[1,8,1024]{2,1,0:T(8,128)S(1)} %select_bitcast_fusion.7), channel_id=1, source_target_pairs={{0,16},{1,17},{2,18},{3,19},{4,20},{5,21},{6,22},{7,23},{8,24},{9,... | collective-permute-start | bytes 98312 | tf_op jit(solution)/shard_map/ppermute | solution.py:21
  43.8 22.5 %collective-permute-start.9 = (bf16[128,4096]{1,0:T(8,128)(2,1)S(1)}, bf16[128,4096]{1,0:T(8,128)(2,1)S(1)}, u32[]{:S(2)}, u32[]{:S(2)}) collective-permute-start(bf16[128,4096]{1,0:T(8,128)(2,1)S(1)} %maximum_select_fusion.1), channel_id=1, source_target_pairs={{0,16},{1,17},{2,18},{3,19},{4,20},{5,21},{6,22},{7,23},{8,24},{9,... | collective-permute-start | bytes 3145736 | tf_op jit(solution)/shard_map/ppermute | solution.py:21
  68.2 10.2 %copy-start.5 = (s32[1,256,8]{1,2,0:T(8,128)S(1)}, s32[1,256,8]{1,2,0:T(8,128)}, u32[]{:S(2)}) copy-start(s32[1,256,8]{1,2,0:T(8,128)} %param.15) | copy-start | bytes 24580
  68.2 10.3 %copy-start.6 = (s32[1,256]{1,0:T(1,128)S(1)}, s32[1,256]{1,0:T(1,128)}, u32[]{:S(2)}) copy-start(s32[1,256]{1,0:T(1,128)} %param.11) | copy-start | bytes 3076
  68.2 187.8 %all-to-all-start = ((bf16[8,4,128,1024]{3,2,1,0:T(8,128)(2,1)}), bf16[8,4,128,1024]{3,2,1,0:T(8,128)(2,1)}, u32[]{:S(2)}, u32[]{:S(2)}) async-start(bf16[8,4,128,1024]{3,2,1,0:T(8,128)(2,1)} %select_select_fusion), calls=%async_computation | async-start | bytes 16777216 | tf_op jit(solution)/shard_map/all_to_all | solution.py:152
  263.8 2.0 copy-start.1
  287.3 2.4 copy-start.2
  291.3 3.8 %collective-permute-start.10 = (f32[16,8,64]{2,1,0:T(8,128)S(1)}, f32[16,8,64]{2,1,0:T(8,128)S(1)}, u32[]{:S(2)}, u32[]{:S(2)}) collective-permute-start(f32[16,8,64]{2,1,0:T(8,128)S(1)} %select_bitcast_fusion.3), channel_id=1, source_target_pairs={{0,1},{1,0},{2,3},{3,2},{4,5},{5,4},{6,7},{7,6},{8,9},{9,8},{10,11... | collective-permute-start | bytes 98312 | tf_op jit(solution)/shard_map/ppermute | solution.py:21
  294.5 11.2 %collective-permute-start.11 = (bf16[16,8,32,128]{3,2,1,0:T(8,128)(2,1)S(1)}, bf16[16,8,32,128]{3,2,1,0:T(8,128)(2,1)S(1)}, u32[]{:S(2)}, u32[]{:S(2)}) collective-permute-start(bf16[16,8,32,128]{3,2,1,0:T(8,128)(2,1)S(1)} %fusion.2), channel_id=1, source_target_pairs={{0,1},{1,0},{2,3},{3,2},{4,5},{5,4},{6,7},{7,6},{8,9},{9,8},{10,11... | collective-permute-start | bytes 3145736 | tf_op jit(solution)/shard_map/ppermute | solution.py:21
  295.3 4.4 %collective-permute-start.12 = (f32[8,8,64]{2,1,0:T(8,128)S(1)}, f32[8,8,64]{2,1,0:T(8,128)S(1)}, u32[]{:S(2)}, u32[]{:S(2)}) collective-permute-start(f32[8,8,64]{2,1,0:T(8,128)S(1)} %select_bitcast_fusion.6), channel_id=1, source_target_pairs={{0,2},{1,3},{2,0},{3,1},{4,6},{5,7},{6,4},{7,5},{8,10},{9,11},{10,... | collective-permute-start | bytes 49160 | tf_op jit(solution)/shard_map/ppermute | solution.py:21
  299.9 4.7 %collective-permute-start.14 = (f32[4,8,64]{2,1,0:T(8,128)S(1)}, f32[4,8,64]{2,1,0:T(8,128)S(1)}, u32[]{:S(2)}, u32[]{:S(2)}) collective-permute-start(f32[4,8,64]{2,1,0:T(8,128)S(1)} %select_bitcast_fusion.8), channel_id=1, source_target_pairs={{0,4},{1,5},{2,6},{3,7},{4,0},{5,1},{6,2},{7,3},{8,12},{9,13},{10,... | collective-permute-start | bytes 24584 | tf_op jit(solution)/shard_map/ppermute | solution.py:21
  304.8 4.4 %collective-permute-start.16 = (f32[2,8,64]{2,1,0:T(8,128)S(1)}, f32[2,8,64]{2,1,0:T(8,128)S(1)}, u32[]{:S(2)}, u32[]{:S(2)}) collective-permute-start(f32[2,8,64]{2,1,0:T(8,128)S(1)} %select_bitcast_fusion.9), channel_id=1, source_target_pairs={{0,8},{1,9},{2,10},{3,11},{4,12},{5,13},{6,14},{7,15},{8,0},{9,1},... | collective-permute-start | bytes 12296 | tf_op jit(solution)/shard_map/ppermute | solution.py:21
  307.1 12.0 %collective-permute-start.13 = (bf16[8,8,32,128]{3,2,1,0:T(8,128)(2,1)S(1)}, bf16[8,8,32,128]{3,2,1,0:T(8,128)(2,1)S(1)}, u32[]{:S(2)}, u32[]{:S(2)}) collective-permute-start(bf16[8,8,32,128]{3,2,1,0:T(8,128)(2,1)S(1)} %fusion.8), channel_id=1, source_target_pairs={{0,2},{1,3},{2,0},{3,1},{4,6},{5,7},{6,4},{7,5},{8,10},{9,11},{10,... | collective-permute-start | bytes 1572872 | tf_op jit(solution)/shard_map/ppermute | solution.py:21
  319.9 11.3 %collective-permute-start.15 = (bf16[4,8,32,128]{3,2,1,0:T(8,128)(2,1)S(1)}, bf16[4,8,32,128]{3,2,1,0:T(8,128)(2,1)S(1)}, u32[]{:S(2)}, u32[]{:S(2)}) collective-permute-start(bf16[4,8,32,128]{3,2,1,0:T(8,128)(2,1)S(1)} %fusion.16), channel_id=1, source_target_pairs={{0,4},{1,5},{2,6},{3,7},{4,0},{5,1},{6,2},{7,3},{8,12},{9,13},{10,... | collective-permute-start | bytes 786440 | tf_op jit(solution)/shard_map/ppermute | solution.py:21
  320.0 5.2 %collective-permute-start.18 = (f32[1,8,64]{2,1,0:T(8,128)S(1)}, f32[1,8,64]{2,1,0:T(8,128)S(1)}, u32[]{:S(2)}, u32[]{:S(2)}) collective-permute-start(f32[1,8,64]{2,1,0:T(8,128)S(1)} %get-tuple-element.43), channel_id=1, source_target_pairs={{0,16},{1,17},{2,18},{3,19},{4,20},{5,21},{6,22},{7,23},{8,24},{9,... | collective-permute-start | bytes 6152 | tf_op jit(solution)/shard_map/ppermute | solution.py:21
  331.6 5.1 %collective-permute-start.17 = (bf16[2,8,32,128]{3,2,1,0:T(8,128)(2,1)S(1)}, bf16[2,8,32,128]{3,2,1,0:T(8,128)(2,1)S(1)}, u32[]{:S(2)}, u32[]{:S(2)}) collective-permute-start(bf16[2,8,32,128]{3,2,1,0:T(8,128)(2,1)S(1)} %fusion.23), channel_id=1, source_target_pairs={{0,8},{1,9},{2,10},{3,11},{4,12},{5,13},{6,14},{7,15},{8,0},{9,1},... | collective-permute-start | bytes 393224 | tf_op jit(solution)/shard_map/ppermute | solution.py:21
  336.9 5.9 %collective-permute-start.19 = (bf16[1,8,32,128]{3,2,1,0:T(8,128)(2,1)S(1)}, bf16[1,8,32,128]{3,2,1,0:T(8,128)(2,1)S(1)}, u32[]{:S(2)}, u32[]{:S(2)}) collective-permute-start(bf16[1,8,32,128]{3,2,1,0:T(8,128)(2,1)S(1)} %fusion.28), channel_id=1, source_target_pairs={{0,16},{1,17},{2,18},{3,19},{4,20},{5,21},{6,22},{7,23},{8,24},{9,... | collective-permute-start | bytes 196616 | tf_op jit(solution)/shard_map/ppermute | solution.py:21

commit v8 on v7

--- a/solution.py
+++ b/solution.py
@@ -16,36 +16,49 @@
 CTX_DEV = 1024
 
 
-def exchange(shard, bit):
+def digit_plan(peers):
+    plan = []
+    stride = 1
+    while stride < peers:
+        radix = 4 if peers // stride >= 4 else 2
+        plan.append((stride, radix))
+        stride *= radix
+    return plan
+
+
+def shifted(shard, stride, radix, step):
     peers = lax.axis_size("ctx")
-    return lax.ppermute(shard, "ctx", [(i, i ^ bit) for i in range(peers)])
+    pairs = []
+    for i in range(peers):
+        digit = (i // stride) % radix
+        pairs.append((i, i + ((digit + step) % radix - digit) * stride))
+    return lax.ppermute(shard, "ctx", pairs)
 
 
 def gather_rows(block, my_ctx):
-    peers = lax.axis_size("ctx")
     held = block
-    bit = 1
-    while bit < peers:
-        other = exchange(held, bit)
-        upper = (my_ctx // bit) % 2 == 1
-        held = jnp.where(
-            upper, jnp.concatenate([other, held]), jnp.concatenate([held, other])
+    for stride, radix in digit_plan(lax.axis_size("ctx")):
+        digit = (my_ctx // stride) % radix
+        pieces = [held] + [shifted(held, stride, radix, step) for step in range(1, radix)]
+        order = (digit - jnp.arange(radix, dtype=jnp.int32)) % radix
+        held = jnp.take(jnp.stack(pieces), order, axis=0)
+        held = held.reshape((radix * block.shape[0] * stride,) + block.shape[1:])
+    return held
+
+
+def scatter_rows(parts, my_ctx, merge, narrow=lambda t: t, widen=lambda t: t):
+    held = parts
+    for stride, radix in digit_plan(lax.axis_size("ctx")):
+        digit = (my_ctx // stride) % radix
+        grouped = jax.tree.map(
+            lambda a: a.reshape((a.shape[0] // radix, radix) + a.shape[1:]), held
         )
-        bit *= 2
-    return held
-
-
-def scatter_rows(parts, my_ctx, merge, narrow=lambda t: t, widen=lambda t: t):
-    peers = lax.axis_size("ctx")
-    held = parts
-    bit = 1
-    while bit < peers:
-        half = jax.tree.map(lambda a: a.reshape((a.shape[0] // 2, 2) + a.shape[1:]), held)
-        upper = (my_ctx // bit) % 2 == 1
-        keep = jax.tree.map(lambda a: jnp.where(upper, a[:, 1], a[:, 0]), half)
-        send = jax.tree.map(lambda a: jnp.where(upper, a[:, 0], a[:, 1]), half)
-        held = merge(keep, widen(exchange(narrow(send), bit)))
-        bit *= 2
+        merged = jax.tree.map(lambda a: jnp.take(a, digit, axis=1), grouped)
+        for step in range(1, radix):
+            target = (digit + step) % radix
+            send = jax.tree.map(lambda a: jnp.take(a, target, axis=1), grouped)
+            merged = merge(merged, widen(shifted(narrow(send), stride, radix, step)))
+        held = merged
     return jax.tree.map(lambda a: a[0], held)
 
 

time: 344 us -> 387 us (1.12)
  local copies, waits for them, and re-layouts: 20.8 us -> 39.3 us
  other arithmetic: 20.8 us -> 34.7 us
  starting transfers between devices: 36.1 us -> 48.4 us
    exp x0 -> x12, local copies, waits for them, and re-layouts: none -> 13.1 us  [the longest x6 6.58 us: merge_softmax(): factor_a = jnp.exp(running_a - newest)]
    ppermute x20 -> x28, starting transfers between devices: 26.6 us -> 37.7 us  [shifted(): return lax.ppermute(shard, 'ctx', pairs)]
    gather x0 -> x3, local copies, waits for them, and re-layouts: none -> 6.94 us  [gather_rows(): held = jnp.take(jnp.stack(pieces), order, axis=0)]
    ppermute x20 -> x28, waiting for transfers between devices: 66 us -> 59.7 us  [shifted(): return lax.ppermute(shard, 'ctx', pairs)]
    select_n x19 -> x16, other arithmetic: 3.38 us -> 7.36 us  [the longest x8 3.77 us: gather_rows(): held = jnp.take(jnp.stack(pieces), order, axis=0)]
    all_to_all x1, waiting for transfers between devices: 173 us -> 177 us  [on_device(): lax.all_to_all(outgoing, 'owner', split_axis=0, concat_axis=0, tiled=True)]
  transfers between devices with their start and end apart: 21 -> 29, of which waited for: 14 -> 9; matrix products, arithmetic and copies ran while one was open for 8% -> 13% of each run, Pallas kernels for 0% -> 0%
where the time goes in v8:
time: 387 us; the launch traced here: 386 us
  waiting for transfers between devices  237 us (61%)
  starting transfers between devices  48.4 us (13%)
  local copies, waits for them, and re-layouts  39.3 us (10%)
  other arithmetic  34.7 us (9%)
  Pallas kernels  21.5 us (6%)
    all_to_all x1, waiting for transfers between devices, on_device(): lax.all_to_all(outgoing, 'owner', split_axis=0, concat_axis=0, tiled=True)  177 us
    ppermute x28, waiting for transfers between devices, shifted(): return lax.ppermute(shard, 'ctx', pairs)  59.7 us
    ppermute x28, starting transfers between devices, shifted(): return lax.ppermute(shard, 'ctx', pairs)  37.7 us
    pallas_call x1, Pallas kernels, attend_local(): pl.pallas_call(attend_kernel, grid=(KVH,), in_specs=[pl.BlockSpec((rows,...  21.5 us
    all_to_all x1, starting transfers between devices, on_device(): lax.all_to_all(outgoing, 'owner', split_axis=0, concat_axis=0, tiled=True)  10.7 us
  transfers between devices with their start and end apart: 29, of which 9 were waited for; matrix products, arithmetic and copies ran while one was open for 13% of the time, Pallas kernels for 0%

profile of v8, /device:TPU:6, one launch (start us, length us, event | category | flops | bytes accessed | tf_op | source)
XLA Modules:
  0.0 385.9 jit_solution(15930251844707718897)
XLA Ops:
  0.8 2.0 collective-permute-start.8
  2.8 1.4 collective-permute-start.9
  4.1 1.4 fusion.14
  5.6 0.8 fusion.31
  8.0 0.7 broadcast_bitcast_fusion.1
  8.7 0.7 select_bitcast_fusion
  9.8 4.8 %gather_fusion = bf16[32,128,1024]{2,1,0:T(8,128)(2,1)} fusion(bf16[8,128,1024]{2,1,0:T(8,128)(2,1)S(1)} %copy-done, s32[1024]{0:T(1024)S(1)} %pad_clamp_fusion.5), kind=kCustom, calls=%fused_computation | custom fusion | bytes 16777344 | tf_op jit(solution)/shard_map/jit(_take)/gather | solution.py:154
  14.5 7.7 %select_select_fusion = bf16[8,4,128,1024]{3,2,1,0:T(8,128)(2,1)} fusion(bf16[8,4,128,1024]{3,2,1,0:T(8,128)(2,1)} %bitcast.367, pred[8,4]{1,0:T(8,128)(4,1)S(1)} %copy.153, pred[8,4]{1,0:T(8,128)(4,1)S(1)} %copy.152), kind=kLoop, calls=%fused_computation.6 | loop fusion | flops 8388608 | bytes 16777280 | tf_op jit(solution)/shard_map/jit(_where)/select_n | solution.py:153
  22.2 1.4 collective-permute-start.2
  23.7 0.7 pad_maximum_fusion.2
  24.4 1.5 gather_fusion.1
  26.0 3.4 collective-permute-start.10
  29.4 1.6 collective-permute-start.11
  31.7 1.2 fusion.35
  32.9 0.7 fusion.39
  33.6 2.4 collective-permute-start.3
  37.0 12.9 %collective-permute-done.10 = bf16[32,4096]{1,0:T(8,128)(2,1)S(1)} collective-permute-done((bf16[32,4096]{1,0:T(8,128)(2,1)S(1)}, bf16[32,4096]{1,0:T(8,128)(2,1)S(1)}, u32[]{:S(2)}, u32[]{:S(2)}) %collective-permute-start.10) | collective-permute-done | bytes 262176 | tf_op jit(solution)/shard_map/ppermute | solution.py:35
  50.0 6.5 %collective-permute-done.12 = bf16[32,4096]{1,0:T(8,128)(2,1)S(1)} collective-permute-done((bf16[32,4096]{1,0:T(8,128)(2,1)S(1)}, bf16[32,4096]{1,0:T(8,128)(2,1)S(1)}, u32[]{:S(2)}, u32[]{:S(2)}) %collective-permute-start.12) | collective-permute-done | bytes 262176 | tf_op jit(solution)/shard_map/ppermute | solution.py:35
  56.5 1.1 pad_maximum_fusion.1
  57.6 1.8 gather_fusion.2
  59.6 3.2 collective-permute-start.13
  62.8 0.9 fusion.44
  63.7 0.7 collective-permute-start.6
  64.6 21.8 %collective-permute-done.6 = f32[1,8,1024]{2,1,0:T(8,128)S(1)} collective-permute-done((f32[1,8,1024]{2,1,0:T(8,128)S(1)}, f32[1,8,1024]{2,1,0:T(8,128)S(1)}, u32[]{:S(2)}, u32[]{:S(2)}) %collective-permute-start.6) | collective-permute-done | bytes 32800 | tf_op jit(solution)/shard_map/ppermute | solution.py:35
  86.4 1.5 pad_maximum_fusion
  87.9 3.6 gather_fusion.3
  91.5 3.2 bitcast_select_fusion.1.query_ref
  94.7 10.7 %all-to-all-start = ((bf16[8,4,128,1024]{3,2,1,0:T(8,128)(2,1)}), bf16[8,4,128,1024]{3,2,1,0:T(8,128)(2,1)}, u32[]{:S(2)}, u32[]{:S(2)}) async-start(bf16[8,4,128,1024]{3,2,1,0:T(8,128)(2,1)} %select_select_fusion), calls=%async_computation | async-start | bytes 16777216 | tf_op jit(solution)/shard_map/all_to_all | solution.py:165
  106.1 0.7 gather_fusion.5
  109.2 1.2 fusion.13.mask_ref
  110.4 177.1 %all-to-all-done = bf16[8,4,128,1024]{3,2,1,0:T(8,128)(2,1)} async-done(((bf16[8,4,128,1024]{3,2,1,0:T(8,128)(2,1)}), bf16[8,4,128,1024]{3,2,1,0:T(8,128)(2,1)}, u32[]{:S(2)}, u32[]{:S(2)}) %all-to-all-start) | async-done | bytes 8388640 | tf_op jit(solution)/shard_map/all_to_all | solution.py:165
  287.5 5.4 %gather_fusion.4 = bf16[8,128,1024]{2,1,0:T(8,128)(2,1)} fusion(bf16[32,128,1024]{2,1,0:T(8,128)(2,1)} %bitcast.38, s32[1024]{0:T(1024)S(1)} %pad_clamp_fusion.1), kind=kCustom, calls=%fused_computation.4 | custom fusion | bytes 4194336 | tf_op jit(solution)/shard_map/jit(_take)/gather | solution.py:177
  292.9 2.4 fusion
  295.3 1.6 fusion.117
  297.3 21.5 %shard_map.95 = (f32[256,4096]{1,0:T(8,128)}, f32[4,256,8]{2,1,0:T(8,128)}, f32[4,256,8]{2,1,0:T(8,128)}) custom-call(bf16[256,4096]{1,0:T(8,128)(2,1)} %bitcast_select_fusion.1.query_ref, bf16[1024,512]{1,0:T(8,128)(2,1)} %get-tuple-element.147.key_ref, bf16[1024,512]{1,0:T(8,128)(2,1)} %get-tuple-element.146.value_ref, f32[256,1024]{1,0:T(8,128)} %fusion.13.mask_ref), custom_call_target="tpu_custom_call" | custom-call | flops 4294967296 | bytes 9437184 | tf_op jit(solution)/shard_map/pallas_call | solution.py:110
  318.9 1.3 copy.163
  320.1 0.7 concatenate.17
  321.3 0.7 concatenate.18
  322.6 1.6 collective-permute-start.18
  324.2 1.8 fusion.4
  327.5 3.7 collective-permute-start.24
  331.2 2.1 bitcast_convert_fusion
  333.9 0.7 collective-permute-start.17
  334.6 1.5 collective-permute-start.19
  337.4 2.9 collective-permute-start.26
  340.4 0.9 copy.170
  341.3 1.5 copy.172
  342.8 1.5 copy.173
  344.3 1.5 copy.174
  345.8 1.4 copy.178
  347.2 1.4 copy.180
  348.6 1.4 copy.182
  349.9 1.4 copy.184
  351.3 1.4 copy.186
  352.7 0.7 copy.188
  353.5 4.2 %collective-permute-done.19 = bf16[8,8,32,128]{3,1,2,0:T(8,128)(2,1)} collective-permute-done((bf16[8,8,32,128]{3,1,2,0:T(8,128)(2,1)}, bf16[8,8,32,128]{3,1,2,0:T(8,128)(2,1)}, u32[]{:S(2)}, u32[]{:S(2)}) %collective-permute-start.19) | collective-permute-done | bytes 524320 | tf_op jit(solution)/shard_map/ppermute | solution.py:35
  357.7 3.8 fusion.11
  362.2 1.6 collective-permute-start.23
  363.7 3.7 collective-permute-start.25
  367.5 7.8 %collective-permute-done.21 = bf16[2,8,32,128]{3,1,2,0:T(8,128)(2,1)S(1)} collective-permute-done((bf16[2,8,32,128]{3,1,2,0:T(8,128)(2,1)S(1)}, bf16[2,8,32,128]{3,1,2,0:T(8,128)(2,1)S(1)}, u32[]{:S(2)}, u32[]{:S(2)}) %collective-permute-start.21) | collective-permute-done | bytes 131104 | tf_op jit(solution)/shard_map/ppermute | solution.py:35
  375.3 3.4 collective-permute-done.25
  379.3 3.0 collective-permute-start.27
  382.6 2.5 collective-permute-done.27
  385.1 0.8 fusion.36
  (138 shorter events, 13.9 us)
Async XLA Ops:
  0.6 9.1 %copy-start = (bf16[8,128,1024]{2,1,0:T(8,128)(2,1)S(1)}, bf16[8,128,1024]{2,1,0:T(8,128)(2,1)}, u32[]{:S(2)}) copy-start(bf16[8,128,1024]{2,1,0:T(8,128)(2,1)} %param.26) | copy-start | bytes 6291460
  0.6 6.4 %copy-start.10 = (s32[8,8]{1,0:T(8,128)S(1)}, s32[8,8]{1,0:T(8,128)}, u32[]{:S(2)}) copy-start(s32[8,8]{1,0:T(8,128)} %param.27) | copy-start | bytes 772
  0.7 6.5 %copy-start.14 = (s32[8]{0:T(128)S(1)}, s32[8]{0:T(128)}, u32[]{:S(2)}) copy-start(s32[8]{0:T(128)} %param.28) | copy-start | bytes 100
  0.7 21.6 %collective-permute-start.7 = (bf16[8,4096]{1,0:T(8,128)(2,1)}, bf16[8,4096]{1,0:T(8,128)(2,1)S(1)}, u32[]{:S(2)}, u32[]{:S(2)}) collective-permute-start(bf16[8,4096]{1,0:T(8,128)(2,1)} %bitcast.388), channel_id=1, source_target_pairs={{0,1},{1,2},{2,3},{3,0},{4,5},{5,6},{6,7},{7,4},{8,9},{9,10},{10,1... | collective-permute-start | bytes 196616 | tf_op jit(solution)/shard_map/ppermute | solution.py:35
  0.8 22.9 %collective-permute-start.8 = (bf16[8,4096]{1,0:T(8,128)(2,1)}, bf16[8,4096]{1,0:T(8,128)(2,1)S(1)}, u32[]{:S(2)}, u32[]{:S(2)}) collective-permute-start(bf16[8,4096]{1,0:T(8,128)(2,1)} %bitcast.389), channel_id=1, source_target_pairs={{0,2},{1,3},{2,0},{3,1},{4,6},{5,7},{6,4},{7,5},{8,10},{9,11},{10,... | collective-permute-start | bytes 196616 | tf_op jit(solution)/shard_map/ppermute | solution.py:35
  2.8 20.9 %collective-permute-start.9 = (bf16[8,4096]{1,0:T(8,128)(2,1)}, bf16[8,4096]{1,0:T(8,128)(2,1)S(1)}, u32[]{:S(2)}, u32[]{:S(2)}) collective-permute-start(bf16[8,4096]{1,0:T(8,128)(2,1)} %bitcast.390), channel_id=1, source_target_pairs={{0,3},{1,0},{2,1},{3,2},{4,7},{5,4},{6,5},{7,6},{8,11},{9,8},{10,9... | collective-permute-start | bytes 196616 | tf_op jit(solution)/shard_map/ppermute | solution.py:35
  6.4 24.7 %collective-permute-start = (f32[8,8,1024]{2,1,0:T(8,128)}, f32[8,8,1024]{2,1,0:T(8,128)}, u32[]{:S(2)}, u32[]{:S(2)}) collective-permute-start(f32[8,8,1024]{2,1,0:T(8,128)} %get-tuple-element.151), channel_id=1, source_target_pairs={{0,1},{1,2},{2,3},{3,0},{4,5},{5,6},{6,7},{7,4},{8,9},{9,10},{10,1... | collective-permute-start | bytes 786440 | tf_op jit(solution)/shard_map/ppermute | solution.py:35
  6.4 25.3 %collective-permute-start.1 = (f32[8,8,1024]{2,1,0:T(8,128)}, f32[8,8,1024]{2,1,0:T(8,128)}, u32[]{:S(2)}, u32[]{:S(2)}) collective-permute-start(f32[8,8,1024]{2,1,0:T(8,128)} %get-tuple-element.152), channel_id=1, source_target_pairs={{0,2},{1,3},{2,0},{3,1},{4,6},{5,7},{6,4},{7,5},{8,10},{9,11},{10,... | collective-permute-start | bytes 786440 | tf_op jit(solution)/shard_map/ppermute | solution.py:35
  14.5 9.1 %copy-start.9 = (bf16[1,8,4096]{2,1,0:T(8,128)(2,1)S(1)}, bf16[1,8,4096]{2,1,0:T(8,128)(2,1)}, u32[]{:S(2)}) copy-start(bf16[1,8,4096]{2,1,0:T(8,128)(2,1)} %param.32) | copy-start | bytes 196612
  22.2 9.5 %collective-permute-start.2 = (f32[8,8,1024]{2,1,0:T(8,128)}, f32[8,8,1024]{2,1,0:T(8,128)}, u32[]{:S(2)}, u32[]{:S(2)}) collective-permute-start(f32[8,8,1024]{2,1,0:T(8,128)} %select_bitcast_fusion), channel_id=1, source_target_pairs={{0,3},{1,0},{2,1},{3,2},{4,7},{5,4},{6,5},{7,6},{8,11},{9,8},{10,9... | collective-permute-start | bytes 786440 | tf_op jit(solution)/shard_map/ppermute | solution.py:35
  26.0 23.9 %collective-permute-start.10 = (bf16[32,4096]{1,0:T(8,128)(2,1)S(1)}, bf16[32,4096]{1,0:T(8,128)(2,1)S(1)}, u32[]{:S(2)}, u32[]{:S(2)}) collective-permute-start(bf16[32,4096]{1,0:T(8,128)(2,1)S(1)} %bitcast_select_fusion.14), channel_id=1, source_target_pairs={{0,4},{1,5},{2,6},{3,7},{4,8},{5,9},{6,10},{7,11},{8,12},{9,13},{1... | collective-permute-start | bytes 786440 | tf_op jit(solution)/shard_map/ppermute | solution.py:35
  29.4 20.6 %collective-permute-start.11 = (bf16[32,4096]{1,0:T(8,128)(2,1)S(1)}, bf16[32,4096]{1,0:T(8,128)(2,1)S(1)}, u32[]{:S(2)}, u32[]{:S(2)}) collective-permute-start(bf16[32,4096]{1,0:T(8,128)(2,1)S(1)} %bitcast_select_fusion.14), channel_id=1, source_target_pairs={{0,8},{1,9},{2,10},{3,11},{4,12},{5,13},{6,14},{7,15},{8,0},{9,1},... | collective-permute-start | bytes 786440 | tf_op jit(solution)/shard_map/ppermute | solution.py:35
  31.1 25.4 %collective-permute-start.12 = (bf16[32,4096]{1,0:T(8,128)(2,1)S(1)}, bf16[32,4096]{1,0:T(8,128)(2,1)S(1)}, u32[]{:S(2)}, u32[]{:S(2)}) collective-permute-start(bf16[32,4096]{1,0:T(8,128)(2,1)S(1)} %bitcast_select_fusion.14), channel_id=1, source_target_pairs={{0,12},{1,13},{2,14},{3,15},{4,0},{5,1},{6,2},{7,3},{8,4},{9,5},{1... | collective-permute-start | bytes 786440 | tf_op jit(solution)/shard_map/ppermute | solution.py:35
  33.6 29.3 %collective-permute-start.3 = (f32[2,8,1024]{2,1,0:T(8,128)}, f32[2,8,1024]{2,1,0:T(8,128)S(1)}, u32[]{:S(2)}, u32[]{:S(2)}) collective-permute-start(f32[2,8,1024]{2,1,0:T(8,128)} %get-tuple-element.157), channel_id=1, source_target_pairs={{0,4},{1,5},{2,6},{3,7},{4,8},{5,9},{6,10},{7,11},{8,12},{9,13},{1... | collective-permute-start | bytes 196616 | tf_op jit(solution)/shard_map/ppermute | solution.py:35
  35.9 26.9 %collective-permute-start.4 = (f32[2,8,1024]{2,1,0:T(8,128)}, f32[2,8,1024]{2,1,0:T(8,128)S(1)}, u32[]{:S(2)}, u32[]{:S(2)}) collective-permute-start(f32[2,8,1024]{2,1,0:T(8,128)} %get-tuple-element.158), channel_id=1, source_target_pairs={{0,8},{1,9},{2,10},{3,11},{4,12},{5,13},{6,14},{7,15},{8,0},{9,1},... | collective-permute-start | bytes 196616 | tf_op jit(solution)/shard_map/ppermute | solution.py:35
  50.0 12.9 %collective-permute-start.5 = (f32[2,8,1024]{2,1,0:T(8,128)}, f32[2,8,1024]{2,1,0:T(8,128)}, u32[]{:S(2)}, u32[]{:S(2)}) collective-permute-start(f32[2,8,1024]{2,1,0:T(8,128)} %select_bitcast_fusion.1), channel_id=1, source_target_pairs={{0,12},{1,13},{2,14},{3,15},{4,0},{5,1},{6,2},{7,3},{8,4},{9,5},{1... | collective-permute-start | bytes 196616 | tf_op jit(solution)/shard_map/ppermute | solution.py:35
  59.6 26.8 %collective-permute-start.13 = (bf16[128,4096]{1,0:T(8,128)(2,1)S(1)}, bf16[128,4096]{1,0:T(8,128)(2,1)S(1)}, u32[]{:S(2)}, u32[]{:S(2)}) collective-permute-start(bf16[128,4096]{1,0:T(8,128)(2,1)S(1)} %bitcast_select_fusion.5), channel_id=1, source_target_pairs={{0,16},{1,17},{2,18},{3,19},{4,20},{5,21},{6,22},{7,23},{8,24},{9,... | collective-permute-start | bytes 3145736 | tf_op jit(solution)/shard_map/ppermute | solution.py:35
  63.7 22.7 %collective-permute-start.6 = (f32[1,8,1024]{2,1,0:T(8,128)S(1)}, f32[1,8,1024]{2,1,0:T(8,128)S(1)}, u32[]{:S(2)}, u32[]{:S(2)}) collective-permute-start(f32[1,8,1024]{2,1,0:T(8,128)S(1)} %select_bitcast_fusion.2), channel_id=1, source_target_pairs={{0,16},{1,17},{2,18},{3,19},{4,20},{5,21},{6,22},{7,23},{8,24},{9,... | collective-permute-start | bytes 98312 | tf_op jit(solution)/shard_map/ppermute | solution.py:35
  87.9 3.6 copy-start.13
  94.7 10.7 %copy-start.15 = (s32[8]{0:T(128)S(1)}, s32[8]{0:T(128)}, u32[]{:S(2)}) copy-start(s32[8]{0:T(128)} %param.28) | copy-start | bytes 100
  94.7 11.3 %copy-start.11 = (s32[1,256,8]{1,2,0:T(8,128)S(1)}, s32[1,256,8]{1,2,0:T(8,128)}, u32[]{:S(2)}) copy-start(s32[1,256,8]{1,2,0:T(8,128)} %param.33) | copy-start | bytes 24580
  94.7 11.4 %copy-start.12 = (s32[1,256]{1,0:T(1,128)S(1)}, s32[1,256]{1,0:T(1,128)}, u32[]{:S(2)}) copy-start(s32[1,256]{1,0:T(1,128)} %param.29) | copy-start | bytes 3076
  94.7 192.8 %all-to-all-start = ((bf16[8,4,128,1024]{3,2,1,0:T(8,128)(2,1)}), bf16[8,4,128,1024]{3,2,1,0:T(8,128)(2,1)}, u32[]{:S(2)}, u32[]{:S(2)}) async-start(bf16[8,4,128,1024]{3,2,1,0:T(8,128)(2,1)} %select_select_fusion), calls=%async_computation | async-start | bytes 16777216 | tf_op jit(solution)/shard_map/all_to_all | solution.py:165
  295.3 2.0 copy-start.1
  318.9 2.3 copy-start.2
  322.4 3.6 collective-permute-start.14
  322.5 4.0 %collective-permute-start.16 = (f32[8,8,64]{2,1,0:T(8,128)S(1)}, f32[8,8,64]{2,1,0:T(8,128)S(1)}, u32[]{:S(2)}, u32[]{:S(2)}) collective-permute-start(f32[8,8,64]{2,1,0:T(8,128)S(1)} %get-tuple-element.155), channel_id=1, source_target_pairs={{0,2},{1,3},{2,0},{3,1},{4,6},{5,7},{6,4},{7,5},{8,10},{9,11},{10,... | collective-permute-start | bytes 49160 | tf_op jit(solution)/shard_map/ppermute | solution.py:35
  322.6 3.9 %collective-permute-start.18 = (f32[8,8,64]{2,1,0:T(8,128)S(1)}, f32[8,8,64]{2,1,0:T(8,128)S(1)}, u32[]{:S(2)}, u32[]{:S(2)}) collective-permute-start(f32[8,8,64]{2,1,0:T(8,128)S(1)} %get-tuple-element.156), channel_id=1, source_target_pairs={{0,3},{1,0},{2,1},{3,2},{4,7},{5,4},{6,5},{7,6},{8,11},{9,8},{10,9... | collective-permute-start | bytes 49160 | tf_op jit(solution)/shard_map/ppermute | solution.py:35
  327.3 7.3 %collective-permute-start.20 = (f32[2,8,64]{2,1,0:T(8,128)S(1)}, f32[2,8,64]{2,1,0:T(8,128)S(1)}, u32[]{:S(2)}, u32[]{:S(2)}) collective-permute-start(f32[2,8,64]{2,1,0:T(8,128)S(1)} %get-tuple-element.161), channel_id=1, source_target_pairs={{0,4},{1,5},{2,6},{3,7},{4,8},{5,9},{6,10},{7,11},{8,12},{9,13},{1... | collective-permute-start | bytes 12296 | tf_op jit(solution)/shard_map/ppermute | solution.py:35
  327.4 8.7 %collective-permute-start.22 = (f32[2,8,64]{2,1,0:T(8,128)S(1)}, f32[2,8,64]{2,1,0:T(8,128)S(1)}, u32[]{:S(2)}, u32[]{:S(2)}) collective-permute-start(f32[2,8,64]{2,1,0:T(8,128)S(1)} %get-tuple-element.160), channel_id=1, source_target_pairs={{0,8},{1,9},{2,10},{3,11},{4,12},{5,13},{6,14},{7,15},{8,0},{9,1},... | collective-permute-start | bytes 12296 | tf_op jit(solution)/shard_map/ppermute | solution.py:35
  327.5 8.6 %collective-permute-start.24 = (f32[2,8,64]{2,1,0:T(8,128)S(1)}, f32[2,8,64]{2,1,0:T(8,128)S(1)}, u32[]{:S(2)}, u32[]{:S(2)}) collective-permute-start(f32[2,8,64]{2,1,0:T(8,128)S(1)} %get-tuple-element.162), channel_id=1, source_target_pairs={{0,12},{1,13},{2,14},{3,15},{4,0},{5,1},{6,2},{7,3},{8,4},{9,5},{1... | collective-permute-start | bytes 12296 | tf_op jit(solution)/shard_map/ppermute | solution.py:35
  333.3 20.2 %collective-permute-start.15 = (bf16[8,8,32,128]{3,1,2,0:T(8,128)(2,1)S(1)}, bf16[8,8,32,128]{3,1,2,0:T(8,128)(2,1)}, u32[]{:S(2)}, u32[]{:S(2)}) collective-permute-start(bf16[8,8,32,128]{3,1,2,0:T(8,128)(2,1)S(1)} %get-tuple-element.144), channel_id=1, source_target_pairs={{0,1},{1,2},{2,3},{3,0},{4,5},{5,6},{6,7},{7,4},{8,9},{9,10},{10,1... | collective-permute-start | bytes 1572872 | tf_op jit(solution)/shard_map/ppermute | solution.py:35
  333.9 19.6 %collective-permute-start.17 = (bf16[8,8,32,128]{3,1,2,0:T(8,128)(2,1)S(1)}, bf16[8,8,32,128]{3,1,2,0:T(8,128)(2,1)}, u32[]{:S(2)}, u32[]{:S(2)}) collective-permute-start(bf16[8,8,32,128]{3,1,2,0:T(8,128)(2,1)S(1)} %get-tuple-element.145), channel_id=1, source_target_pairs={{0,2},{1,3},{2,0},{3,1},{4,6},{5,7},{6,4},{7,5},{8,10},{9,11},{10,... | collective-permute-start | bytes 1572872 | tf_op jit(solution)/shard_map/ppermute | solution.py:35
  334.6 23.1 %collective-permute-start.19 = (bf16[8,8,32,128]{3,1,2,0:T(8,128)(2,1)}, bf16[8,8,32,128]{3,1,2,0:T(8,128)(2,1)}, u32[]{:S(2)}, u32[]{:S(2)}) collective-permute-start(bf16[8,8,32,128]{3,1,2,0:T(8,128)(2,1)} %bitcast_convert_fusion), channel_id=1, source_target_pairs={{0,3},{1,0},{2,1},{3,2},{4,7},{5,4},{6,5},{7,6},{8,11},{9,8},{10,9... | collective-permute-start | bytes 1572872 | tf_op jit(solution)/shard_map/ppermute | solution.py:35
  337.4 16.0 %collective-permute-start.26 = (f32[1,8,64]{2,1,0:T(8,128)}, f32[1,8,64]{2,1,0:T(8,128)S(1)}, u32[]{:S(2)}, u32[]{:S(2)}) collective-permute-start(f32[1,8,64]{2,1,0:T(8,128)} %get-tuple-element.166), channel_id=1, source_target_pairs={{0,16},{1,17},{2,18},{3,19},{4,20},{5,21},{6,22},{7,23},{8,24},{9,... | collective-permute-start | bytes 6152 | tf_op jit(solution)/shard_map/ppermute | solution.py:35
  353.4 25.3 %copy-start.3 = (f32[2,8,32]{1,2,0:T(8,128)S(1)}, f32[2,8,32]{1,2,0:T(8,128)}, u32[]{:S(2)}) copy-start(f32[2,8,32]{1,2,0:T(8,128)} %copy.178) | copy-start | bytes 6148
  353.4 25.3 %copy-start.4 = (f32[2,8,32]{1,2,0:T(8,128)S(1)}, f32[2,8,32]{1,2,0:T(8,128)}, u32[]{:S(2)}) copy-start(f32[2,8,32]{1,2,0:T(8,128)} %copy.180) | copy-start | bytes 6148
  353.4 25.3 %copy-start.5 = (f32[2,8,32]{1,2,0:T(8,128)S(1)}, f32[2,8,32]{1,2,0:T(8,128)}, u32[]{:S(2)}) copy-start(f32[2,8,32]{1,2,0:T(8,128)} %copy.182) | copy-start | bytes 6148
  353.4 25.3 %copy-start.6 = (f32[2,8,32]{1,2,0:T(8,128)S(1)}, f32[2,8,32]{1,2,0:T(8,128)}, u32[]{:S(2)}) copy-start(f32[2,8,32]{1,2,0:T(8,128)} %copy.184) | copy-start | bytes 6148
  353.5 25.3 %copy-start.7 = (f32[2,8,32]{1,2,0:T(8,128)S(1)}, f32[2,8,32]{1,2,0:T(8,128)}, u32[]{:S(2)}) copy-start(f32[2,8,32]{1,2,0:T(8,128)} %copy.186) | copy-start | bytes 6148
  353.5 25.3 %copy-start.8 = (f32[2,8,32]{1,2,0:T(8,128)S(1)}, f32[2,8,32]{1,2,0:T(8,128)}, u32[]{:S(2)}) copy-start(f32[2,8,32]{1,2,0:T(8,128)} %copy.188) | copy-start | bytes 6148
  361.5 13.8 %collective-permute-start.21 = (bf16[2,8,32,128]{3,1,2,0:T(8,128)(2,1)S(1)}, bf16[2,8,32,128]{3,1,2,0:T(8,128)(2,1)S(1)}, u32[]{:S(2)}, u32[]{:S(2)}) collective-permute-start(bf16[2,8,32,128]{3,1,2,0:T(8,128)(2,1)S(1)} %get-tuple-element.148), channel_id=1, source_target_pairs={{0,4},{1,5},{2,6},{3,7},{4,8},{5,9},{6,10},{7,11},{8,12},{9,13},{1... | collective-permute-start | bytes 393224 | tf_op jit(solution)/shard_map/ppermute | solution.py:35
  362.2 13.2 %collective-permute-start.23 = (bf16[2,8,32,128]{3,1,2,0:T(8,128)(2,1)S(1)}, bf16[2,8,32,128]{3,1,2,0:T(8,128)(2,1)S(1)}, u32[]{:S(2)}, u32[]{:S(2)}) collective-permute-start(bf16[2,8,32,128]{3,1,2,0:T(8,128)(2,1)S(1)} %get-tuple-element.149), channel_id=1, source_target_pairs={{0,8},{1,9},{2,10},{3,11},{4,12},{5,13},{6,14},{7,15},{8,0},{9,1},... | collective-permute-start | bytes 393224 | tf_op jit(solution)/shard_map/ppermute | solution.py:35
  363.7 15.0 %collective-permute-start.25 = (bf16[2,8,32,128]{3,1,2,0:T(8,128)(2,1)S(1)}, bf16[2,8,32,128]{3,1,2,0:T(8,128)(2,1)S(1)}, u32[]{:S(2)}, u32[]{:S(2)}) collective-permute-start(bf16[2,8,32,128]{3,1,2,0:T(8,128)(2,1)S(1)} %get-tuple-element.150), channel_id=1, source_target_pairs={{0,12},{1,13},{2,14},{3,15},{4,0},{5,1},{6,2},{7,3},{8,4},{9,5},{1... | collective-permute-start | bytes 393224 | tf_op jit(solution)/shard_map/ppermute | solution.py:35
  379.3 5.9 %collective-permute-start.27 = (bf16[1,8,32,128]{3,1,2,0:T(8,128)(2,1)S(1)}, bf16[1,8,32,128]{3,1,2,0:T(8,128)(2,1)S(1)}, u32[]{:S(2)}, u32[]{:S(2)}) collective-permute-start(bf16[1,8,32,128]{3,1,2,0:T(8,128)(2,1)S(1)} %bitcast_convert_fusion.1), channel_id=1, source_target_pairs={{0,16},{1,17},{2,18},{3,19},{4,20},{5,21},{6,22},{7,23},{8,24},{9,... | collective-permute-start | bytes 196616 | tf_op jit(solution)/shard_map/ppermute | solution.py:35

commit v9 on v7

--- a/solution.py
+++ b/solution.py
@@ -24,15 +24,20 @@
 def gather_rows(block, my_ctx):
     peers = lax.axis_size("ctx")
     held = block
-    bit = 1
-    while bit < peers:
+    bit = peers // 2
+    while bit >= 1:
         other = exchange(held, bit)
         upper = (my_ctx // bit) % 2 == 1
         held = jnp.where(
             upper, jnp.concatenate([other, held]), jnp.concatenate([held, other])
         )
-        bit *= 2
+        bit //= 2
     return held
+
+
+def reversed_order(peers):
+    width = peers.bit_length() - 1
+    return [int(format(i, "0%db" % width)[::-1], 2) for i in range(peers)]
 
 
 def scatter_rows(parts, my_ctx, merge, narrow=lambda t: t, widen=lambda t: t):
@@ -149,6 +154,9 @@
     outgoing, recomputed, all_queries = lax.optimization_barrier(
         (outgoing, recomputed, all_queries)
     )
+    all_queries = all_queries.reshape(cycle_size, RCP, QH * HD)[
+        jnp.array(reversed_order(cycle_size))
+    ].reshape(cycle_size * RCP, QH * HD)
     arrived = lax.all_to_all(outgoing, "owner", split_axis=0, concat_axis=0, tiled=True)
     wanted = lax.dynamic_index_in_dim(retrieval, my_owner, 0, keepdims=False)
     my_count = lax.dynamic_index_in_dim(counts, my_owner, 0, keepdims=False)

time: 344 us -> 339 us (0.985)
  waiting for transfers between devices: 239 us -> 228 us
  local copies, waits for them, and re-layouts: 20.8 us -> 24.6 us
    ppermute x20, waiting for transfers between devices: 66 us -> 51.4 us  [exchange(): return lax.ppermute(shard, 'ctx', [(i, i ^ bit) for i in range(peers)])]
    gather x0 -> x1, local copies, waits for them, and re-layouts: none -> 3.61 us  [on_device(): all_queries.reshape(cycle_size, RCP, QH * HD)]
  transfers between devices with their start and end apart: 21 -> 21, of which waited for: 14 -> 15; matrix products, arithmetic and copies ran while one was open for 8% -> 9% of each run, Pallas kernels for 0% -> 0%
where the time goes in v9:
time: 339 us; the launch traced here: 338 us
  waiting for transfers between devices  228 us (67%)
  starting transfers between devices  38.1 us (11%)
  local copies, waits for them, and re-layouts  24.6 us (7%)
  Pallas kernels  21.5 us (6%)
  other arithmetic  20.8 us (6%)
  matrix products  3.85 us (1%)
    all_to_all x1, waiting for transfers between devices, on_device(): lax.all_to_all(outgoing, 'owner', split_axis=0, concat_axis=0, tiled=True)  176 us
    ppermute x20, waiting for transfers between devices, exchange(): return lax.ppermute(shard, 'ctx', [(i, i ^ bit) for i in range(peers)])  51.4 us
    ppermute x20, starting transfers between devices, exchange(): return lax.ppermute(shard, 'ctx', [(i, i ^ bit) for i in range(peers)])  27.1 us
    pallas_call x1, Pallas kernels, attend_local(): pl.pallas_call(attend_kernel, grid=(KVH,), in_specs=[pl.BlockSpec((rows,...  21.5 us
    all_to_all x1, starting transfers between devices, on_device(): lax.all_to_all(outgoing, 'owner', split_axis=0, concat_axis=0, tiled=True)  10.9 us
    select_n x1, other arithmetic, on_device(): jnp.where(filled[:, :, None, None], jnp.take(span_cache, chosen, axis=0),...  7.63 us
  transfers between devices with their start and end apart: 21, of which 15 were waited for; matrix products, arithmetic and copies ran while one was open for 9% of the time, Pallas kernels for 0%

profile of v9, /device:TPU:6, one launch (start us, length us, event | category | flops | bytes accessed | tf_op | source)
XLA Modules:
  0.0 337.7 jit_solution(605418108742495769)
XLA Ops:
  0.7 3.3 collective-permute-start.5
  4.0 1.4 fusion.14
  5.4 0.9 select_bitcast_fusion
  6.3 0.2 reduce_window_sum.11
  7.0 0.1 fusion.43
  7.3 1.2 collective-permute-start.6
  8.5 1.1 fusion.13
  9.7 2.0 collective-permute-start.1
  11.7 1.6 collective-permute-done.6
  13.3 3.4 collective-permute-start.7
  16.7 5.5 %collective-permute-done.1 = f32[8,8,1024]{2,1,0:T(8,128)S(1)} collective-permute-done((f32[8,8,1024]{2,1,0:T(8,128)S(1)}, f32[8,8,1024]{2,1,0:T(8,128)S(1)}, u32[]{:S(2)}, u32[]{:S(2)}) %collective-permute-start.1) | collective-permute-done | bytes 262176 | tf_op jit(solution)/shard_map/ppermute | solution.py:21
  22.4 9.9 %collective-permute-done.7 = bf16[32,4096]{1,0:T(8,128)(2,1)S(1)} collective-permute-done((bf16[32,4096]{1,0:T(8,128)(2,1)S(1)}, bf16[32,4096]{1,0:T(8,128)(2,1)S(1)}, u32[]{:S(2)}, u32[]{:S(2)}) %collective-permute-start.7) | collective-permute-done | bytes 262176 | tf_op jit(solution)/shard_map/ppermute | solution.py:21
  32.3 0.8 collective-permute-start.8
  33.1 1.0 collective-permute-done.2
  34.2 0.4 collective-permute-start.3
  34.6 4.7 %gather_fusion = bf16[32,128,1024]{2,1,0:T(8,128)(2,1)} fusion(bf16[8,128,1024]{2,1,0:T(8,128)(2,1)S(1)} %copy-done, s32[1024]{0:T(1024)S(1)} %pad_clamp_fusion.3), kind=kCustom, calls=%fused_computation | custom fusion | bytes 16777344 | tf_op jit(solution)/shard_map/jit(_take)/gather | solution.py:146
  39.3 1.1 collective-permute-start.4
  40.4 4.8 %collective-permute-done.8 = bf16[64,4096]{1,0:T(8,128)(2,1)S(1)} collective-permute-done((bf16[64,4096]{1,0:T(8,128)(2,1)S(1)}, bf16[64,4096]{1,0:T(8,128)(2,1)S(1)}, u32[]{:S(2)}, u32[]{:S(2)}) %collective-permute-start.8) | collective-permute-done | bytes 524320 | tf_op jit(solution)/shard_map/ppermute | solution.py:21
  45.3 0.2 maximum_select_fusion.1
  45.6 7.6 %select_select_fusion = bf16[8,4,128,1024]{3,2,1,0:T(8,128)(2,1)} fusion(bf16[8,4,128,1024]{3,2,1,0:T(8,128)(2,1)} %bitcast.327, pred[8,4]{1,0:T(8,128)(4,1)S(1)} %copy.360, pred[8,4]{1,0:T(8,128)(4,1)S(1)} %copy.359), kind=kLoop, calls=%fused_computation.4 | loop fusion | flops 8388608 | bytes 16777280 | tf_op jit(solution)/shard_map/jit(_where)/select_n | solution.py:145
  53.3 1.8 maximum_select_fusion
  55.1 10.9 %all-to-all-start = ((bf16[8,4,128,1024]{3,2,1,0:T(8,128)(2,1)}), bf16[8,4,128,1024]{3,2,1,0:T(8,128)(2,1)}, u32[]{:S(2)}, u32[]{:S(2)}) async-start(bf16[8,4,128,1024]{3,2,1,0:T(8,128)(2,1)} %select_select_fusion), calls=%async_computation | async-start | bytes 16777216 | tf_op jit(solution)/shard_map/all_to_all | solution.py:160
  66.0 0.6 dynamic_slice.12
  66.8 0.7 gather_fusion.3
  67.6 0.7 broadcast_compare_fusion
  68.3 0.7 fusion.49
  69.0 0.2 convert_reduce_fusion
  69.5 0.3 broadcast_in_dim.125
  69.8 1.3 fusion.7.mask_ref
  71.1 3.6 %gather_fusion.2 = bf16[32,8,4096]{2,1,0:T(8,128)(2,1)} fusion(bf16[32,8,4096]{2,1,0:T(8,128)(2,1)} %bitcast.331, s32[1024]{0:T(1024)S(1)} %pad_clamp_fusion.1), kind=kCustom, calls=%fused_computation.2 | custom fusion | bytes 4194432 | tf_op jit(solution)/shard_map/gather | solution.py:157
  74.7 176.4 %all-to-all-done = bf16[8,4,128,1024]{3,2,1,0:T(8,128)(2,1)} async-done(((bf16[8,4,128,1024]{3,2,1,0:T(8,128)(2,1)}), bf16[8,4,128,1024]{3,2,1,0:T(8,128)(2,1)}, u32[]{:S(2)}, u32[]{:S(2)}) %all-to-all-start) | async-done | bytes 8388640 | tf_op jit(solution)/shard_map/all_to_all | solution.py:160
  251.1 5.4 %gather_fusion.1 = bf16[8,128,1024]{2,1,0:T(8,128)(2,1)} fusion(bf16[32,128,1024]{2,1,0:T(8,128)(2,1)} %bitcast.36, s32[1024]{0:T(1024)S(1)} %pad_clamp_fusion.2), kind=kCustom, calls=%fused_computation.1 | custom fusion | bytes 4194336 | tf_op jit(solution)/shard_map/jit(_take)/gather | solution.py:172
  256.5 2.4 fusion.1
  259.0 1.7 fusion.65
  260.6 0.3 copy-done.2
  261.0 21.5 %shard_map.104 = (f32[256,4096]{1,0:T(8,128)}, f32[4,256,8]{2,1,0:T(8,128)}, f32[4,256,8]{2,1,0:T(8,128)}) custom-call(bf16[256,4096]{1,0:T(8,128)(2,1)} %bitcast.342, bf16[1024,512]{1,0:T(8,128)(2,1)} %get-tuple-element.41.key_ref, bf16[1024,512]{1,0:T(8,128)(2,1)} %get-tuple-element.40.value_ref, f32[256,1024]{1,0:T(8,128)} %fusion.7.mask_ref), custom_call_target="tpu_custom_call" | custom-call | flops 4294967296 | bytes 9437184 | tf_op jit(solution)/shard_map/pallas_call | solution.py:102
  282.5 1.3 copy.381
  283.7 0.8 concatenate.63
  284.6 0.3 copy.383
  284.9 0.2 copy.382
  285.1 0.8 concatenate.64
  285.9 0.3 copy.384
  286.5 2.6 fusion.64
  289.1 0.6 fusion.2
  289.8 0.6 collective-permute-start.11
  290.7 3.9 %collective-permute-done.12 = f32[8,8,64]{2,1,0:T(8,128)S(1)} collective-permute-done((f32[8,8,64]{2,1,0:T(8,128)S(1)}, f32[8,8,64]{2,1,0:T(8,128)S(1)}, u32[]{:S(2)}, u32[]{:S(2)}) %collective-permute-start.12) | collective-permute-done | bytes 16416 | tf_op jit(solution)/shard_map/ppermute | solution.py:21
  294.7 1.0 collective-permute-start.14
  295.7 3.8 %collective-permute-done.14 = f32[4,8,64]{2,1,0:T(8,128)S(1)} collective-permute-done((f32[4,8,64]{2,1,0:T(8,128)S(1)}, f32[4,8,64]{2,1,0:T(8,128)S(1)}, u32[]{:S(2)}, u32[]{:S(2)}) %collective-permute-start.14) | collective-permute-done | bytes 8224 | tf_op jit(solution)/shard_map/ppermute | solution.py:21
  299.6 0.5 collective-permute-start.16
  300.1 1.2 fusion
  301.6 1.9 collective-permute-done.16
  303.7 9.2 %collective-permute-done.13 = bf16[8,8,32,128]{3,2,1,0:T(8,128)(2,1)S(1)} collective-permute-done((bf16[8,8,32,128]{3,2,1,0:T(8,128)(2,1)S(1)}, bf16[8,8,32,128]{3,2,1,0:T(8,128)(2,1)S(1)}, u32[]{:S(2)}, u32[]{:S(2)}) %collective-permute-start.13) | collective-permute-done | bytes 524320 | tf_op jit(solution)/shard_map/ppermute | solution.py:21
  312.9 0.7 fusion.5
  313.7 1.2 collective-permute-start.15
  314.9 5.8 %collective-permute-start.18 = (f32[1,8,64]{2,1,0:T(8,128)S(1)}, f32[1,8,64]{2,1,0:T(8,128)S(1)}, u32[]{:S(2)}, u32[]{:S(2)}) collective-permute-start(f32[1,8,64]{2,1,0:T(8,128)S(1)} %get-tuple-element.43), channel_id=1, source_target_pairs={{0,16},{1,17},{2,18},{3,19},{4,20},{5,21},{6,22},{7,23},{8,24},{9,... | collective-permute-start | bytes 6152 | tf_op jit(solution)/shard_map/ppermute | solution.py:21
  320.7 1.6 collective-permute-done.18
  322.3 2.8 collective-permute-done.15
  325.1 0.3 fusion.11
  325.5 1.8 collective-permute-start.17
  327.2 3.3 collective-permute-done.17
  330.5 0.2 fusion.20
  330.8 3.8 %collective-permute-start.19 = (bf16[1,8,32,128]{3,2,1,0:T(8,128)(2,1)S(1)}, bf16[1,8,32,128]{3,2,1,0:T(8,128)(2,1)S(1)}, u32[]{:S(2)}, u32[]{:S(2)}) collective-permute-start(bf16[1,8,32,128]{3,2,1,0:T(8,128)(2,1)S(1)} %fusion.28), channel_id=1, source_target_pairs={{0,16},{1,17},{2,18},{3,19},{4,20},{5,21},{6,22},{7,23},{8,24},{9,... | collective-permute-start | bytes 196616 | tf_op jit(solution)/shard_map/ppermute | solution.py:21
  334.7 2.0 collective-permute-done.19
  336.9 0.7 fusion.26
  (96 shorter events, 3.7 us)
Async XLA Ops:
  0.6 33.9 %copy-start = (bf16[8,128,1024]{2,1,0:T(8,128)(2,1)S(1)}, bf16[8,128,1024]{2,1,0:T(8,128)(2,1)}, u32[]{:S(2)}) copy-start(bf16[8,128,1024]{2,1,0:T(8,128)(2,1)} %param.9) | copy-start | bytes 6291460
  0.6 6.6 %copy-start.4 = (bf16[1,8,4096]{2,1,0:T(8,128)(2,1)S(1)}, bf16[1,8,4096]{2,1,0:T(8,128)(2,1)}, u32[]{:S(2)}) copy-start(bf16[1,8,4096]{2,1,0:T(8,128)(2,1)} %param.15) | copy-start | bytes 196612
  0.7 5.6 %copy-start.5 = (s32[8,8]{1,0:T(8,128)S(1)}, s32[8,8]{1,0:T(8,128)}, u32[]{:S(2)}) copy-start(s32[8,8]{1,0:T(8,128)} %param.10) | copy-start | bytes 772
  0.7 5.6 %copy-start.9 = (s32[8]{0:T(128)S(1)}, s32[8]{0:T(128)}, u32[]{:S(2)}) copy-start(s32[8]{0:T(128)} %param.11) | copy-start | bytes 100
  0.7 6.6 %collective-permute-start.5 = (bf16[8,4096]{1,0:T(8,128)(2,1)}, bf16[8,4096]{1,0:T(8,128)(2,1)S(1)}, u32[]{:S(2)}, u32[]{:S(2)}) collective-permute-start(bf16[8,4096]{1,0:T(8,128)(2,1)} %bitcast.355), channel_id=1, source_target_pairs={{0,16},{1,17},{2,18},{3,19},{4,20},{5,21},{6,22},{7,23},{8,24},{9,... | collective-permute-start | bytes 196616 | tf_op jit(solution)/shard_map/ppermute | solution.py:21
  6.2 2.3 collective-permute-start
  7.3 6.0 %collective-permute-start.6 = (bf16[16,4096]{1,0:T(8,128)(2,1)S(1)}, bf16[16,4096]{1,0:T(8,128)(2,1)S(1)}, u32[]{:S(2)}, u32[]{:S(2)}) collective-permute-start(bf16[16,4096]{1,0:T(8,128)(2,1)S(1)} %maximum_select_fusion.4), channel_id=1, source_target_pairs={{0,8},{1,9},{2,10},{3,11},{4,12},{5,13},{6,14},{7,15},{8,0},{9,1},... | collective-permute-start | bytes 393224 | tf_op jit(solution)/shard_map/ppermute | solution.py:21
  9.7 12.5 %collective-permute-start.1 = (f32[8,8,1024]{2,1,0:T(8,128)S(1)}, f32[8,8,1024]{2,1,0:T(8,128)S(1)}, u32[]{:S(2)}, u32[]{:S(2)}) collective-permute-start(f32[8,8,1024]{2,1,0:T(8,128)S(1)} %select_bitcast_fusion.1), channel_id=1, source_target_pairs={{0,2},{1,3},{2,0},{3,1},{4,6},{5,7},{6,4},{7,5},{8,10},{9,11},{10,... | collective-permute-start | bytes 786440 | tf_op jit(solution)/shard_map/ppermute | solution.py:21
  13.3 18.9 %collective-permute-start.7 = (bf16[32,4096]{1,0:T(8,128)(2,1)S(1)}, bf16[32,4096]{1,0:T(8,128)(2,1)S(1)}, u32[]{:S(2)}, u32[]{:S(2)}) collective-permute-start(bf16[32,4096]{1,0:T(8,128)(2,1)S(1)} %maximum_select_fusion.3), channel_id=1, source_target_pairs={{0,4},{1,5},{2,6},{3,7},{4,0},{5,1},{6,2},{7,3},{8,12},{9,13},{10,... | collective-permute-start | bytes 786440 | tf_op jit(solution)/shard_map/ppermute | solution.py:21
  22.2 11.9 %collective-permute-start.2 = (f32[4,8,1024]{2,1,0:T(8,128)S(1)}, f32[4,8,1024]{2,1,0:T(8,128)S(1)}, u32[]{:S(2)}, u32[]{:S(2)}) collective-permute-start(f32[4,8,1024]{2,1,0:T(8,128)S(1)} %select_bitcast_fusion.2), channel_id=1, source_target_pairs={{0,4},{1,5},{2,6},{3,7},{4,0},{5,1},{6,2},{7,3},{8,12},{9,13},{10,... | collective-permute-start | bytes 393224 | tf_op jit(solution)/shard_map/ppermute | solution.py:21
  32.3 13.0 %collective-permute-start.8 = (bf16[64,4096]{1,0:T(8,128)(2,1)S(1)}, bf16[64,4096]{1,0:T(8,128)(2,1)S(1)}, u32[]{:S(2)}, u32[]{:S(2)}) collective-permute-start(bf16[64,4096]{1,0:T(8,128)(2,1)S(1)} %maximum_select_fusion.2), channel_id=1, source_target_pairs={{0,2},{1,3},{2,0},{3,1},{4,6},{5,7},{6,4},{7,5},{8,10},{9,11},{10,... | collective-permute-start | bytes 1572872 | tf_op jit(solution)/shard_map/ppermute | solution.py:21
  34.2 5.1 %collective-permute-start.3 = (f32[2,8,1024]{2,1,0:T(8,128)S(1)}, f32[2,8,1024]{2,1,0:T(8,128)S(1)}, u32[]{:S(2)}, u32[]{:S(2)}) collective-permute-start(f32[2,8,1024]{2,1,0:T(8,128)S(1)} %select_bitcast_fusion.5), channel_id=1, source_target_pairs={{0,8},{1,9},{2,10},{3,11},{4,12},{5,13},{6,14},{7,15},{8,0},{9,1},... | collective-permute-start | bytes 196616 | tf_op jit(solution)/shard_map/ppermute | solution.py:21
  39.3 13.9 %collective-permute-start.4 = (f32[1,8,1024]{2,1,0:T(8,128)S(1)}, f32[1,8,1024]{2,1,0:T(8,128)S(1)}, u32[]{:S(2)}, u32[]{:S(2)}) collective-permute-start(f32[1,8,1024]{2,1,0:T(8,128)S(1)} %select_bitcast_fusion.7), channel_id=1, source_target_pairs={{0,16},{1,17},{2,18},{3,19},{4,20},{5,21},{6,22},{7,23},{8,24},{9,... | collective-permute-start | bytes 98312 | tf_op jit(solution)/shard_map/ppermute | solution.py:21
  45.5 7.7 %collective-permute-start.9 = (bf16[128,4096]{1,0:T(8,128)(2,1)S(1)}, bf16[128,4096]{1,0:T(8,128)(2,1)S(1)}, u32[]{:S(2)}, u32[]{:S(2)}) collective-permute-start(bf16[128,4096]{1,0:T(8,128)(2,1)S(1)} %maximum_select_fusion.1), channel_id=1, source_target_pairs={{0,1},{1,0},{2,3},{3,2},{4,5},{5,4},{6,7},{7,6},{8,9},{9,8},{10,11... | collective-permute-start | bytes 3145736 | tf_op jit(solution)/shard_map/ppermute | solution.py:21
  55.1 11.5 %copy-start.6 = (s32[1,256,8]{1,2,0:T(8,128)S(1)}, s32[1,256,8]{1,2,0:T(8,128)}, u32[]{:S(2)}) copy-start(s32[1,256,8]{1,2,0:T(8,128)} %param.16) | copy-start | bytes 24580
  55.1 11.6 %copy-start.7 = (s32[1,256]{1,0:T(1,128)S(1)}, s32[1,256]{1,0:T(1,128)}, u32[]{:S(2)}) copy-start(s32[1,256]{1,0:T(1,128)} %param.12) | copy-start | bytes 3076
  55.1 14.1 %copy-start.8 = (s32[32]{0:T(128)S(1)}, s32[32]{0:T(128)}, u32[]{:S(2)}) copy-start(s32[32]{0:T(128)} %constant.263) | copy-start | bytes 388
  55.1 196.0 %all-to-all-start = ((bf16[8,4,128,1024]{3,2,1,0:T(8,128)(2,1)}), bf16[8,4,128,1024]{3,2,1,0:T(8,128)(2,1)}, u32[]{:S(2)}, u32[]{:S(2)}) async-start(bf16[8,4,128,1024]{3,2,1,0:T(8,128)(2,1)} %select_select_fusion), calls=%async_computation | async-start | bytes 16777216 | tf_op jit(solution)/shard_map/all_to_all | solution.py:160
  258.9 2.0 copy-start.2
  282.5 2.4 copy-start.3
  286.4 3.9 %collective-permute-start.10 = (f32[16,8,64]{2,1,0:T(8,128)S(1)}, f32[16,8,64]{2,1,0:T(8,128)S(1)}, u32[]{:S(2)}, u32[]{:S(2)}) collective-permute-start(f32[16,8,64]{2,1,0:T(8,128)S(1)} %select_bitcast_fusion.3), channel_id=1, source_target_pairs={{0,1},{1,0},{2,3},{3,2},{4,5},{5,4},{6,7},{7,6},{8,9},{9,8},{10,11... | collective-permute-start | bytes 98312 | tf_op jit(solution)/shard_map/ppermute | solution.py:21
  289.8 10.4 %collective-permute-start.11 = (bf16[16,8,32,128]{3,2,1,0:T(8,128)(2,1)S(1)}, bf16[16,8,32,128]{3,2,1,0:T(8,128)(2,1)S(1)}, u32[]{:S(2)}, u32[]{:S(2)}) collective-permute-start(bf16[16,8,32,128]{3,2,1,0:T(8,128)(2,1)S(1)} %fusion.2), channel_id=1, source_target_pairs={{0,1},{1,0},{2,3},{3,2},{4,5},{5,4},{6,7},{7,6},{8,9},{9,8},{10,11... | collective-permute-start | bytes 3145736 | tf_op jit(solution)/shard_map/ppermute | solution.py:21
  290.5 4.0 %collective-permute-start.12 = (f32[8,8,64]{2,1,0:T(8,128)S(1)}, f32[8,8,64]{2,1,0:T(8,128)S(1)}, u32[]{:S(2)}, u32[]{:S(2)}) collective-permute-start(f32[8,8,64]{2,1,0:T(8,128)S(1)} %select_bitcast_fusion.6), channel_id=1, source_target_pairs={{0,2},{1,3},{2,0},{3,1},{4,6},{5,7},{6,4},{7,5},{8,10},{9,11},{10,... | collective-permute-start | bytes 49160 | tf_op jit(solution)/shard_map/ppermute | solution.py:21
  294.7 4.7 %collective-permute-start.14 = (f32[4,8,64]{2,1,0:T(8,128)S(1)}, f32[4,8,64]{2,1,0:T(8,128)S(1)}, u32[]{:S(2)}, u32[]{:S(2)}) collective-permute-start(f32[4,8,64]{2,1,0:T(8,128)S(1)} %select_bitcast_fusion.8), channel_id=1, source_target_pairs={{0,4},{1,5},{2,6},{3,7},{4,0},{5,1},{6,2},{7,3},{8,12},{9,13},{10,... | collective-permute-start | bytes 24584 | tf_op jit(solution)/shard_map/ppermute | solution.py:21
  299.6 3.9 %collective-permute-start.16 = (f32[2,8,64]{2,1,0:T(8,128)S(1)}, f32[2,8,64]{2,1,0:T(8,128)S(1)}, u32[]{:S(2)}, u32[]{:S(2)}) collective-permute-start(f32[2,8,64]{2,1,0:T(8,128)S(1)} %select_bitcast_fusion.9), channel_id=1, source_target_pairs={{0,8},{1,9},{2,10},{3,11},{4,12},{5,13},{6,14},{7,15},{8,0},{9,1},... | collective-permute-start | bytes 12296 | tf_op jit(solution)/shard_map/ppermute | solution.py:21
  301.5 11.4 %collective-permute-start.13 = (bf16[8,8,32,128]{3,2,1,0:T(8,128)(2,1)S(1)}, bf16[8,8,32,128]{3,2,1,0:T(8,128)(2,1)S(1)}, u32[]{:S(2)}, u32[]{:S(2)}) collective-permute-start(bf16[8,8,32,128]{3,2,1,0:T(8,128)(2,1)S(1)} %fusion.8), channel_id=1, source_target_pairs={{0,2},{1,3},{2,0},{3,1},{4,6},{5,7},{6,4},{7,5},{8,10},{9,11},{10,... | collective-permute-start | bytes 1572872 | tf_op jit(solution)/shard_map/ppermute | solution.py:21
  313.7 11.4 %collective-permute-start.15 = (bf16[4,8,32,128]{3,2,1,0:T(8,128)(2,1)S(1)}, bf16[4,8,32,128]{3,2,1,0:T(8,128)(2,1)S(1)}, u32[]{:S(2)}, u32[]{:S(2)}) collective-permute-start(bf16[4,8,32,128]{3,2,1,0:T(8,128)(2,1)S(1)} %fusion.16), channel_id=1, source_target_pairs={{0,4},{1,5},{2,6},{3,7},{4,0},{5,1},{6,2},{7,3},{8,12},{9,13},{10,... | collective-permute-start | bytes 786440 | tf_op jit(solution)/shard_map/ppermute | solution.py:21
  314.9 7.4 %collective-permute-start.18 = (f32[1,8,64]{2,1,0:T(8,128)S(1)}, f32[1,8,64]{2,1,0:T(8,128)S(1)}, u32[]{:S(2)}, u32[]{:S(2)}) collective-permute-start(f32[1,8,64]{2,1,0:T(8,128)S(1)} %get-tuple-element.43), channel_id=1, source_target_pairs={{0,16},{1,17},{2,18},{3,19},{4,20},{5,21},{6,22},{7,23},{8,24},{9,... | collective-permute-start | bytes 6152 | tf_op jit(solution)/shard_map/ppermute | solution.py:21
  325.1 12.6 %copy-start.1 = (bf16[8,128,1024]{2,1,0:T(8,128)(2,1)S(1)}, bf16[8,128,1024]{2,1,0:T(8,128)(2,1)}, u32[]{:S(2)}) copy-start(bf16[8,128,1024]{2,1,0:T(8,128)(2,1)} %param.9) | copy-start | bytes 6291460
  325.5 5.1 %collective-permute-start.17 = (bf16[2,8,32,128]{3,2,1,0:T(8,128)(2,1)S(1)}, bf16[2,8,32,128]{3,2,1,0:T(8,128)(2,1)S(1)}, u32[]{:S(2)}, u32[]{:S(2)}) collective-permute-start(bf16[2,8,32,128]{3,2,1,0:T(8,128)(2,1)S(1)} %fusion.23), channel_id=1, source_target_pairs={{0,8},{1,9},{2,10},{3,11},{4,12},{5,13},{6,14},{7,15},{8,0},{9,1},... | collective-permute-start | bytes 393224 | tf_op jit(solution)/shard_map/ppermute | solution.py:21
  330.8 6.0 %collective-permute-start.19 = (bf16[1,8,32,128]{3,2,1,0:T(8,128)(2,1)S(1)}, bf16[1,8,32,128]{3,2,1,0:T(8,128)(2,1)S(1)}, u32[]{:S(2)}, u32[]{:S(2)}) collective-permute-start(bf16[1,8,32,128]{3,2,1,0:T(8,128)(2,1)S(1)} %fusion.28), channel_id=1, source_target_pairs={{0,16},{1,17},{2,18},{3,19},{4,20},{5,21},{6,22},{7,23},{8,24},{9,... | collective-permute-start | bytes 196616 | tf_op jit(solution)/shard_map/ppermute | solution.py:21

commit v10 on v9

--- a/solution.py
+++ b/solution.py
@@ -21,18 +21,22 @@
     return lax.ppermute(shard, "ctx", [(i, i ^ bit) for i in range(peers)])
 
 
-def gather_rows(block, my_ctx):
+def gather_rows(block, my_ctx, rider):
     peers = lax.axis_size("ctx")
     held = block
     bit = peers // 2
     while bit >= 1:
         other = exchange(held, bit)
+        if rider is not None:
+            other, rider = lax.optimization_barrier((other, rider))
         upper = (my_ctx // bit) % 2 == 1
         held = jnp.where(
             upper, jnp.concatenate([other, held]), jnp.concatenate([held, other])
         )
         bit //= 2
-    return held
+        if bit * 2 == peers // 2:
+            result_rider, rider = rider, None
+    return held, result_rider
 
 
 def reversed_order(peers):
@@ -150,7 +154,7 @@
     recomputed = scatter_rows(
         partial.reshape(cycle_size, RCP, feature_count), my_ctx, add_parts
     ).astype(jnp.bfloat16)
-    all_queries = gather_rows(queries[0], my_ctx)
+    all_queries, outgoing = gather_rows(queries[0], my_ctx, outgoing)
     outgoing, recomputed, all_queries = lax.optimization_barrier(
         (outgoing, recomputed, all_queries)
     )

time: 339 us -> 349 us (1.029)
  waiting for transfers between devices: 228 us -> 237 us
    ppermute x20, waiting for transfers between devices: 51.4 us -> 65.2 us  [exchange(): return lax.ppermute(shard, 'ctx', [(i, i ^ bit) for i in range(peers)])]
    all_to_all x1, waiting for transfers between devices: 176 us -> 171 us  [on_device(): lax.all_to_all(outgoing, 'owner', split_axis=0, concat_axis=0, tiled=True)]
  transfers between devices with their start and end apart: 21 -> 21, of which waited for: 15 -> 13; matrix products, arithmetic and copies ran while one was open for 9% -> 9% of each run, Pallas kernels for 0% -> 0%
where the time goes in v10:
time: 349 us; the launch traced here: 347 us
  waiting for transfers between devices  237 us (68%)
  starting transfers between devices  37.7 us (11%)
  local copies, waits for them, and re-layouts  24.7 us (7%)
  other arithmetic  22.4 us (6%)
  Pallas kernels  21.6 us (6%)
    all_to_all x1, waiting for transfers between devices, on_device(): lax.all_to_all(outgoing, 'owner', split_axis=0, concat_axis=0, tiled=True)  171 us
    ppermute x20, waiting for transfers between devices, exchange(): return lax.ppermute(shard, 'ctx', [(i, i ^ bit) for i in range(peers)])  65.2 us
    ppermute x20, starting transfers between devices, exchange(): return lax.ppermute(shard, 'ctx', [(i, i ^ bit) for i in range(peers)])  26.1 us
    pallas_call x1, Pallas kernels, attend_local(): pl.pallas_call(attend_kernel, grid=(KVH,), in_specs=[pl.BlockSpec((rows,...  21.6 us
    all_to_all x1, starting transfers between devices, on_device(): lax.all_to_all(outgoing, 'owner', split_axis=0, concat_axis=0, tiled=True)  11.6 us
    select_n x1, other arithmetic, on_device(): jnp.where(filled[:, :, None, None], jnp.take(span_cache, chosen, axis=0),...  7.69 us
  transfers between devices with their start and end apart: 21, of which 13 were waited for; matrix products, arithmetic and copies ran while one was open for 9% of the time, Pallas kernels for 0%

profile of v10, /device:TPU:6, one launch (start us, length us, event | category | flops | bytes accessed | tf_op | source)
XLA Modules:
  0.0 347.0 jit_solution(6987329459667655449)
XLA Ops:
  0.6 3.3 collective-permute-start
  3.9 0.8 fusion.63
  4.9 0.7 add_select_fusion.1
  6.2 4.9 %gather_fusion = bf16[32,128,1024]{2,1,0:T(8,128)(2,1)} fusion(bf16[8,128,1024]{2,1,0:T(8,128)(2,1)S(1)} %copy-done, s32[1024]{0:T(1024)S(1)} %pad_clamp_fusion.3), kind=kCustom, calls=%fused_computation | custom fusion | bytes 16777344 | tf_op jit(solution)/shard_map/jit(_take)/gather | solution.py:150
  11.1 7.7 %select_select_fusion = bf16[8,4,128,1024]{3,2,1,0:T(8,128)(2,1)} fusion(bf16[8,4,128,1024]{3,2,1,0:T(8,128)(2,1)} %bitcast.327, pred[8,4]{1,0:T(8,128)(4,1)S(1)} %copy.360, pred[8,4]{1,0:T(8,128)(4,1)S(1)} %copy.359), kind=kLoop, calls=%fused_computation.4 | loop fusion | flops 8388608 | bytes 16777280 | tf_op jit(solution)/shard_map/jit(_where)/select_n | solution.py:149
  18.8 0.3 fusion.14
  19.2 0.8 collective-permute-start.6
  20.3 4.0 %collective-permute-done.6 = bf16[16,4096]{1,0:T(8,128)(2,1)S(1)} collective-permute-done((bf16[16,4096]{1,0:T(8,128)(2,1)S(1)}, bf16[16,4096]{1,0:T(8,128)(2,1)S(1)}, u32[]{:S(2)}, u32[]{:S(2)}) %collective-permute-start.6) | collective-permute-done | bytes 131104 | tf_op jit(solution)/shard_map/ppermute | solution.py:21
  24.3 3.4 collective-permute-start.7
  27.9 2.1 collective-permute-start.2
  29.9 8.4 %collective-permute-done.7 = bf16[32,4096]{1,0:T(8,128)(2,1)S(1)} collective-permute-done((bf16[32,4096]{1,0:T(8,128)(2,1)S(1)}, bf16[32,4096]{1,0:T(8,128)(2,1)S(1)}, u32[]{:S(2)}, u32[]{:S(2)}) %collective-permute-start.7) | collective-permute-done | bytes 262176 | tf_op jit(solution)/shard_map/ppermute | solution.py:21
  38.4 0.7 collective-permute-start.8
  39.2 3.5 collective-permute-start.3
  42.6 11.4 %collective-permute-done.8 = bf16[64,4096]{1,0:T(8,128)(2,1)S(1)} collective-permute-done((bf16[64,4096]{1,0:T(8,128)(2,1)S(1)}, bf16[64,4096]{1,0:T(8,128)(2,1)S(1)}, u32[]{:S(2)}, u32[]{:S(2)}) %collective-permute-start.8) | collective-permute-done | bytes 524320 | tf_op jit(solution)/shard_map/ppermute | solution.py:21
  54.0 0.2 maximum_select_fusion.1
  54.4 0.7 collective-permute-start.4
  55.1 3.8 %collective-permute-done.4 = f32[2,8,1024]{2,1,0:T(8,128)S(1)} collective-permute-done((f32[2,8,1024]{2,1,0:T(8,128)S(1)}, f32[2,8,1024]{2,1,0:T(8,128)S(1)}, u32[]{:S(2)}, u32[]{:S(2)}) %collective-permute-start.4) | collective-permute-done | bytes 65568 | tf_op jit(solution)/shard_map/ppermute | solution.py:21
  59.0 1.2 collective-permute-start.5
  60.2 4.3 %collective-permute-done.5 = f32[1,8,1024]{2,1,0:T(8,128)S(1)} collective-permute-done((f32[1,8,1024]{2,1,0:T(8,128)S(1)}, f32[1,8,1024]{2,1,0:T(8,128)S(1)}, u32[]{:S(2)}, u32[]{:S(2)}) %collective-permute-start.5) | collective-permute-done | bytes 32800 | tf_op jit(solution)/shard_map/ppermute | solution.py:21
  64.5 1.9 maximum_select_fusion
  66.4 11.6 %all-to-all-start = ((bf16[8,4,128,1024]{3,2,1,0:T(8,128)(2,1)}), bf16[8,4,128,1024]{3,2,1,0:T(8,128)(2,1)}, u32[]{:S(2)}, u32[]{:S(2)}) async-start(bf16[8,4,128,1024]{3,2,1,0:T(8,128)(2,1)} %select_select_fusion), calls=%async_computation | async-start | bytes 16777216 | tf_op jit(solution)/shard_map/all_to_all | solution.py:164
  78.0 0.6 dynamic_slice.12
  78.8 0.7 gather_fusion.3
  79.5 0.7 and_select_fusion.5
  80.2 0.7 fusion.61
  80.9 0.7 broadcast_compare_fusion
  81.7 0.7 fusion.49
  82.5 0.7 fusion.60
  83.6 0.3 broadcast_in_dim.125
  83.9 1.3 fusion.7.mask_ref
  85.2 3.6 %gather_fusion.2 = bf16[32,8,4096]{2,1,0:T(8,128)(2,1)} fusion(bf16[32,8,4096]{2,1,0:T(8,128)(2,1)} %bitcast.331, s32[1024]{0:T(1024)S(1)} %pad_clamp_fusion.1), kind=kCustom, calls=%fused_computation.2 | custom fusion | bytes 4194432 | tf_op jit(solution)/shard_map/gather | solution.py:161
  88.8 171.4 %all-to-all-done = bf16[8,4,128,1024]{3,2,1,0:T(8,128)(2,1)} async-done(((bf16[8,4,128,1024]{3,2,1,0:T(8,128)(2,1)}), bf16[8,4,128,1024]{3,2,1,0:T(8,128)(2,1)}, u32[]{:S(2)}, u32[]{:S(2)}) %all-to-all-start) | async-done | bytes 8388640 | tf_op jit(solution)/shard_map/all_to_all | solution.py:164
  260.2 5.4 %gather_fusion.1 = bf16[8,128,1024]{2,1,0:T(8,128)(2,1)} fusion(bf16[32,128,1024]{2,1,0:T(8,128)(2,1)} %bitcast.36, s32[1024]{0:T(1024)S(1)} %pad_clamp_fusion.2), kind=kCustom, calls=%fused_computation.1 | custom fusion | bytes 4194336 | tf_op jit(solution)/shard_map/jit(_take)/gather | solution.py:176
  265.5 2.4 fusion.1
  268.0 1.7 fusion.65
  269.7 0.3 copy-done.2
  270.0 21.6 %shard_map.104 = (f32[256,4096]{1,0:T(8,128)}, f32[4,256,8]{2,1,0:T(8,128)}, f32[4,256,8]{2,1,0:T(8,128)}) custom-call(bf16[256,4096]{1,0:T(8,128)(2,1)} %bitcast.342, bf16[1024,512]{1,0:T(8,128)(2,1)} %get-tuple-element.45.key_ref, bf16[1024,512]{1,0:T(8,128)(2,1)} %get-tuple-element.44.value_ref, f32[256,1024]{1,0:T(8,128)} %fusion.7.mask_ref), custom_call_target="tpu_custom_call" | custom-call | flops 4294967296 | bytes 9437184 | tf_op jit(solution)/shard_map/pallas_call | solution.py:106
  291.6 1.3 copy.381
  292.8 0.8 concatenate.63
  293.7 0.3 copy.383
  294.2 0.8 concatenate.64
  295.0 0.3 copy.384
  295.6 2.6 fusion.64
  298.2 0.6 fusion.2
  298.9 0.6 collective-permute-start.11
  299.8 3.9 %collective-permute-done.12 = f32[8,8,64]{2,1,0:T(8,128)S(1)} collective-permute-done((f32[8,8,64]{2,1,0:T(8,128)S(1)}, f32[8,8,64]{2,1,0:T(8,128)S(1)}, u32[]{:S(2)}, u32[]{:S(2)}) %collective-permute-start.12) | collective-permute-done | bytes 16416 | tf_op jit(solution)/shard_map/ppermute | solution.py:21
  303.8 0.9 collective-permute-start.14
  304.8 3.8 %collective-permute-done.14 = f32[4,8,64]{2,1,0:T(8,128)S(1)} collective-permute-done((f32[4,8,64]{2,1,0:T(8,128)S(1)}, f32[4,8,64]{2,1,0:T(8,128)S(1)}, u32[]{:S(2)}, u32[]{:S(2)}) %collective-permute-start.14) | collective-permute-done | bytes 8224 | tf_op jit(solution)/shard_map/ppermute | solution.py:21
  308.7 0.8 collective-permute-start.16
  309.6 1.2 fusion
  310.9 1.9 collective-permute-start.13
  312.9 9.4 %collective-permute-done.13 = bf16[8,8,32,128]{3,2,1,0:T(8,128)(2,1)S(1)} collective-permute-done((bf16[8,8,32,128]{3,2,1,0:T(8,128)(2,1)S(1)}, bf16[8,8,32,128]{3,2,1,0:T(8,128)(2,1)S(1)}, u32[]{:S(2)}, u32[]{:S(2)}) %collective-permute-start.13) | collective-permute-done | bytes 524320 | tf_op jit(solution)/shard_map/ppermute | solution.py:21
  322.3 0.7 fusion.5
  323.1 0.9 collective-permute-start.15
  324.0 1.7 collective-permute-start.18
  325.7 3.4 collective-permute-done.18
  329.1 5.4 %collective-permute-done.15 = bf16[4,8,32,128]{3,2,1,0:T(8,128)(2,1)S(1)} collective-permute-done((bf16[4,8,32,128]{3,2,1,0:T(8,128)(2,1)S(1)}, bf16[4,8,32,128]{3,2,1,0:T(8,128)(2,1)S(1)}, u32[]{:S(2)}, u32[]{:S(2)}) %collective-permute-start.15) | collective-permute-done | bytes 262176 | tf_op jit(solution)/shard_map/ppermute | solution.py:21
  334.5 0.3 fusion.11
  334.9 1.4 collective-permute-start.17
  336.3 3.6 %collective-permute-done.17 = bf16[2,8,32,128]{3,2,1,0:T(8,128)(2,1)S(1)} collective-permute-done((bf16[2,8,32,128]{3,2,1,0:T(8,128)(2,1)S(1)}, bf16[2,8,32,128]{3,2,1,0:T(8,128)(2,1)S(1)}, u32[]{:S(2)}, u32[]{:S(2)}) %collective-permute-start.17) | collective-permute-done | bytes 131104 | tf_op jit(solution)/shard_map/ppermute | solution.py:21
  339.9 0.2 fusion.20
  340.2 1.9 collective-permute-start.19
  342.3 3.8 %collective-permute-done.19 = bf16[1,8,32,128]{3,2,1,0:T(8,128)(2,1)S(1)} collective-permute-done((bf16[1,8,32,128]{3,2,1,0:T(8,128)(2,1)S(1)}, bf16[1,8,32,128]{3,2,1,0:T(8,128)(2,1)S(1)}, u32[]{:S(2)}, u32[]{:S(2)}) %collective-permute-start.19) | collective-permute-done | bytes 65568 | tf_op jit(solution)/shard_map/ppermute | solution.py:21
  346.2 0.7 fusion.26
  (98 shorter events, 4.2 us)
Async XLA Ops:
  0.6 5.6 %copy-start = (bf16[8,128,1024]{2,1,0:T(8,128)(2,1)S(1)}, bf16[8,128,1024]{2,1,0:T(8,128)(2,1)}, u32[]{:S(2)}) copy-start(bf16[8,128,1024]{2,1,0:T(8,128)(2,1)} %param.9) | copy-start | bytes 6291460
  0.6 18.5 %collective-permute-start = (bf16[8,4096]{1,0:T(8,128)(2,1)}, bf16[8,4096]{1,0:T(8,128)(2,1)S(1)}, u32[]{:S(2)}, u32[]{:S(2)}) collective-permute-start(bf16[8,4096]{1,0:T(8,128)(2,1)} %bitcast.355), channel_id=1, source_target_pairs={{0,16},{1,17},{2,18},{3,19},{4,20},{5,21},{6,22},{7,23},{8,24},{9,... | collective-permute-start | bytes 196616 | tf_op jit(solution)/shard_map/ppermute | solution.py:21
  11.1 7.7 %copy-start.3 = (bf16[256,1024]{1,0:T(8,128)(2,1)S(1)}, bf16[256,1024]{1,0:T(8,128)(2,1)}, u32[]{:S(2)}) copy-start(bf16[256,1024]{1,0:T(8,128)(2,1)} %param.14) | copy-start | bytes 1572868
  11.1 7.7 %copy-start.5 = (bf16[1,256,256]{2,1,0:T(8,128)(2,1)S(1)}, bf16[1,256,256]{2,1,0:T(8,128)(2,1)}, u32[]{:S(2)}) copy-start(bf16[1,256,256]{2,1,0:T(8,128)(2,1)} %param.13) | copy-start | bytes 393220
  11.1 8.1 %copy-start.6 = (bf16[1,8,4096]{2,1,0:T(8,128)(2,1)S(1)}, bf16[1,8,4096]{2,1,0:T(8,128)(2,1)}, u32[]{:S(2)}) copy-start(bf16[1,8,4096]{2,1,0:T(8,128)(2,1)} %param.15) | copy-start | bytes 196612
  19.2 5.1 %collective-permute-start.6 = (bf16[16,4096]{1,0:T(8,128)(2,1)S(1)}, bf16[16,4096]{1,0:T(8,128)(2,1)S(1)}, u32[]{:S(2)}, u32[]{:S(2)}) collective-permute-start(bf16[16,4096]{1,0:T(8,128)(2,1)S(1)} %maximum_select_fusion.4), channel_id=1, source_target_pairs={{0,8},{1,9},{2,10},{3,11},{4,12},{5,13},{6,14},{7,15},{8,0},{9,1},... | collective-permute-start | bytes 393224 | tf_op jit(solution)/shard_map/ppermute | solution.py:21
  20.1 7.6 %collective-permute-start.1 = (f32[16,8,1024]{2,1,0:T(8,128)S(1)}, f32[16,8,1024]{2,1,0:T(8,128)S(1)}, u32[]{:S(2)}, u32[]{:S(2)}) collective-permute-start(f32[16,8,1024]{2,1,0:T(8,128)S(1)} %select_bitcast_fusion), channel_id=1, source_target_pairs={{0,1},{1,0},{2,3},{3,2},{4,5},{5,4},{6,7},{7,6},{8,9},{9,8},{10,11... | collective-permute-start | bytes 1572872 | tf_op jit(solution)/shard_map/ppermute | solution.py:21
  24.3 14.0 %collective-permute-start.7 = (bf16[32,4096]{1,0:T(8,128)(2,1)S(1)}, bf16[32,4096]{1,0:T(8,128)(2,1)S(1)}, u32[]{:S(2)}, u32[]{:S(2)}) collective-permute-start(bf16[32,4096]{1,0:T(8,128)(2,1)S(1)} %maximum_select_fusion.3), channel_id=1, source_target_pairs={{0,4},{1,5},{2,6},{3,7},{4,0},{5,1},{6,2},{7,3},{8,12},{9,13},{10,... | collective-permute-start | bytes 786440 | tf_op jit(solution)/shard_map/ppermute | solution.py:21
  27.9 11.2 %collective-permute-start.2 = (f32[8,8,1024]{2,1,0:T(8,128)S(1)}, f32[8,8,1024]{2,1,0:T(8,128)S(1)}, u32[]{:S(2)}, u32[]{:S(2)}) collective-permute-start(f32[8,8,1024]{2,1,0:T(8,128)S(1)} %select_bitcast_fusion.1), channel_id=1, source_target_pairs={{0,2},{1,3},{2,0},{3,1},{4,6},{5,7},{6,4},{7,5},{8,10},{9,11},{10,... | collective-permute-start | bytes 786440 | tf_op jit(solution)/shard_map/ppermute | solution.py:21
  38.4 15.6 %collective-permute-start.8 = (bf16[64,4096]{1,0:T(8,128)(2,1)S(1)}, bf16[64,4096]{1,0:T(8,128)(2,1)S(1)}, u32[]{:S(2)}, u32[]{:S(2)}) collective-permute-start(bf16[64,4096]{1,0:T(8,128)(2,1)S(1)} %maximum_select_fusion.2), channel_id=1, source_target_pairs={{0,2},{1,3},{2,0},{3,1},{4,6},{5,7},{6,4},{7,5},{8,10},{9,11},{10,... | collective-permute-start | bytes 1572872 | tf_op jit(solution)/shard_map/ppermute | solution.py:21
  39.2 15.2 %collective-permute-start.3 = (f32[4,8,1024]{2,1,0:T(8,128)S(1)}, f32[4,8,1024]{2,1,0:T(8,128)S(1)}, u32[]{:S(2)}, u32[]{:S(2)}) collective-permute-start(f32[4,8,1024]{2,1,0:T(8,128)S(1)} %select_bitcast_fusion.2), channel_id=1, source_target_pairs={{0,4},{1,5},{2,6},{3,7},{4,0},{5,1},{6,2},{7,3},{8,12},{9,13},{10,... | collective-permute-start | bytes 393224 | tf_op jit(solution)/shard_map/ppermute | solution.py:21
  54.2 10.3 %collective-permute-start.9 = (bf16[128,4096]{1,0:T(8,128)(2,1)S(1)}, bf16[128,4096]{1,0:T(8,128)(2,1)S(1)}, u32[]{:S(2)}, u32[]{:S(2)}) collective-permute-start(bf16[128,4096]{1,0:T(8,128)(2,1)S(1)} %maximum_select_fusion.1), channel_id=1, source_target_pairs={{0,1},{1,0},{2,3},{3,2},{4,5},{5,4},{6,7},{7,6},{8,9},{9,8},{10,11... | collective-permute-start | bytes 3145736 | tf_op jit(solution)/shard_map/ppermute | solution.py:21
  54.4 4.6 %collective-permute-start.4 = (f32[2,8,1024]{2,1,0:T(8,128)S(1)}, f32[2,8,1024]{2,1,0:T(8,128)S(1)}, u32[]{:S(2)}, u32[]{:S(2)}) collective-permute-start(f32[2,8,1024]{2,1,0:T(8,128)S(1)} %select_bitcast_fusion.5), channel_id=1, source_target_pairs={{0,8},{1,9},{2,10},{3,11},{4,12},{5,13},{6,14},{7,15},{8,0},{9,1},... | collective-permute-start | bytes 196616 | tf_op jit(solution)/shard_map/ppermute | solution.py:21
  59.0 5.5 %collective-permute-start.5 = (f32[1,8,1024]{2,1,0:T(8,128)S(1)}, f32[1,8,1024]{2,1,0:T(8,128)S(1)}, u32[]{:S(2)}, u32[]{:S(2)}) collective-permute-start(f32[1,8,1024]{2,1,0:T(8,128)S(1)} %select_bitcast_fusion.7), channel_id=1, source_target_pairs={{0,16},{1,17},{2,18},{3,19},{4,20},{5,21},{6,22},{7,23},{8,24},{9,... | collective-permute-start | bytes 98312 | tf_op jit(solution)/shard_map/ppermute | solution.py:21
  66.4 11.7 %copy-start.10 = (s32[8]{0:T(128)S(1)}, s32[8]{0:T(128)}, u32[]{:S(2)}) copy-start(s32[8]{0:T(128)} %param.11) | copy-start | bytes 100
  66.4 12.2 %copy-start.7 = (s32[1,256,8]{1,2,0:T(8,128)S(1)}, s32[1,256,8]{1,2,0:T(8,128)}, u32[]{:S(2)}) copy-start(s32[1,256,8]{1,2,0:T(8,128)} %param.16) | copy-start | bytes 24580
  66.4 12.4 %copy-start.8 = (s32[1,256]{1,0:T(1,128)S(1)}, s32[1,256]{1,0:T(1,128)}, u32[]{:S(2)}) copy-start(s32[1,256]{1,0:T(1,128)} %param.12) | copy-start | bytes 3076
  66.4 16.9 %copy-start.9 = (s32[32]{0:T(128)S(1)}, s32[32]{0:T(128)}, u32[]{:S(2)}) copy-start(s32[32]{0:T(128)} %constant.263) | copy-start | bytes 388
  66.4 193.8 %all-to-all-start = ((bf16[8,4,128,1024]{3,2,1,0:T(8,128)(2,1)}), bf16[8,4,128,1024]{3,2,1,0:T(8,128)(2,1)}, u32[]{:S(2)}, u32[]{:S(2)}) async-start(bf16[8,4,128,1024]{3,2,1,0:T(8,128)(2,1)} %select_select_fusion), calls=%async_computation | async-start | bytes 16777216 | tf_op jit(solution)/shard_map/all_to_all | solution.py:164
  268.0 2.0 copy-start.2
  291.6 2.4 copy-start.4
  295.5 3.9 %collective-permute-start.10 = (f32[16,8,64]{2,1,0:T(8,128)S(1)}, f32[16,8,64]{2,1,0:T(8,128)S(1)}, u32[]{:S(2)}, u32[]{:S(2)}) collective-permute-start(f32[16,8,64]{2,1,0:T(8,128)S(1)} %select_bitcast_fusion.3), channel_id=1, source_target_pairs={{0,1},{1,0},{2,3},{3,2},{4,5},{5,4},{6,7},{7,6},{8,9},{9,8},{10,11... | collective-permute-start | bytes 98312 | tf_op jit(solution)/shard_map/ppermute | solution.py:21
  298.9 10.7 %collective-permute-start.11 = (bf16[16,8,32,128]{3,2,1,0:T(8,128)(2,1)S(1)}, bf16[16,8,32,128]{3,2,1,0:T(8,128)(2,1)S(1)}, u32[]{:S(2)}, u32[]{:S(2)}) collective-permute-start(bf16[16,8,32,128]{3,2,1,0:T(8,128)(2,1)S(1)} %fusion.2), channel_id=1, source_target_pairs={{0,1},{1,0},{2,3},{3,2},{4,5},{5,4},{6,7},{7,6},{8,9},{9,8},{10,11... | collective-permute-start | bytes 3145736 | tf_op jit(solution)/shard_map/ppermute | solution.py:21
  299.7 4.0 %collective-permute-start.12 = (f32[8,8,64]{2,1,0:T(8,128)S(1)}, f32[8,8,64]{2,1,0:T(8,128)S(1)}, u32[]{:S(2)}, u32[]{:S(2)}) collective-permute-start(f32[8,8,64]{2,1,0:T(8,128)S(1)} %select_bitcast_fusion.6), channel_id=1, source_target_pairs={{0,2},{1,3},{2,0},{3,1},{4,6},{5,7},{6,4},{7,5},{8,10},{9,11},{10,... | collective-permute-start | bytes 49160 | tf_op jit(solution)/shard_map/ppermute | solution.py:21
  303.8 4.7 %collective-permute-start.14 = (f32[4,8,64]{2,1,0:T(8,128)S(1)}, f32[4,8,64]{2,1,0:T(8,128)S(1)}, u32[]{:S(2)}, u32[]{:S(2)}) collective-permute-start(f32[4,8,64]{2,1,0:T(8,128)S(1)} %select_bitcast_fusion.8), channel_id=1, source_target_pairs={{0,4},{1,5},{2,6},{3,7},{4,0},{5,1},{6,2},{7,3},{8,12},{9,13},{10,... | collective-permute-start | bytes 24584 | tf_op jit(solution)/shard_map/ppermute | solution.py:21
  308.7 4.1 %collective-permute-start.16 = (f32[2,8,64]{2,1,0:T(8,128)S(1)}, f32[2,8,64]{2,1,0:T(8,128)S(1)}, u32[]{:S(2)}, u32[]{:S(2)}) collective-permute-start(f32[2,8,64]{2,1,0:T(8,128)S(1)} %select_bitcast_fusion.9), channel_id=1, source_target_pairs={{0,8},{1,9},{2,10},{3,11},{4,12},{5,13},{6,14},{7,15},{8,0},{9,1},... | collective-permute-start | bytes 12296 | tf_op jit(solution)/shard_map/ppermute | solution.py:21
  310.9 11.4 %collective-permute-start.13 = (bf16[8,8,32,128]{3,2,1,0:T(8,128)(2,1)S(1)}, bf16[8,8,32,128]{3,2,1,0:T(8,128)(2,1)S(1)}, u32[]{:S(2)}, u32[]{:S(2)}) collective-permute-start(bf16[8,8,32,128]{3,2,1,0:T(8,128)(2,1)S(1)} %fusion.8), channel_id=1, source_target_pairs={{0,2},{1,3},{2,0},{3,1},{4,6},{5,7},{6,4},{7,5},{8,10},{9,11},{10,... | collective-permute-start | bytes 1572872 | tf_op jit(solution)/shard_map/ppermute | solution.py:21
  323.1 11.4 %collective-permute-start.15 = (bf16[4,8,32,128]{3,2,1,0:T(8,128)(2,1)S(1)}, bf16[4,8,32,128]{3,2,1,0:T(8,128)(2,1)S(1)}, u32[]{:S(2)}, u32[]{:S(2)}) collective-permute-start(bf16[4,8,32,128]{3,2,1,0:T(8,128)(2,1)S(1)} %fusion.16), channel_id=1, source_target_pairs={{0,4},{1,5},{2,6},{3,7},{4,0},{5,1},{6,2},{7,3},{8,12},{9,13},{10,... | collective-permute-start | bytes 786440 | tf_op jit(solution)/shard_map/ppermute | solution.py:21
  324.0 5.1 %collective-permute-start.18 = (f32[1,8,64]{2,1,0:T(8,128)S(1)}, f32[1,8,64]{2,1,0:T(8,128)S(1)}, u32[]{:S(2)}, u32[]{:S(2)}) collective-permute-start(f32[1,8,64]{2,1,0:T(8,128)S(1)} %get-tuple-element.47), channel_id=1, source_target_pairs={{0,16},{1,17},{2,18},{3,19},{4,20},{5,21},{6,22},{7,23},{8,24},{9,... | collective-permute-start | bytes 6152 | tf_op jit(solution)/shard_map/ppermute | solution.py:21
  334.5 12.4 %copy-start.1 = (bf16[8,128,1024]{2,1,0:T(8,128)(2,1)S(1)}, bf16[8,128,1024]{2,1,0:T(8,128)(2,1)}, u32[]{:S(2)}) copy-start(bf16[8,128,1024]{2,1,0:T(8,128)(2,1)} %param.9) | copy-start | bytes 6291460
  334.9 5.1 %collective-permute-start.17 = (bf16[2,8,32,128]{3,2,1,0:T(8,128)(2,1)S(1)}, bf16[2,8,32,128]{3,2,1,0:T(8,128)(2,1)S(1)}, u32[]{:S(2)}, u32[]{:S(2)}) collective-permute-start(bf16[2,8,32,128]{3,2,1,0:T(8,128)(2,1)S(1)} %fusion.23), channel_id=1, source_target_pairs={{0,8},{1,9},{2,10},{3,11},{4,12},{5,13},{6,14},{7,15},{8,0},{9,1},... | collective-permute-start | bytes 393224 | tf_op jit(solution)/shard_map/ppermute | solution.py:21
  340.2 5.9 %collective-permute-start.19 = (bf16[1,8,32,128]{3,2,1,0:T(8,128)(2,1)S(1)}, bf16[1,8,32,128]{3,2,1,0:T(8,128)(2,1)S(1)}, u32[]{:S(2)}, u32[]{:S(2)}) collective-permute-start(bf16[1,8,32,128]{3,2,1,0:T(8,128)(2,1)S(1)} %fusion.28), channel_id=1, source_target_pairs={{0,16},{1,17},{2,18},{3,19},{4,20},{5,21},{6,22},{7,23},{8,24},{9,... | collective-permute-start | bytes 196616 | tf_op jit(solution)/shard_map/ppermute | solution.py:21
